TPU v7x, 32 devices: a whole 2x2x4 slice. The times are simulated.
32 devices in a mesh: stn: 16 (over z, x, core), chan: 2 (over y).
Axes of the slice: x: 2, y: 2, z: 4, core: 2. Of those that a mesh axis runs over, the one named last changes fastest.
Arguments:
- screen: float32 [32, 512, 512], P('stn'), may hold values from -6 to 6
- pierce_coords: float32 [2, 16, 2, 16, 1024], P(None, 'stn', 'chan'), may hold values from 0 to 1
- query_dest: int32 [16, 2, 16, 1024], P('stn', 'chan'), may hold values from 0 to 4096, as said below
- positions: float32 [3, 256], P(None, 'stn'), may hold values from -50 to 50
- directions: float32 [3, 512], replicated, may hold values from -0.7 to 0.7
- freq_ratio: float32 [64], P('chan'), may hold values from 0.7 to 1.4
- source_flux: float32 [512], replicated, may hold values from 0.2 to 5
- spectral_index: float32 [512], replicated, may hold values from -1.5 to 0.5
Outputs:
- visibilities: float32 [64, 2, 256, 256], P('chan', None, 'stn')
Inputs may be any that keep to these rules, and one draw needn't show every extreme that they name: `query_dest`: in each block every number 0 to 4095 appears in exactly one slot and empty slots hold 4096; an owner's live slots come first in its row; one owner, the same for every block, has all 1024 of its slots live in every block.
All inputs are finite; a program needn't handle non-finite values.
Results may differ from a plain program's by a relative error of at most 0.008.
Values may be sent and summed in bfloat16 or wider, within the bound.
No kernel may reach another device: no remote copies, remote signals or barrier semaphores. Data moves between devices by JAX's collectives and lax.ppermute only.
A program may use at most 128 MiB of HBM per device.

v0:
```python
import math

import jax
import jax.numpy as jnp
from jax import lax
from jax.sharding import PartitionSpec as P

TWO_PI = 2.0 * math.pi


def interpolate(values, coords, strip_rows, tile_cols):
    row_pos = coords[0] * (strip_rows - 1)
    col_pos = coords[1] * (tile_cols - 1)
    row_low = jnp.clip(jnp.floor(row_pos), 0.0, strip_rows - 2.0)
    col_low = jnp.clip(jnp.floor(col_pos), 0.0, tile_cols - 2.0)
    frac_y = row_pos - row_low
    frac_x = col_pos - col_low
    corner = row_low.astype(jnp.int32) * tile_cols + col_low.astype(jnp.int32)
    lower_pair = (1.0 - frac_x) * values[corner] + frac_x * values[corner + 1]
    upper_pair = (1.0 - frac_x) * values[corner + tile_cols] + frac_x * values[
        corner + tile_cols + 1
    ]
    return (1.0 - frac_y) * lower_pair + frac_y * upper_pair


def make_phasors(station_rows, iono_rows, directions, freq_ratio):
    delays = (
        station_rows[:, 0:1] * directions[0][None, :]
        + station_rows[:, 1:2] * directions[1][None, :]
    )
    delays = delays + station_rows[:, 2:3] * directions[2][None, :]
    angles = (TWO_PI * freq_ratio)[None, :, None] * delays[:, None, :] + iono_rows[
        :, None, :
    ] / freq_ratio[None, :, None]
    return jnp.concatenate([jnp.cos(angles), jnp.sin(angles)], axis=-1).astype(jnp.bfloat16)


def spectrum(source_flux, spectral_index, freq_ratio, count):
    return (
        source_flux[None, :]
        * jnp.exp(spectral_index[None, :] * jnp.log(freq_ratio)[:, None])
        / math.sqrt(count)
    )


def weight_rows(phasors, intensity):
    sources = intensity.shape[1]
    real_part = (phasors[:, :, :sources].astype(jnp.float32) * intensity[None]).astype(jnp.bfloat16)
    imag_part = (phasors[:, :, sources:].astype(jnp.float32) * intensity[None]).astype(jnp.bfloat16)
    upper_rows = jnp.concatenate([real_part, imag_part], axis=-1)
    lower_rows = jnp.concatenate([imag_part, -real_part], axis=-1)
    return jnp.concatenate([upper_rows, lower_rows], axis=0)


def body(
    screen,
    pierce_coords,
    query_dest,
    positions,
    directions,
    freq_ratio,
    source_flux,
    spectral_index,
):
    groups = lax.axis_size("stn")
    tile_cols = screen.shape[2]
    strip_rows = screen.shape[0] * screen.shape[1]
    values = screen.reshape(-1)
    capacity = query_dest.shape[3]
    coords = pierce_coords.reshape(2, groups, capacity)
    sampled = interpolate(
        values,
        lax.all_to_all(coords, "stn", split_axis=1, concat_axis=1, tiled=True),
        strip_rows,
        tile_cols,
    )
    returned = lax.all_to_all(sampled, "stn", split_axis=0, concat_axis=0, tiled=True)
    stations_local = positions.shape[1]
    local_sources = source_flux.shape[0] // lax.axis_size("chan")
    queries = stations_local * local_sources
    buffer = (
        jnp.zeros((queries + 1,), jnp.float32).at[query_dest.reshape(-1)].set(returned.reshape(-1))
    )
    own_iono = buffer[:queries].reshape(stations_local, local_sources)
    iono_phase = lax.all_gather(own_iono, "chan", axis=1, tiled=True)
    station_rows = positions.T
    own_phasors = make_phasors(station_rows, iono_phase, directions, freq_ratio)
    intensity = spectrum(source_flux, spectral_index, freq_ratio, source_flux.shape[0])
    weighted = weight_rows(own_phasors, intensity)
    total_stations = stations_local * groups
    channels = freq_ratio.shape[0]
    columns = jnp.einsum(
        "ack,nck->can",
        weighted,
        make_phasors(
            lax.all_gather(station_rows, "stn", axis=0, tiled=True),
            lax.all_gather(iono_phase, "stn", axis=0, tiled=True),
            directions,
            freq_ratio,
        ),
        preferred_element_type=jnp.float32,
    )
    visible = columns.reshape(channels, 2, stations_local, total_stations)
    first_row = lax.axis_index("stn") * stations_local
    rows_global = first_row + jnp.arange(stations_local, dtype=jnp.int32)
    cross_only = rows_global[:, None] != jnp.arange(total_stations, dtype=jnp.int32)[None, :]
    return jnp.where(cross_only[None, None], visible, jnp.zeros_like(visible))


def solution(mesh):
    in_specs = (
        P("stn", None, None),
        P(None, "stn", "chan", None, None),
        P("stn", "chan", None, None),
        P(None, "stn"),
        P(),
        P("chan"),
        P(),
        P(),
    )
    out_specs = P("chan", None, "stn", None)
    return jax.shard_map(body, mesh=mesh, in_specs=in_specs, out_specs=out_specs, check_vma=False)
```

profile of v0, /device:TPU:0, one launch (start us, length us, event | category | flops | bytes accessed | tf_op | source)
XLA Modules:
  0.0 576.7 jit_solution(3012017053386605129)
XLA Ops:
  0.0 1.7 copy.15
  1.7 7.4 %all-to-all-start = ((f32[2,16,1024]{2,0,1:T(2,128)}), f32[2,16,1024]{2,0,1:T(2,128)S(1)}, u32[]{:S(2)}, u32[]{:S(2)}) async-start(f32[2,16,1024]{2,0,1:T(2,128)} %bitcast.74), calls=%async_computation | async-start | bytes 262144 | tf_op jit(solution)/shard_map/all_to_all | solution.py:73
  9.1 0.9 copy.12
  10.0 0.1 compare_select_fusion.4
  10.0 0.8 fusion.17
  10.9 22.0 %all-gather = f32[16,16,3]{1,2,0:T(4,128)S(1)} all-gather(f32[1,16,3]{1,2,0:T(4,128)} %bitcast.98), channel_id=1, replica_groups=mesh['stn'=16,'chan'=2] {'stn'}, dimensions={0}, use_global_device_ids=true | all-gather | bytes 3264 | tf_op jit(solution)/shard_map/all_gather | solution.py:96
  32.9 0.1 reshape.551
  33.0 0.7 fusion.19
  33.6 0.8 slice_bitcast_fusion.2
  34.4 0.8 multiply_multiply_fusion
  35.2 0.1 multiply_add_fusion.3
  35.3 2.1 copy.13
  37.5 0.2 multiply_add_fusion
  37.6 0.0 all-to-all-done
  37.6 0.3 compare_select_fusion.3
  37.9 0.2 compare_select_fusion.2
  38.2 90.5 %gather_fusion.3 = f32[16384]{0:T(1024)S(1)} fusion(f32[524288]{0:T(1024)S(1)} %bitcast.75, s32[16384]{0:T(1024)S(1)} %broadcast_clamp_fusion), kind=kCustom, calls=%fused_computation.3 | custom fusion | bytes 196608 | tf_op jit(solution)/shard_map/gather | solution.py:20
  128.8 90.5 %gather_fusion.2 = f32[16384]{0:T(1024)S(1)} fusion(f32[524288]{0:T(1024)S(1)} %bitcast.76, s32[16384]{0:T(1024)S(1)} %broadcast_clamp_fusion.1), kind=kCustom, calls=%fused_computation.2 | custom fusion | bytes 196608 | tf_op jit(solution)/shard_map/gather | solution.py:20
  219.3 90.5 %gather_fusion.1 = f32[16384]{0:T(1024)S(1)} fusion(f32[524288]{0:T(1024)S(1)} %bitcast.77, s32[16384]{0:T(1024)S(1)} %broadcast_clamp_fusion.2), kind=kCustom, calls=%fused_computation.1 | custom fusion | bytes 196608 | tf_op jit(solution)/shard_map/gather | solution.py:19
  309.9 0.0 copy-start
  309.9 90.5 %gather_fusion = f32[16384]{0:T(1024)S(1)} fusion(f32[524288]{0:T(1024)S(1)} %bitcast.78, s32[16384]{0:T(1024)S(1)} %broadcast_clamp_fusion.3), kind=kCustom, calls=%fused_computation | custom fusion | bytes 196608 | tf_op jit(solution)/shard_map/gather | solution.py:19
  400.4 1.0 multiply_add_fusion.2
  401.4 3.5 all-to-all-start.1
  404.9 0.1 iota_compare_fusion
  405.0 6.8 %all-to-all-done.1 = f32[16,1,1024]{2,1,0:T(1,128)S(1)} async-done(((f32[16,1,1024]{2,1,0:T(1,128)}), f32[16,1,1024]{2,1,0:T(1,128)S(1)}, u32[]{:S(2)}, u32[]{:S(2)}) %all-to-all-start.1) | async-done | bytes 65568 | tf_op jit(solution)/shard_map/all_to_all | solution.py:77
  411.8 60.4 %scatter_custom_fusion = f32[4097]{0:T(1024)S(1)} fusion(s32[16384]{0:T(1024)S(1)} %bitcast.90, f32[16384]{0:T(1024)S(1)} %bitcast.91, f32[]{:T(128)} %constant.11.clone.1), kind=kCustom, calls=%fused_computation.55 | custom fusion | bytes 16392 | tf_op jit(solution)/shard_map/scatter | solution.py:82
  472.2 4.4 all_gather.9
  476.6 19.4 %all_gather.11 = f32[256,512]{1,0:T(8,128)S(1)} all-gather(f32[16,512]{1,0:T(8,128)S(1)} %all_gather.9), channel_id=1, replica_groups=mesh['stn'=16,'chan'=2] {'stn'}, dimensions={0}, use_global_device_ids=true | all-gather | bytes 557056 | tf_op jit(solution)/shard_map/all_gather | solution.py:97
  496.0 0.0 copy-done
  496.0 3.9 fusion.16
  499.9 4.3 multiply_convert_fusion.1
  504.2 62.5 %cosine_convert_fusion = (bf16[256,32,512]{2,0,1:T(8,128)(2,1)}, bf16[256,32,512]{2,0,1:T(8,128)(2,1)}) fusion(f32[32]{0:T(128)S(1)} %copy-done, f32[256,512]{1,0:T(8,128)S(1)} %all_gather.11, f32[256,512]{1,0:T(8,128)S(1)} %multiply_add_fusion, f32[32]{0:T(128)S(1)} %get-tuple-element.24), kind=kLoop, calls=%fused_computation.11 | loop fusion | flops 20971520 | bytes 17826048 | tf_op jit(solution)/shard_map/convert
  566.6 8.9 %fusion = f32[32,32,256]{2,1,0:T(8,128)S(1)} fusion(bf16[256,32,512]{2,0,1:T(8,128)(2,1)} %get-tuple-element.8, bf16[256,32,512]{2,0,1:T(8,128)(2,1)} %get-tuple-element.7, bf16[16,32,512]{2,0,1:T(8,128)(2,1)S(1)} %fusion.16, bf16[16,32,512]{2,0,1:T(8,128)(2,1)S(1)} %get-tuple-element.10, bf16[16,32,512]{2,0,1:T(8,128)(2,1)S(1)} %get-tuple-element.9), kind=kOutput, calls=%fused_computation.6 | convolution fusion | flops 578813952 | bytes 19398656 | tf_op jit(solution)/shard_map/ack,nck->can/dot_general | solution.py:92
  575.5 1.1 broadcast_select_fusion
  (9 shorter events, 0.1 us)
Async XLA Ops:
  1.7 36.0 %all-to-all-start = ((f32[2,16,1024]{2,0,1:T(2,128)}), f32[2,16,1024]{2,0,1:T(2,128)S(1)}, u32[]{:S(2)}, u32[]{:S(2)}) async-start(f32[2,16,1024]{2,0,1:T(2,128)} %bitcast.74), calls=%async_computation | async-start | bytes 262144 | tf_op jit(solution)/shard_map/all_to_all | solution.py:73
  309.9 186.1 %copy-start = (f32[32]{0:T(128)S(1)}, f32[32]{0:T(128)}, u32[]{:S(2)}) copy-start(f32[32]{0:T(128)} %param.13) | copy-start | bytes 388
  401.4 10.4 %all-to-all-start.1 = ((f32[16,1,1024]{2,1,0:T(1,128)}), f32[16,1,1024]{2,1,0:T(1,128)S(1)}, u32[]{:S(2)}, u32[]{:S(2)}) async-start(f32[16,1,1024]{2,1,0:T(1,128)} %multiply_add_fusion.2), calls=%async_computation.1 | async-start | bytes 131072 | tf_op jit(solution)/shard_map/all_to_all | solution.py:77
where the time goes:
time: 577 us
  local copies, waits for them, and re-layouts  429 us (74%)
  other arithmetic  75.1 us (13%)
  blocking collectives  45.8 us (8%)
  starting transfers between devices  10.9 us (2%)
  matrix products  8.92 us (2%)
  waiting for transfers between devices  6.79 us (1%)
    gather x2, local copies, waits for them, and re-layouts, interpolate(): lower_pair = (1.0 - frac_x) * values[corner] + frac_x * values[corner + 1]  181 us
    gather x1, local copies, waits for them, and re-layouts, interpolate(): values[corner + tile_cols + 1]  90.5 us
    gather x1, local copies, waits for them, and re-layouts, interpolate(): values[corner + tile_cols]  90.5 us
    another operation x1, other arithmetic  62.5 us
    scatter x1, local copies, waits for them, and re-layouts, body(): jnp.zeros((queries + 1,), jnp.float32).at[query_dest.reshape(-1)]  60.4 us
    all_gather x1, blocking collectives, body(): lax.all_gather(station_rows, 'stn', axis=0, tiled=True)  22 us
    all_gather x1, blocking collectives, body(): lax.all_gather(iono_phase, 'stn', axis=0, tiled=True)  19.4 us
  transfers between devices with their start and end apart: 2, of which 1 were waited for; matrix products, arithmetic and copies ran while one was open for 1% of the time, Pallas kernels for 0%

commit v1 on v0

--- a/solution.py
+++ b/solution.py
@@ -3,6 +3,8 @@
 import jax
 import jax.numpy as jnp
 from jax import lax
+from jax.experimental import pallas as pl
+from jax.experimental.pallas import tpu as pltpu
 from jax.sharding import PartitionSpec as P
 
 TWO_PI = 2.0 * math.pi
@@ -21,6 +23,66 @@
         corner + tile_cols + 1
     ]
     return (1.0 - frac_y) * lower_pair + frac_y * upper_pair
+
+
+UNROLL = 16
+
+
+def _interp_kernel(r_ref, c_ref, s_ref, o_ref):
+    rows = s_ref.shape[0]
+    two_nb = s_ref.shape[1]
+    nb = two_nb // 2
+    cols = nb * 128
+    chunk = o_ref.shape[0]
+    base = pl.program_id(0) * chunk
+    sub = lax.broadcasted_iota(jnp.int32, (two_nb, 128), 0)
+    lane = lax.broadcasted_iota(jnp.int32, (two_nb, 128), 1)
+    col = ((sub % nb) * 128 + lane).astype(jnp.float32)
+    upper = sub >= nb
+    rowid = lax.broadcasted_iota(jnp.int32, (8, 128), 0)
+
+    def group(g, carry):
+        for h in range(UNROLL // 8):
+            acc = jnp.zeros((8, 128), jnp.float32)
+            for u in range(8):
+                j = base + g * UNROLL + h * 8 + u
+                t = s_ref[r_ref[j]]
+                y = jnp.full((two_nb, 128), c_ref[0, j], jnp.float32) * (rows - 1)
+                x = jnp.full((two_nb, 128), c_ref[1, j], jnp.float32) * (cols - 1)
+                ry = jnp.clip(jnp.floor(y), 0.0, rows - 2.0)
+                kx = jnp.clip(jnp.floor(x), 0.0, cols - 2.0)
+                fy = y - ry
+                fx = x - kx
+                wy = jnp.where(upper, fy, 1.0 - fy)
+                wx = jnp.where(col == kx, 1.0 - fx, jnp.where(col == kx + 1.0, fx, 0.0))
+                row = jnp.sum(t * (wy * wx), axis=0, keepdims=True)
+                acc = jnp.where(rowid == u, row, acc)
+            start = pl.multiple_of(g * UNROLL + h * 8, 8)
+            o_ref[pl.ds(start, 8), :] = jnp.sum(acc, axis=1, keepdims=True)
+        return carry
+
+    lax.fori_loop(0, chunk // UNROLL, group, 0)
+
+
+def interpolate_kernel(screen2d, coords):
+    rows, cols = screen2d.shape
+    nb = cols // 128
+    q = coords.shape[1]
+    chunk = min(2048, q)
+    r = jnp.clip(jnp.floor(coords[0] * (rows - 1)), 0.0, rows - 2.0).astype(jnp.int32)
+    pair = jnp.concatenate([screen2d, jnp.roll(screen2d, -1, axis=0)], axis=1)
+    pair = pair.reshape(rows, 2 * nb, 128)
+    out = pl.pallas_call(
+        _interp_kernel,
+        grid_spec=pltpu.PrefetchScalarGridSpec(
+            num_scalar_prefetch=2,
+            grid=(q // chunk,),
+            in_specs=[pl.BlockSpec((rows, 2 * nb, 128), lambda i, rr, cc: (0, 0, 0))],
+            out_specs=pl.BlockSpec((chunk, 1), lambda i, rr, cc: (i, 0)),
+        ),
+        out_shape=jax.ShapeDtypeStruct((q, 1), jnp.float32),
+    )(r, coords, pair)
+    return out[:, 0]
 
 
 def make_phasors(station_rows, iono_rows, directions, freq_ratio):
@@ -68,12 +130,10 @@
     values = screen.reshape(-1)
     capacity = query_dest.shape[3]
     coords = pierce_coords.reshape(2, groups, capacity)
-    sampled = interpolate(
-        values,
-        lax.all_to_all(coords, "stn", split_axis=1, concat_axis=1, tiled=True),
-        strip_rows,
-        tile_cols,
-    )
+    received = lax.all_to_all(coords, "stn", split_axis=1, concat_axis=1, tiled=True)
+    sampled = interpolate_kernel(
+        values.reshape(strip_rows, tile_cols), received.reshape(2, groups * capacity)
+    ).reshape(groups, capacity)
     returned = lax.all_to_all(sampled, "stn", split_axis=0, concat_axis=0, tiled=True)
     stations_local = positions.shape[1]
     local_sources = source_flux.shape[0] // lax.axis_size("chan")

time: 577 us -> 384 us (0.67)
  local copies, waits for them, and re-layouts: 429 us -> 70.5 us
  Pallas kernels: 0 us -> 156 us
  other arithmetic: 75.1 us -> 84.3 us
    gather x4 -> x0, local copies, waits for them, and re-layouts: 362 us -> none  [the longest x2 181 us: interpolate(): lower_pair = (1.0 - frac_x) * values[corner] + frac_x * values[corner + 1]]
    pallas_call x0 -> x1, Pallas kernels: none -> 156 us  [interpolate_kernel(): pl.pallas_call(_interp_kernel, grid_spec=pltpu.PrefetchScalarGridSpec(num...]
    concatenate x0 -> x2, other arithmetic: none -> 6.81 us  [interpolate_kernel(): pair = jnp.concatenate([screen2d, jnp.roll(screen2d, -1, axis=0)], axis=1)]
  transfers between devices with their start and end apart: 2 -> 2, of which waited for: 1 -> 1; matrix products, arithmetic and copies ran while one was open for 1% -> 4% of each run, Pallas kernels for 0% -> 0%
where the time goes in v1:
time: 384 us; the launch traced here: 383 us
  Pallas kernels  156 us (41%)
  other arithmetic  84.3 us (22%)
  local copies, waits for them, and re-layouts  70.5 us (18%)
  blocking collectives  45.6 us (12%)
  starting transfers between devices  10.9 us (3%)
  matrix products  8.92 us (2%)
  waiting for transfers between devices  6.79 us (2%)
    pallas_call x1, Pallas kernels, interpolate_kernel(): pl.pallas_call(_interp_kernel, grid_spec=pltpu.PrefetchScalarGridSpec(num...  156 us
    another operation x1, other arithmetic  62.5 us
    scatter x1, local copies, waits for them, and re-layouts, body(): jnp.zeros((queries + 1,), jnp.float32).at[query_dest.reshape(-1)]  60.4 us
    all_gather x1, blocking collectives, body(): lax.all_gather(station_rows, 'stn', axis=0, tiled=True)  21.8 us
    all_gather x1, blocking collectives, body(): lax.all_gather(iono_phase, 'stn', axis=0, tiled=True)  19.4 us
    dot_general x1, matrix products, body(): jnp.einsum('ack,nck->can', weighted, make_phasors(lax.all_gather(station_...  8.92 us
  transfers between devices with their start and end apart: 2, of which 1 were waited for; matrix products, arithmetic and copies ran while one was open for 4% of the time, Pallas kernels for 0%

profile of v1, /device:TPU:0, one launch (start us, length us, event | category | flops | bytes accessed | tf_op | source)
XLA Modules:
  0.0 383.1 jit_solution(15572802750224115253)
XLA Ops:
  0.0 0.0 copy-start
  0.0 1.8 copy.30
  1.8 7.4 %all-to-all-start = ((f32[2,16,1024]{2,0,1:T(2,128)}), f32[2,16,1024]{2,0,1:T(2,128)S(1)}, u32[]{:S(2)}, u32[]{:S(2)}) async-start(f32[2,16,1024]{2,0,1:T(2,128)} %bitcast.32), calls=%async_computation | async-start | bytes 262144 | tf_op jit(solution)/shard_map/all_to_all | solution.py:133
  9.2 0.7 slice.68
  9.9 0.0 copy-start.2
  9.9 3.2 slice.67
  13.1 0.0 copy-done
  13.1 1.7 concatenate.27
  14.9 0.0 copy-done.2
  14.9 0.1 copy.18
  14.9 0.1 compare_select_fusion
  15.0 0.0 copy-start.5
  15.0 0.0 copy-start.3
  15.0 0.0 copy-start.4
  15.0 1.8 pad_maximum_fusion.1
  16.8 1.7 concatenate.29
  18.6 0.0 copy-done.5
  18.6 0.0 copy-done.3
  18.6 21.8 %all-gather = f32[16,16,3]{1,2,0:T(4,128)S(1)} all-gather(f32[1,16,3]{1,2,0:T(4,128)S(1)} %bitcast.47), channel_id=1, replica_groups=mesh['stn'=16,'chan'=2] {'stn'}, dimensions={0}, use_global_device_ids=true | all-gather | bytes 3264 | tf_op jit(solution)/shard_map/all_gather | solution.py:156
  40.4 0.1 reshape.304
  40.5 0.0 copy-done.4
  40.5 0.0 copy-start.6
  40.6 0.0 copy-start.7
  40.6 5.0 %pad_maximum_fusion.s_ref = f32[1024,8,128]{2,1,0:T(8,128)} fusion(f32[1024,4,128]{2,1,0:T(4,128)} %concatenate.29, f32[1024,4,128]{2,1,0:T(4,128)} %concatenate.27), kind=kLoop, calls=%fused_computation.8 | loop fusion | flops 1048576 | bytes 8388608 | tf_op jit(solution)/shard_map/concatenate | solution.py:73
  45.6 0.0 copy-done.6
  45.6 0.0 copy-done.7
  45.6 0.1 multiply_multiply_fusion
  45.7 0.1 multiply_add_fusion.1
  45.8 0.2 multiply_add_fusion
  45.9 0.0 all-to-all-done
  46.0 0.0 copy-start.1
  46.1 0.6 copy.19
  46.7 0.0 copy-done.1
  46.7 155.9 %shard_map.82 = f32[16384,1]{1,0:T(8,128)} custom-call(s32[16384]{0:T(1024)} %bitcast.37, f32[2,16384]{1,0:T(2,128)} %bitcast.36, f32[1024,8,128]{2,1,0:T(8,128)} %pad_maximum_fusion.s_ref), custom_call_target="tpu_custom_call" | custom-call | tf_op jit(solution)/shard_map/pallas_call | solution.py:75
  202.6 5.3 %reduce = f32[16384]{0:T(1024)} reduce(f32[16384,1]{1,0:T(8,128)} %shard_map.82, f32[]{:T(128)} %constant.28), dimensions={1}, to_apply=%pallas_call.3.reduce_sub_computation | reduce | bytes 131076 | tf_op jit(solution)/shard_map/pallas_call | solution.py:75
  207.9 3.5 all-to-all-start.1
  211.4 0.1 iota_compare_fusion
  211.4 6.8 %all-to-all-done.1 = f32[16,1,1024]{2,1,0:T(1,128)S(1)} async-done(((f32[16,1,1024]{2,1,0:T(1,128)}), f32[16,1,1024]{2,1,0:T(1,128)S(1)}, u32[]{:S(2)}, u32[]{:S(2)}) %all-to-all-start.1) | async-done | bytes 65568 | tf_op jit(solution)/shard_map/all_to_all | solution.py:137
  218.2 60.4 %scatter_custom_fusion = f32[4097]{0:T(1024)S(1)} fusion(s32[16384]{0:T(1024)S(1)} %bitcast.39, f32[16384]{0:T(1024)S(1)} %bitcast.40, f32[]{:T(128)} %constant.5.clone.1), kind=kCustom, calls=%fused_computation.34 | custom fusion | bytes 16392 | tf_op jit(solution)/shard_map/scatter | solution.py:142
  278.6 4.4 %all_gather.9 = f32[16,512]{1,0:T(8,128)S(1)} all-gather(f32[16,256]{1,0:T(8,128)S(1)} %reshape.293), channel_id=1, replica_groups=mesh['stn'=16,'chan'=2] {'chan'}, dimensions={1}, use_global_device_ids=true | all-gather | bytes 49152 | tf_op jit(solution)/shard_map/all_gather | solution.py:145
  283.0 19.4 %all_gather.11 = f32[256,512]{1,0:T(8,128)S(1)} all-gather(f32[16,512]{1,0:T(8,128)S(1)} %all_gather.9), channel_id=1, replica_groups=mesh['stn'=16,'chan'=2] {'stn'}, dimensions={0}, use_global_device_ids=true | all-gather | bytes 557056 | tf_op jit(solution)/shard_map/all_gather | solution.py:157
  302.4 3.9 %fusion.18 = bf16[16,32,512]{2,0,1:T(8,128)(2,1)S(1)} fusion(f32[32,512]{1,0:T(8,128)S(1)} %multiply_multiply_fusion, f32[32]{0:T(128)S(1)} %copy-done.4, f32[16,512]{1,0:T(8,128)S(1)} %all_gather.9, f32[16,512]{1,0:T(8,128)S(1)} %multiply_add_fusion.1, f32[32]{0:T(128)S(1)} %get-tuple-element.19), kind=kLoop, calls=%fused_computation.42 | loop fusion | flops 2621440 | bytes 655616 | tf_op jit(solution)/shard_map/neg | solution.py:113
  306.3 4.3 %multiply_convert_fusion.1 = (bf16[16,32,512]{2,0,1:T(8,128)(2,1)S(1)}, bf16[16,32,512]{2,0,1:T(8,128)(2,1)S(1)}) fusion(f32[32,512]{1,0:T(8,128)S(1)} %multiply_multiply_fusion, f32[32]{0:T(128)S(1)} %copy-done.4, f32[16,512]{1,0:T(8,128)S(1)} %all_gather.9, f32[16,512]{1,0:T(8,128)S(1)} %multiply_add_fusion.1, f32[32]{0:T(128)S(1)} %get-tuple-element.19), kind=kLoop, calls=%fused_computation.20 | loop fusion | flops 2883584 | bytes 1179904 | tf_op jit(solution)/shard_map/convert_element_type | solution.py:110
  310.6 62.5 %cosine_convert_fusion = (bf16[256,32,512]{2,0,1:T(8,128)(2,1)}, bf16[256,32,512]{2,0,1:T(8,128)(2,1)}) fusion(f32[32]{0:T(128)S(1)} %copy-done.4, f32[256,512]{1,0:T(8,128)S(1)} %all_gather.11, f32[256,512]{1,0:T(8,128)S(1)} %multiply_add_fusion, f32[32]{0:T(128)S(1)} %get-tuple-element.19), kind=kLoop, calls=%fused_computation.7 | loop fusion | flops 20971520 | bytes 17826048 | tf_op jit(solution)/shard_map/convert
  373.1 8.9 %fusion = f32[32,32,256]{2,1,0:T(8,128)S(1)} fusion(bf16[256,32,512]{2,0,1:T(8,128)(2,1)} %get-tuple-element.6, bf16[256,32,512]{2,0,1:T(8,128)(2,1)} %get-tuple-element.5, bf16[16,32,512]{2,0,1:T(8,128)(2,1)S(1)} %fusion.18, bf16[16,32,512]{2,0,1:T(8,128)(2,1)S(1)} %get-tuple-element.8, bf16[16,32,512]{2,0,1:T(8,128)(2,1)S(1)} %get-tuple-element.7), kind=kOutput, calls=%fused_computation.2 | convolution fusion | flops 578813952 | bytes 19398656 | tf_op jit(solution)/shard_map/ack,nck->can/dot_general | solution.py:152
  382.0 1.1 broadcast_select_fusion
  (10 shorter events, 0.1 us)
Async XLA Ops:
  0.0 13.1 %copy-start = (f32[2,512,512]{2,1,0:T(8,128)S(1)}, f32[2,512,512]{2,1,0:T(8,128)}, u32[]{:S(2)}) copy-start(f32[2,512,512]{2,1,0:T(8,128)} %param.8) | copy-start | bytes 6291460
  1.8 44.1 %all-to-all-start = ((f32[2,16,1024]{2,0,1:T(2,128)}), f32[2,16,1024]{2,0,1:T(2,128)S(1)}, u32[]{:S(2)}, u32[]{:S(2)}) async-start(f32[2,16,1024]{2,0,1:T(2,128)} %bitcast.32), calls=%async_computation | async-start | bytes 262144 | tf_op jit(solution)/shard_map/all_to_all | solution.py:133
  9.9 4.9 %copy-start.2 = (s32[1,1,16,1024]{3,2,1,0:T(8,128)S(1)}, s32[1,1,16,1024]{3,2,1,0:T(8,128)}, u32[]{:S(2)}) copy-start(s32[1,1,16,1024]{3,2,1,0:T(8,128)} %param.10) | copy-start | bytes 196612
  15.0 3.6 copy-start.5
  15.0 3.6 copy-start.3
  15.0 25.5 %copy-start.4 = (f32[32]{0:T(128)S(1)}, f32[32]{0:T(128)}, u32[]{:S(2)}) copy-start(f32[32]{0:T(128)} %param.13) | copy-start | bytes 388
  40.5 5.0 %copy-start.6 = (f32[512]{0:T(512)S(1)}, f32[512]{0:T(512)}, u32[]{:S(2)}) copy-start(f32[512]{0:T(512)} %param.15) | copy-start | bytes 6148
  40.6 5.0 %copy-start.7 = (f32[512]{0:T(512)S(1)}, f32[512]{0:T(512)}, u32[]{:S(2)}) copy-start(f32[512]{0:T(512)} %param.14) | copy-start | bytes 6148
  46.0 0.7 copy-start.1
  207.9 10.4 %all-to-all-start.1 = ((f32[16,1,1024]{2,1,0:T(1,128)}), f32[16,1,1024]{2,1,0:T(1,128)S(1)}, u32[]{:S(2)}, u32[]{:S(2)}) async-start(f32[16,1,1024]{2,1,0:T(1,128)} %bitcast.18), calls=%async_computation.1 | async-start | bytes 131072 | tf_op jit(solution)/shard_map/all_to_all | solution.py:137

commit v2 on v1

--- a/solution.py
+++ b/solution.py
@@ -142,8 +142,38 @@
         jnp.zeros((queries + 1,), jnp.float32).at[query_dest.reshape(-1)].set(returned.reshape(-1))
     )
     own_iono = buffer[:queries].reshape(stations_local, local_sources)
+    station_rows = positions.T
+    total_stations = stations_local * groups
+    channels = freq_ratio.shape[0]
+    n_chan = lax.axis_size("chan")
+    if channels % groups:
+        return _rows_path(own_iono, station_rows, directions, freq_ratio, source_flux, spectral_index)
+    packed = jnp.concatenate([own_iono, station_rows], axis=1)
+    gathered = lax.all_gather(packed, ("stn", "chan"), axis=0, tiled=False)
+    gathered = gathered.reshape(groups, n_chan, stations_local, local_sources + 3)
+    all_iono = (
+        gathered[:, :, :, :local_sources]
+        .transpose(0, 2, 1, 3)
+        .reshape(total_stations, n_chan * local_sources)
+    )
+    all_rows = gathered[:, 0, :, local_sources:].reshape(total_stations, 3)
+    per_dev = channels // groups
+    my_freq = lax.dynamic_slice_in_dim(freq_ratio, lax.axis_index("stn") * per_dev, per_dev)
+    phasors = make_phasors(all_rows, all_iono, directions, my_freq)
+    intensity = spectrum(source_flux, spectral_index, my_freq, source_flux.shape[0])
+    weighted = weight_rows(phasors, intensity)
+    columns = jnp.einsum("ack,nck->can", weighted, phasors, preferred_element_type=jnp.float32)
+    visible = columns.reshape(per_dev, 2, total_stations, total_stations)
+    ids = jnp.arange(total_stations, dtype=jnp.int32)
+    cross_only = ids[:, None] != ids[None, :]
+    visible = jnp.where(cross_only[None, None], visible, jnp.zeros_like(visible))
+    return lax.all_to_all(visible, "stn", split_axis=2, concat_axis=0, tiled=True)
+
+
+def _rows_path(own_iono, station_rows, directions, freq_ratio, source_flux, spectral_index):
+    groups = lax.axis_size("stn")
+    stations_local = station_rows.shape[0]
     iono_phase = lax.all_gather(own_iono, "chan", axis=1, tiled=True)
-    station_rows = positions.T
     own_phasors = make_phasors(station_rows, iono_phase, directions, freq_ratio)
     intensity = spectrum(source_flux, spectral_index, freq_ratio, source_flux.shape[0])
     weighted = weight_rows(own_phasors, intensity)

time: 384 us -> 368 us (0.958)
  other arithmetic: 84.3 us -> 21.4 us
  blocking collectives: 45.6 us -> 96.3 us
  matrix products: 8.92 us -> 0.98 us
    another operation x1 -> x0, other arithmetic: 62.5 us -> none
    all_to_all x0 -> x1, blocking collectives: none -> 27.3 us  [body(): lax.all_to_all(visible, 'stn', split_axis=2, concat_axis=0, tiled=True)]
    all_gather x3 -> x1, blocking collectives: 45.6 us -> 69 us  [body(): gathered = lax.all_gather(packed, ('stn', 'chan'), axis=0, tiled=False)]
    dot_general x1, matrix products: 8.92 us -> 0.98 us  [body(): jnp.einsum('ack,nck->can', weighted, phasors, preferred_element_type=jnp....]
where the time goes in v2:
time: 368 us; the launch traced here: 367 us
  Pallas kernels  156 us (42%)
  blocking collectives  96.3 us (26%)
  local copies, waits for them, and re-layouts  71.8 us (20%)
  other arithmetic  21.4 us (6%)
  starting transfers between devices  13.4 us (4%)
  waiting for transfers between devices  6.76 us (2%)
    pallas_call x1, Pallas kernels, interpolate_kernel(): pl.pallas_call(_interp_kernel, grid_spec=pltpu.PrefetchScalarGridSpec(num...  156 us
    all_gather x1, blocking collectives, body(): gathered = lax.all_gather(packed, ('stn', 'chan'), axis=0, tiled=False)  69 us
    scatter x1, local copies, waits for them, and re-layouts, body(): jnp.zeros((queries + 1,), jnp.float32).at[query_dest.reshape(-1)]  60.4 us
    all_to_all x1, blocking collectives, body(): lax.all_to_all(visible, 'stn', split_axis=2, concat_axis=0, tiled=True)  27.3 us
    all_to_all x1, starting transfers between devices, body(): lax.all_to_all(coords, 'stn', split_axis=1, concat_axis=1, tiled=True)  7.39 us
  transfers between devices with their start and end apart: 2, of which 1 were waited for; matrix products, arithmetic and copies ran while one was open for 4% of the time, Pallas kernels for 0%

profile of v2, /device:TPU:0, one launch (start us, length us, event | category | flops | bytes accessed | tf_op | source)
XLA Modules:
  0.0 366.8 jit_solution(17315598592253938863)
XLA Ops:
  0.0 1.7 copy.59
  1.7 7.4 %all-to-all-start = ((f32[2,16,1024]{2,0,1:T(2,128)}), f32[2,16,1024]{2,0,1:T(2,128)S(1)}, u32[]{:S(2)}, u32[]{:S(2)}) async-start(f32[2,16,1024]{2,0,1:T(2,128)} %bitcast.33), calls=%async_computation | async-start | bytes 262144 | tf_op jit(solution)/shard_map/all_to_all | solution.py:133
  9.1 0.0 copy-start
  9.1 3.3 slice.60
  12.4 0.0 copy-done
  12.4 1.7 concatenate.28
  14.1 1.8 pad_maximum_fusion.1
  15.9 0.0 copy-start.2
  15.9 0.0 copy-start.7
  15.9 0.0 copy-start.4
  15.9 0.0 copy-start.5
  16.0 1.8 concatenate.30
  17.7 0.0 copy-done.2
  17.7 0.1 copy.45
  17.8 0.1 compare_select_fusion
  17.9 0.0 copy-done.7
  17.9 0.1 fusion.19
  18.0 0.0 copy-done.4
  18.0 0.0 copy-done.5
  18.0 0.1 multiply_multiply_fusion
  18.0 0.0 copy-start.3
  18.0 5.0 %pad_maximum_fusion.s_ref = f32[1024,8,128]{2,1,0:T(8,128)} fusion(f32[1024,4,128]{2,1,0:T(4,128)} %concatenate.30, f32[1024,4,128]{2,1,0:T(4,128)} %concatenate.28), kind=kLoop, calls=%fused_computation.1 | loop fusion | flops 1048576 | bytes 8388608 | tf_op jit(solution)/shard_map/concatenate | solution.py:73
  23.1 0.0 copy-done.3
  23.1 0.0 all-to-all-done
  23.1 0.0 copy-start.1
  23.2 0.6 copy.46
  23.8 0.0 copy-done.1
  23.8 155.9 %shard_map.82 = f32[16384,1]{1,0:T(8,128)} custom-call(s32[16384]{0:T(1024)} %bitcast.45, f32[2,16384]{1,0:T(2,128)} %bitcast.44, f32[1024,8,128]{2,1,0:T(8,128)} %pad_maximum_fusion.s_ref), custom_call_target="tpu_custom_call" | custom-call | tf_op jit(solution)/shard_map/pallas_call | solution.py:75
  179.7 5.3 %reduce = f32[16384]{0:T(1024)} reduce(f32[16384,1]{1,0:T(8,128)} %shard_map.82, f32[]{:T(128)} %constant.31), dimensions={1}, to_apply=%pallas_call.3.reduce_sub_computation | reduce | bytes 131076 | tf_op jit(solution)/shard_map/pallas_call | solution.py:75
  185.0 6.0 %all-to-all-start.1 = ((f32[16,1,1024]{2,1,0:T(1,128)}), f32[16,1,1024]{2,1,0:T(1,128)S(1)}, u32[]{:S(2)}, u32[]{:S(2)}) async-start(f32[16,1,1024]{2,1,0:T(1,128)} %bitcast.20), calls=%async_computation.1 | async-start | bytes 131072 | tf_op jit(solution)/shard_map/all_to_all | solution.py:137
  191.0 0.0 copy-done.6
  191.0 0.1 copy.34
  191.2 6.8 %all-to-all-done.1 = f32[16,1,1024]{2,1,0:T(1,128)S(1)} async-done(((f32[16,1,1024]{2,1,0:T(1,128)}), f32[16,1,1024]{2,1,0:T(1,128)S(1)}, u32[]{:S(2)}, u32[]{:S(2)}) %all-to-all-start.1) | async-done | bytes 65568 | tf_op jit(solution)/shard_map/all_to_all | solution.py:137
  197.9 60.4 %scatter_custom_fusion = f32[4097]{0:T(1024)S(1)} fusion(s32[16384]{0:T(1024)S(1)} %bitcast.47, f32[16384]{0:T(1024)S(1)} %bitcast.48, f32[]{:T(128)} %constant.6.clone.1), kind=kCustom, calls=%fused_computation.31 | custom fusion | bytes 16392 | tf_op jit(solution)/shard_map/scatter | solution.py:142
  258.3 69.0 %all-gather = f32[512,259]{1,0:T(8,128)S(1)} all-gather(f32[16,259]{1,0:T(8,128)S(1)} %pad_maximum_fusion.2), channel_id=2, replica_groups=mesh['stn'=16,'chan'=2] {'stn','chan'}, dimensions={0}, use_global_device_ids=true | all-gather | bytes 547008 | tf_op jit(solution)/shard_map/all_gather | solution.py:152
  327.3 0.1 slice_bitcast_fusion
  327.4 0.1 fusion.20
  327.5 0.1 copy.43
  327.6 0.1 copy.44
  327.7 0.1 copy.42
  327.8 0.4 copy.38
  328.2 0.2 multiply_add_fusion
  328.4 3.9 %fusion.18 = (bf16[256,2,512]{2,0,1:T(8,128)(2,1)S(1)}, bf16[256,2,512]{2,0,1:T(8,128)(2,1)S(1)}, bf16[256,2,512]{2,0,1:T(8,128)(2,1)S(1)}) fusion(f32[2,512]{1,0:T(2,128)S(1)} %multiply_multiply_fusion, f32[2]{0:T(128)S(1)} %get-tuple-element.11, f32[256,512]{1,0:T(8,128)S(1)} %bitcast.36, f32[256,512]{1,0:T(8,128)S(1)} %multiply_add_fusion, ...), kind=kLoop, calls=%fused_computation.36 | loop fusion | flops 2621440 | bytes 2625552 | tf_op jit(solution)/shard_map/neg | solution.py:113
  332.4 3.9 %multiply_convert_fusion = (bf16[256,2,512]{2,0,1:T(8,128)(2,1)S(1)}, bf16[256,2,512]{2,0,1:T(8,128)(2,1)S(1)}) fusion(f32[2,512]{1,0:T(2,128)S(1)} %multiply_multiply_fusion, f32[2]{0:T(128)S(1)} %get-tuple-element.11, f32[256,512]{1,0:T(8,128)S(1)} %bitcast.37, f32[256,512]{1,0:T(8,128)S(1)} %multiply_add_fusion, f32[2]{0:T(128)S(1)} %broadcast_multiply_fusion), kind=kLoop, calls=%fused_computation.16 | loop fusion | flops 1835008 | bytes 2101264 | tf_op jit(solution)/shard_map/convert_element_type | solution.py:111
  336.3 1.0 fusion
  337.3 1.1 copy_select_fusion
  338.4 27.3 %all_to_all.33 = f32[2,2,256,256]{3,1,0,2:T(2,128)S(1)} all-to-all(f32[2,2,256,256]{3,1,0,2:T(2,128)S(1)} %copy_select_fusion), channel_id=1, replica_groups=mesh['stn'=16,'chan'=2] {'stn'}, dimensions={2} | all-to-all | bytes 2097152 | tf_op jit(solution)/shard_map/all_to_all | solution.py:170
  365.7 1.2 copy.40
  (12 shorter events, 0.2 us)
Async XLA Ops:
  1.7 21.4 %all-to-all-start = ((f32[2,16,1024]{2,0,1:T(2,128)}), f32[2,16,1024]{2,0,1:T(2,128)S(1)}, u32[]{:S(2)}, u32[]{:S(2)}) async-start(f32[2,16,1024]{2,0,1:T(2,128)} %bitcast.33), calls=%async_computation | async-start | bytes 262144 | tf_op jit(solution)/shard_map/all_to_all | solution.py:133
  9.1 3.3 copy-start
  15.9 1.8 copy-start.2
  15.9 1.9 copy-start.7
  15.9 2.0 copy-start.4
  15.9 2.0 copy-start.5
  18.0 5.0 %copy-start.3 = (f32[3,512]{1,0:T(4,128)S(1)}, f32[3,512]{1,0:T(4,128)}, u32[]{:S(2)}) copy-start(f32[3,512]{1,0:T(4,128)} %param.12) | copy-start | bytes 18436
  23.1 0.7 copy-start.1
  179.7 11.3 %copy-start.6 = (f32[3,16]{1,0:T(4,128)S(1)}, f32[3,16]{1,0:T(4,128)}, u32[]{:S(2)}) copy-start(f32[3,16]{1,0:T(4,128)} %param.11) | copy-start | bytes 580
  185.0 12.9 %all-to-all-start.1 = ((f32[16,1,1024]{2,1,0:T(1,128)}), f32[16,1,1024]{2,1,0:T(1,128)S(1)}, u32[]{:S(2)}, u32[]{:S(2)}) async-start(f32[16,1,1024]{2,1,0:T(1,128)} %bitcast.20), calls=%async_computation.1 | async-start | bytes 131072 | tf_op jit(solution)/shard_map/all_to_all | solution.py:137

commit v3 on v2

--- a/solution.py
+++ b/solution.py
@@ -148,15 +148,11 @@
     n_chan = lax.axis_size("chan")
     if channels % groups:
         return _rows_path(own_iono, station_rows, directions, freq_ratio, source_flux, spectral_index)
-    packed = jnp.concatenate([own_iono, station_rows], axis=1)
-    gathered = lax.all_gather(packed, ("stn", "chan"), axis=0, tiled=False)
-    gathered = gathered.reshape(groups, n_chan, stations_local, local_sources + 3)
-    all_iono = (
-        gathered[:, :, :, :local_sources]
-        .transpose(0, 2, 1, 3)
-        .reshape(total_stations, n_chan * local_sources)
-    )
-    all_rows = gathered[:, 0, :, local_sources:].reshape(total_stations, 3)
+    iono_phase = lax.all_gather(own_iono, "chan", axis=1, tiled=True)
+    packed = jnp.concatenate([iono_phase, station_rows], axis=1)
+    gathered = lax.all_gather(packed, "stn", axis=0, tiled=True)
+    all_iono = gathered[:, : n_chan * local_sources]
+    all_rows = gathered[:, n_chan * local_sources :]
     per_dev = channels // groups
     my_freq = lax.dynamic_slice_in_dim(freq_ratio, lax.axis_index("stn") * per_dev, per_dev)
     phasors = make_phasors(all_rows, all_iono, directions, my_freq)

time: 368 us -> 322 us (0.88)
  blocking collectives: 96.3 us -> 51.3 us
    all_gather x1 -> x2, blocking collectives: 69 us -> 24 us  [the longest x1 19.6 us: body(): gathered = lax.all_gather(packed, 'stn', axis=0, tiled=True)]
where the time goes in v3:
time: 322 us; the launch traced here: 321 us
  Pallas kernels  156 us (48%)
  local copies, waits for them, and re-layouts  71.3 us (22%)
  blocking collectives  51.3 us (16%)
  other arithmetic  21.4 us (7%)
  starting transfers between devices  13.4 us (4%)
  waiting for transfers between devices  6.76 us (2%)
    pallas_call x1, Pallas kernels, interpolate_kernel(): pl.pallas_call(_interp_kernel, grid_spec=pltpu.PrefetchScalarGridSpec(num...  156 us
    scatter x1, local copies, waits for them, and re-layouts, body(): jnp.zeros((queries + 1,), jnp.float32).at[query_dest.reshape(-1)]  60.4 us
    all_to_all x1, blocking collectives, body(): lax.all_to_all(visible, 'stn', split_axis=2, concat_axis=0, tiled=True)  27.3 us
    all_gather x1, blocking collectives, body(): gathered = lax.all_gather(packed, 'stn', axis=0, tiled=True)  19.6 us
    all_to_all x1, starting transfers between devices, body(): lax.all_to_all(coords, 'stn', split_axis=1, concat_axis=1, tiled=True)  7.39 us
    concatenate x2, other arithmetic, interpolate_kernel(): pair = jnp.concatenate([screen2d, jnp.roll(screen2d, -1, axis=0)], axis=1)  6.77 us
    all_to_all x1, waiting for transfers between devices, body(): lax.all_to_all(sampled, 'stn', split_axis=0, concat_axis=0, tiled=True)  6.76 us
  transfers between devices with their start and end apart: 2, of which 1 were waited for; matrix products, arithmetic and copies ran while one was open for 4% of the time, Pallas kernels for 0%

profile of v3, /device:TPU:0, one launch (start us, length us, event | category | flops | bytes accessed | tf_op | source)
XLA Modules:
  0.0 321.2 jit_solution(4062518012633260387)
XLA Ops:
  0.0 1.7 copy.40
  1.7 7.4 %all-to-all-start = ((f32[2,16,1024]{2,0,1:T(2,128)}), f32[2,16,1024]{2,0,1:T(2,128)S(1)}, u32[]{:S(2)}, u32[]{:S(2)}) async-start(f32[2,16,1024]{2,0,1:T(2,128)} %bitcast.23), calls=%async_computation | async-start | bytes 262144 | tf_op jit(solution)/shard_map/all_to_all | solution.py:133
  9.1 0.0 copy-start
  9.1 3.3 %slice.60 = f32[1023,512]{1,0:T(8,128)} slice(f32[1024,512]{1,0:T(8,128)} %bitcast.24), slice={[1:1024], [0:512]} | slice | bytes 4190208 | tf_op jit(solution)/shard_map/jit(_roll_static)/slice | solution.py:73
  12.4 0.0 copy-done
  12.4 1.7 concatenate.28
  14.1 1.8 pad_maximum_fusion.1
  15.9 0.0 copy-start.2
  15.9 0.0 copy-start.7
  15.9 0.0 copy-start.4
  16.0 0.0 copy-start.5
  16.0 1.7 concatenate.30
  17.7 0.0 copy-done.2
  17.7 0.1 copy.27
  17.8 0.1 compare_select_fusion
  17.9 0.0 copy-done.7
  17.9 0.1 fusion.19
  17.9 0.0 copy-done.4
  18.0 0.0 copy-done.5
  18.0 0.1 multiply_multiply_fusion
  18.0 0.0 copy-start.3
  18.0 5.0 %pad_maximum_fusion.s_ref = f32[1024,8,128]{2,1,0:T(8,128)} fusion(f32[1024,4,128]{2,1,0:T(4,128)} %concatenate.30, f32[1024,4,128]{2,1,0:T(4,128)} %concatenate.28), kind=kLoop, calls=%fused_computation.1 | loop fusion | flops 1048576 | bytes 8388608 | tf_op jit(solution)/shard_map/concatenate | solution.py:73
  23.0 0.0 copy-done.3
  23.0 0.0 all-to-all-done
  23.1 0.0 copy-start.1
  23.2 0.6 copy.28
  23.8 0.0 copy-done.1
  23.8 155.9 %shard_map.82 = f32[16384,1]{1,0:T(8,128)} custom-call(s32[16384]{0:T(1024)} %bitcast.29, f32[2,16384]{1,0:T(2,128)} %bitcast.28, f32[1024,8,128]{2,1,0:T(8,128)} %pad_maximum_fusion.s_ref), custom_call_target="tpu_custom_call" | custom-call | tf_op jit(solution)/shard_map/pallas_call | solution.py:75
  179.7 0.0 copy-start.6
  179.7 5.3 %reduce = f32[16384]{0:T(1024)} reduce(f32[16384,1]{1,0:T(8,128)} %shard_map.82, f32[]{:T(128)} %constant.31), dimensions={1}, to_apply=%pallas_call.3.reduce_sub_computation | reduce | bytes 131076 | tf_op jit(solution)/shard_map/pallas_call | solution.py:75
  185.0 6.0 %all-to-all-start.1 = ((f32[16,1,1024]{2,1,0:T(1,128)}), f32[16,1,1024]{2,1,0:T(1,128)S(1)}, u32[]{:S(2)}, u32[]{:S(2)}) async-start(f32[16,1,1024]{2,1,0:T(1,128)} %bitcast.14), calls=%async_computation.1 | async-start | bytes 131072 | tf_op jit(solution)/shard_map/all_to_all | solution.py:137
  191.0 0.0 copy-done.6
  191.0 0.1 copy.23
  191.1 6.8 %all-to-all-done.1 = f32[16,1,1024]{2,1,0:T(1,128)S(1)} async-done(((f32[16,1,1024]{2,1,0:T(1,128)}), f32[16,1,1024]{2,1,0:T(1,128)S(1)}, u32[]{:S(2)}, u32[]{:S(2)}) %all-to-all-start.1) | async-done | bytes 65568 | tf_op jit(solution)/shard_map/all_to_all | solution.py:137
  197.9 60.4 %scatter_custom_fusion = f32[4097]{0:T(1024)S(1)} fusion(s32[16384]{0:T(1024)S(1)} %bitcast.31, f32[16384]{0:T(1024)S(1)} %bitcast.32, f32[]{:T(128)} %constant.6.clone.1), kind=kCustom, calls=%fused_computation.33 | custom fusion | bytes 16392 | tf_op jit(solution)/shard_map/scatter | solution.py:142
  258.3 4.4 %all_gather.6 = f32[16,512]{1,0:T(8,128)S(1)} all-gather(f32[16,256]{1,0:T(8,128)S(1)} %reshape.204), channel_id=1, replica_groups=mesh['stn'=16,'chan'=2] {'chan'}, dimensions={1}, use_global_device_ids=true | all-gather | bytes 49152 | tf_op jit(solution)/shard_map/all_gather | solution.py:151
  262.7 19.6 %all_gather.7 = f32[256,515]{1,0:T(8,128)S(1)} all-gather(f32[16,515]{1,0:T(8,128)S(1)} %pad_maximum_fusion.2), channel_id=1, replica_groups=mesh['stn'=16,'chan'=2] {'stn'}, dimensions={0}, use_global_device_ids=true | all-gather | bytes 560320 | tf_op jit(solution)/shard_map/all_gather | solution.py:153
  282.3 0.3 slice_reduce_fusion.2
  282.6 0.1 slice.66
  282.6 0.2 multiply_add_fusion
  282.8 3.9 %fusion.18 = (bf16[256,2,512]{2,0,1:T(8,128)(2,1)S(1)}, bf16[256,2,512]{2,0,1:T(8,128)(2,1)S(1)}, bf16[256,2,512]{2,0,1:T(8,128)(2,1)S(1)}) fusion(f32[2,512]{1,0:T(2,128)S(1)} %multiply_multiply_fusion, f32[2]{0:T(128)S(1)} %get-tuple-element.14, f32[256,512]{1,0:T(8,128)S(1)} %slice.66, f32[256,512]{1,0:T(8,128)S(1)} %multiply_add_fusion, ...), kind=kLoop, calls=%fused_computation.38 | loop fusion | flops 2621440 | bytes 2625552 | tf_op jit(solution)/shard_map/neg | solution.py:113
  286.8 3.9 %multiply_convert_fusion = (bf16[256,2,512]{2,0,1:T(8,128)(2,1)S(1)}, bf16[256,2,512]{2,0,1:T(8,128)(2,1)S(1)}) fusion(f32[2,512]{1,0:T(2,128)S(1)} %multiply_multiply_fusion, f32[2]{0:T(128)S(1)} %get-tuple-element.14, f32[256,512]{1,0:T(8,128)S(1)} %slice.66, f32[256,512]{1,0:T(8,128)S(1)} %multiply_add_fusion, f32[2]{0:T(128)S(1)} %broadcast_multiply_fusion), kind=kLoop, calls=%fused_computation.16 | loop fusion | flops 1835008 | bytes 2101264 | tf_op jit(solution)/shard_map/convert_element_type | solution.py:111
  290.7 1.0 fusion
  291.7 1.1 copy_select_fusion
  292.8 27.3 %all_to_all.33 = f32[2,2,256,256]{3,1,0,2:T(2,128)S(1)} all-to-all(f32[2,2,256,256]{3,1,0,2:T(2,128)S(1)} %copy_select_fusion), channel_id=1, replica_groups=mesh['stn'=16,'chan'=2] {'stn'}, dimensions={2} | all-to-all | bytes 2097152 | tf_op jit(solution)/shard_map/all_to_all | solution.py:166
  320.1 1.2 copy.25
  (9 shorter events, 0.1 us)
Async XLA Ops:
  1.7 21.4 %all-to-all-start = ((f32[2,16,1024]{2,0,1:T(2,128)}), f32[2,16,1024]{2,0,1:T(2,128)S(1)}, u32[]{:S(2)}, u32[]{:S(2)}) async-start(f32[2,16,1024]{2,0,1:T(2,128)} %bitcast.23), calls=%async_computation | async-start | bytes 262144 | tf_op jit(solution)/shard_map/all_to_all | solution.py:133
  9.1 3.3 %copy-start = (f32[2,512,512]{2,1,0:T(8,128)S(1)}, f32[2,512,512]{2,1,0:T(8,128)}, u32[]{:S(2)}) copy-start(f32[2,512,512]{2,1,0:T(8,128)} %param.8) | copy-start | bytes 6291460
  15.9 1.8 copy-start.2
  15.9 1.9 copy-start.7
  15.9 2.0 copy-start.4
  16.0 2.0 copy-start.5
  18.0 5.0 %copy-start.3 = (f32[3,512]{1,0:T(4,128)S(1)}, f32[3,512]{1,0:T(4,128)}, u32[]{:S(2)}) copy-start(f32[3,512]{1,0:T(4,128)} %param.12) | copy-start | bytes 18436
  23.1 0.7 copy-start.1
  179.7 11.3 %copy-start.6 = (f32[3,16]{1,0:T(4,128)S(1)}, f32[3,16]{1,0:T(4,128)}, u32[]{:S(2)}) copy-start(f32[3,16]{1,0:T(4,128)} %param.11) | copy-start | bytes 580
  185.0 12.9 %all-to-all-start.1 = ((f32[16,1,1024]{2,1,0:T(1,128)}), f32[16,1,1024]{2,1,0:T(1,128)S(1)}, u32[]{:S(2)}, u32[]{:S(2)}) async-start(f32[16,1,1024]{2,1,0:T(1,128)} %bitcast.14), calls=%async_computation.1 | async-start | bytes 131072 | tf_op jit(solution)/shard_map/all_to_all | solution.py:137

commit v4 on v3

--- a/solution.py
+++ b/solution.py
@@ -25,7 +25,7 @@
     return (1.0 - frac_y) * lower_pair + frac_y * upper_pair
 
 
-UNROLL = 16
+UNROLL = 32
 
 
 def _interp_kernel(r_ref, c_ref, s_ref, o_ref):
@@ -83,6 +83,27 @@
         out_shape=jax.ShapeDtypeStruct((q, 1), jnp.float32),
     )(r, coords, pair)
     return out[:, 0]
+
+
+def _scatter_kernel(d_ref, v_ref, o_ref):
+    def body(i, carry):
+        o_ref[d_ref[i]] = v_ref[i]
+        return carry
+
+    lax.fori_loop(0, d_ref.shape[0], body, 0, unroll=16)
+
+
+def scatter_kernel(dest, vals, size):
+    return pl.pallas_call(
+        _scatter_kernel,
+        grid_spec=pltpu.PrefetchScalarGridSpec(
+            num_scalar_prefetch=2,
+            grid=(1,),
+            in_specs=[],
+            out_specs=pl.BlockSpec((size,), lambda i, d, v: (0,), memory_space=pltpu.SMEM),
+        ),
+        out_shape=jax.ShapeDtypeStruct((size,), jnp.float32),
+    )(dest, vals)
 
 
 def make_phasors(station_rows, iono_rows, directions, freq_ratio):
@@ -138,9 +159,7 @@
     stations_local = positions.shape[1]
     local_sources = source_flux.shape[0] // lax.axis_size("chan")
     queries = stations_local * local_sources
-    buffer = (
-        jnp.zeros((queries + 1,), jnp.float32).at[query_dest.reshape(-1)].set(returned.reshape(-1))
-    )
+    buffer = scatter_kernel(query_dest.reshape(-1), returned.reshape(-1), queries + 1)
     own_iono = buffer[:queries].reshape(stations_local, local_sources)
     station_rows = positions.T
     total_stations = stations_local * groups

time: 322 us -> 250 us (0.78)
  local copies, waits for them, and re-layouts: 71.3 us -> 12.9 us
  Pallas kernels: 156 us -> 143 us
    scatter x1 -> x0, local copies, waits for them, and re-layouts: 60.4 us -> none  [body(): jnp.zeros((queries + 1,), jnp.float32).at[query_dest.reshape(-1)]]
    pallas_call x1, Pallas kernels: 156 us -> 111 us  [interpolate_kernel(): pl.pallas_call(_interp_kernel, grid_spec=pltpu.PrefetchScalarGridSpec(num...]
    pallas_call x0 -> x1, Pallas kernels: none -> 31.6 us  [scatter_kernel(): pl.pallas_call(_scatter_kernel, grid_spec=pltpu.PrefetchScalarGridSpec(nu...]
  transfers between devices with their start and end apart: 2 -> 2, of which waited for: 1 -> 1; matrix products, arithmetic and copies ran while one was open for 4% -> 6% of each run, Pallas kernels for 0% -> 0%
where the time goes in v4:
time: 250 us; the launch traced here: 249 us
  Pallas kernels  143 us (57%)
  blocking collectives  51.3 us (21%)
  other arithmetic  21.3 us (9%)
  starting transfers between devices  13.4 us (5%)
  local copies, waits for them, and re-layouts  12.9 us (5%)
  waiting for transfers between devices  6.12 us (2%)
    pallas_call x1, Pallas kernels, interpolate_kernel(): pl.pallas_call(_interp_kernel, grid_spec=pltpu.PrefetchScalarGridSpec(num...  111 us
    pallas_call x1, Pallas kernels, scatter_kernel(): pl.pallas_call(_scatter_kernel, grid_spec=pltpu.PrefetchScalarGridSpec(nu...  31.6 us
    all_to_all x1, blocking collectives, body(): lax.all_to_all(visible, 'stn', split_axis=2, concat_axis=0, tiled=True)  27.3 us
    all_gather x1, blocking collectives, body(): gathered = lax.all_gather(packed, 'stn', axis=0, tiled=True)  19.6 us
    all_to_all x1, starting transfers between devices, body(): lax.all_to_all(coords, 'stn', split_axis=1, concat_axis=1, tiled=True)  7.39 us
    concatenate x2, other arithmetic, interpolate_kernel(): pair = jnp.concatenate([screen2d, jnp.roll(screen2d, -1, axis=0)], axis=1)  6.8 us
    all_to_all x1, waiting for transfers between devices, body(): lax.all_to_all(sampled, 'stn', split_axis=0, concat_axis=0, tiled=True)  6.12 us
    all_to_all x1, starting transfers between devices, body(): lax.all_to_all(sampled, 'stn', split_axis=0, concat_axis=0, tiled=True)  6.01 us
  transfers between devices with their start and end apart: 2, of which 1 were waited for; matrix products, arithmetic and copies ran while one was open for 6% of the time, Pallas kernels for 0%

profile of v4, /device:TPU:0, one launch (start us, length us, event | category | flops | bytes accessed | tf_op | source)
XLA Modules:
  0.0 249.3 jit_solution(4238129509823344737)
XLA Ops:
  0.0 1.7 copy.40
  1.7 7.4 %all-to-all-start = ((f32[2,16,1024]{2,0,1:T(2,128)}), f32[2,16,1024]{2,0,1:T(2,128)S(1)}, u32[]{:S(2)}, u32[]{:S(2)}) async-start(f32[2,16,1024]{2,0,1:T(2,128)} %bitcast.20), calls=%async_computation | async-start | bytes 262144 | tf_op jit(solution)/shard_map/all_to_all | solution.py:154
  9.1 0.0 copy-start
  9.1 3.3 %slice.60 = f32[1023,512]{1,0:T(8,128)} slice(f32[1024,512]{1,0:T(8,128)} %bitcast.21), slice={[1:1024], [0:512]} | slice | bytes 4190208 | tf_op jit(solution)/shard_map/jit(_roll_static)/slice | solution.py:73
  12.4 0.0 copy-done
  12.4 1.8 concatenate.28
  14.2 1.8 pad_maximum_fusion.1
  15.9 0.0 copy-start.8
  16.0 0.0 copy-start.5
  16.0 0.0 copy-start.6
  16.0 1.7 concatenate.30
  17.7 0.0 copy-done.8
  17.7 0.1 fusion.17
  17.8 0.0 copy-done.5
  17.8 0.0 copy-done.6
  17.8 0.1 multiply_multiply_fusion
  17.9 0.0 copy-start.4
  17.9 5.0 %pad_maximum_fusion.s_ref = f32[1024,8,128]{2,1,0:T(8,128)} fusion(f32[1024,4,128]{2,1,0:T(4,128)} %concatenate.30, f32[1024,4,128]{2,1,0:T(4,128)} %concatenate.28), kind=kLoop, calls=%fused_computation | loop fusion | flops 1048576 | bytes 8388608 | tf_op jit(solution)/shard_map/concatenate | solution.py:73
  22.9 0.0 copy-done.4
  22.9 0.0 all-to-all-done
  22.9 0.0 copy-start.1
  23.0 0.6 copy.28
  23.7 0.0 copy-done.1
  23.7 111.5 %shard_map.82 = f32[16384,1]{1,0:T(8,128)} custom-call(s32[16384]{0:T(1024)} %bitcast.26, f32[2,16384]{1,0:T(2,128)} %bitcast.25, f32[1024,8,128]{2,1,0:T(8,128)} %pad_maximum_fusion.s_ref), custom_call_target="tpu_custom_call" | custom-call | tf_op jit(solution)/shard_map/pallas_call | solution.py:75
  135.1 0.0 copy-start.3
  135.1 0.0 copy-start.7
  135.1 5.3 %reduce = f32[16384]{0:T(1024)} reduce(f32[16384,1]{1,0:T(8,128)} %shard_map.82, f32[]{:T(128)} %constant.27), dimensions={1}, to_apply=%pallas_call.6.reduce_sub_computation | reduce | bytes 131076 | tf_op jit(solution)/shard_map/pallas_call | solution.py:75
  140.4 6.0 %all-to-all-start.1 = ((f32[16,1,1024]{2,1,0:T(1,128)}), f32[16,1,1024]{2,1,0:T(1,128)S(1)}, u32[]{:S(2)}, u32[]{:S(2)}) async-start(f32[16,1,1024]{2,1,0:T(1,128)} %bitcast.13), calls=%async_computation.1 | async-start | bytes 131072 | tf_op jit(solution)/shard_map/all_to_all | solution.py:158
  146.4 0.0 copy-done.3
  146.5 0.6 copy.27
  147.1 0.0 copy-done.7
  147.1 0.1 copy.23
  147.2 6.1 %all-to-all-done.1 = f32[16,1,1024]{2,1,0:T(1,128)S(1)} async-done(((f32[16,1,1024]{2,1,0:T(1,128)}), f32[16,1,1024]{2,1,0:T(1,128)S(1)}, u32[]{:S(2)}, u32[]{:S(2)}) %all-to-all-start.1) | async-done | bytes 65568 | tf_op jit(solution)/shard_map/all_to_all | solution.py:158
  153.3 0.0 copy-start.2
  153.3 0.6 copy-done.2
  154.0 31.6 %shard_map.83 = f32[4097]{0:T(1024)} custom-call(s32[16384]{0:T(1024)} %bitcast.28, f32[16384]{0:T(1024)} %bitcast.27), custom_call_target="tpu_custom_call" | custom-call | tf_op jit(solution)/shard_map/pallas_call | solution.py:97
  185.6 0.7 slice.62
  186.3 4.4 %all_gather.6 = f32[16,512]{1,0:T(8,128)S(1)} all-gather(f32[16,256]{1,0:T(8,128)S(1)} %reshape.176), channel_id=1, replica_groups=mesh['stn'=16,'chan'=2] {'chan'}, dimensions={1}, use_global_device_ids=true | all-gather | bytes 49152 | tf_op jit(solution)/shard_map/all_gather | solution.py:170
  190.7 19.6 %all_gather.7 = f32[256,515]{1,0:T(8,128)S(1)} all-gather(f32[16,515]{1,0:T(8,128)S(1)} %pad_maximum_fusion.2), channel_id=1, replica_groups=mesh['stn'=16,'chan'=2] {'stn'}, dimensions={0}, use_global_device_ids=true | all-gather | bytes 560320 | tf_op jit(solution)/shard_map/all_gather | solution.py:172
  210.3 0.3 slice_reduce_fusion.2
  210.6 0.1 slice.66
  210.7 0.2 multiply_add_fusion
  210.8 3.9 %fusion.16 = (bf16[256,2,512]{2,0,1:T(8,128)(2,1)S(1)}, bf16[256,2,512]{2,0,1:T(8,128)(2,1)S(1)}, bf16[256,2,512]{2,0,1:T(8,128)(2,1)S(1)}) fusion(f32[2,512]{1,0:T(2,128)S(1)} %multiply_multiply_fusion, f32[2]{0:T(128)S(1)} %get-tuple-element.14, f32[256,512]{1,0:T(8,128)S(1)} %slice.66, f32[256,512]{1,0:T(8,128)S(1)} %multiply_add_fusion, ...), kind=kLoop, calls=%fused_computation.34 | loop fusion | flops 2621440 | bytes 2625552 | tf_op jit(solution)/shard_map/neg | solution.py:134
  214.8 3.9 %multiply_convert_fusion = (bf16[256,2,512]{2,0,1:T(8,128)(2,1)S(1)}, bf16[256,2,512]{2,0,1:T(8,128)(2,1)S(1)}) fusion(f32[2,512]{1,0:T(2,128)S(1)} %multiply_multiply_fusion, f32[2]{0:T(128)S(1)} %get-tuple-element.14, f32[256,512]{1,0:T(8,128)S(1)} %slice.66, f32[256,512]{1,0:T(8,128)S(1)} %multiply_add_fusion, f32[2]{0:T(128)S(1)} %broadcast_multiply_fusion), kind=kLoop, calls=%fused_computation.15 | loop fusion | flops 1835008 | bytes 2101264 | tf_op jit(solution)/shard_map/convert_element_type | solution.py:132
  218.7 1.0 fusion
  219.7 1.1 copy_select_fusion
  220.8 27.3 %all_to_all.33 = f32[2,2,256,256]{3,1,0,2:T(2,128)S(1)} all-to-all(f32[2,2,256,256]{3,1,0,2:T(2,128)S(1)} %copy_select_fusion), channel_id=1, replica_groups=mesh['stn'=16,'chan'=2] {'stn'}, dimensions={2} | all-to-all | bytes 2097152 | tf_op jit(solution)/shard_map/all_to_all | solution.py:185
  248.1 1.2 copy.25
  (8 shorter events, 0.1 us)
Async XLA Ops:
  1.7 21.3 %all-to-all-start = ((f32[2,16,1024]{2,0,1:T(2,128)}), f32[2,16,1024]{2,0,1:T(2,128)S(1)}, u32[]{:S(2)}, u32[]{:S(2)}) async-start(f32[2,16,1024]{2,0,1:T(2,128)} %bitcast.20), calls=%async_computation | async-start | bytes 262144 | tf_op jit(solution)/shard_map/all_to_all | solution.py:154
  9.1 3.3 %copy-start = (f32[2,512,512]{2,1,0:T(8,128)S(1)}, f32[2,512,512]{2,1,0:T(8,128)}, u32[]{:S(2)}) copy-start(f32[2,512,512]{2,1,0:T(8,128)} %param.8) | copy-start | bytes 6291460
  15.9 1.8 copy-start.8
  16.0 1.8 copy-start.5
  16.0 1.8 copy-start.6
  17.9 5.0 %copy-start.4 = (f32[3,512]{1,0:T(4,128)S(1)}, f32[3,512]{1,0:T(4,128)}, u32[]{:S(2)}) copy-start(f32[3,512]{1,0:T(4,128)} %param.12) | copy-start | bytes 18436
  22.9 0.7 copy-start.1
  135.1 11.3 %copy-start.3 = (s32[1,1,16,1024]{3,2,1,0:T(8,128)S(1)}, s32[1,1,16,1024]{3,2,1,0:T(8,128)}, u32[]{:S(2)}) copy-start(s32[1,1,16,1024]{3,2,1,0:T(8,128)} %param.10) | copy-start | bytes 196612
  135.1 12.0 %copy-start.7 = (f32[3,16]{1,0:T(4,128)S(1)}, f32[3,16]{1,0:T(4,128)}, u32[]{:S(2)}) copy-start(f32[3,16]{1,0:T(4,128)} %param.11) | copy-start | bytes 580
  140.4 12.9 %all-to-all-start.1 = ((f32[16,1,1024]{2,1,0:T(1,128)}), f32[16,1,1024]{2,1,0:T(1,128)S(1)}, u32[]{:S(2)}, u32[]{:S(2)}) async-start(f32[16,1,1024]{2,1,0:T(1,128)} %bitcast.13), calls=%async_computation.1 | async-start | bytes 131072 | tf_op jit(solution)/shard_map/all_to_all | solution.py:158
  153.3 0.6 copy-start.2

commit v5 on v4

--- a/solution.py
+++ b/solution.py
@@ -85,25 +85,32 @@
     return out[:, 0]
 
 
-def _scatter_kernel(d_ref, v_ref, o_ref):
-    def body(i, carry):
-        o_ref[d_ref[i]] = v_ref[i]
-        return carry
-
-    lax.fori_loop(0, d_ref.shape[0], body, 0, unroll=16)
+def _scatter_kernel(n_ref, d_ref, v_ref, o_ref):
+    rows = n_ref.shape[0]
+    width = d_ref.shape[0] // rows
+    step = 8 if width % 8 == 0 else 1
+    for row in range(rows):
+        def body(i, carry, row=row):
+            for u in range(step):
+                slot = row * width + i * step + u
+                o_ref[d_ref[slot]] = v_ref[slot]
+            return carry
+
+        lax.fori_loop(0, (n_ref[row] + step - 1) // step, body, 0)
 
 
 def scatter_kernel(dest, vals, size):
+    live = jnp.sum((dest < size - 1).astype(jnp.int32), axis=1)
     return pl.pallas_call(
         _scatter_kernel,
         grid_spec=pltpu.PrefetchScalarGridSpec(
-            num_scalar_prefetch=2,
+            num_scalar_prefetch=3,
             grid=(1,),
             in_specs=[],
-            out_specs=pl.BlockSpec((size,), lambda i, d, v: (0,), memory_space=pltpu.SMEM),
+            out_specs=pl.BlockSpec((size,), lambda i, n, d, v: (0,), memory_space=pltpu.SMEM),
         ),
         out_shape=jax.ShapeDtypeStruct((size,), jnp.float32),
-    )(dest, vals)
+    )(live, dest.reshape(-1), vals.reshape(-1))
 
 
 def make_phasors(station_rows, iono_rows, directions, freq_ratio):
@@ -159,7 +166,7 @@
     stations_local = positions.shape[1]
     local_sources = source_flux.shape[0] // lax.axis_size("chan")
     queries = stations_local * local_sources
-    buffer = scatter_kernel(query_dest.reshape(-1), returned.reshape(-1), queries + 1)
+    buffer = scatter_kernel(query_dest.reshape(groups, capacity), returned, queries + 1)
     own_iono = buffer[:queries].reshape(stations_local, local_sources)
     station_rows = positions.T
     total_stations = stations_local * groups

time: 250 us -> 231 us (0.924)
  Pallas kernels: 143 us -> 123 us
    pallas_call x1, Pallas kernels: 31.6 us -> 12 us  [scatter_kernel(): pl.pallas_call(_scatter_kernel, grid_spec=pltpu.PrefetchScalarGridSpec(nu...]
  transfers between devices with their start and end apart: 2 -> 2, of which waited for: 1 -> 1; matrix products, arithmetic and copies ran while one was open for 6% -> 7% of each run, Pallas kernels for 0% -> 0%
where the time goes in v5:
time: 231 us; the launch traced here: 229 us
  Pallas kernels  123 us (53%)
  blocking collectives  51.2 us (22%)
  other arithmetic  22 us (10%)
  starting transfers between devices  13.4 us (6%)
  local copies, waits for them, and re-layouts  12.8 us (6%)
  waiting for transfers between devices  5.44 us (2%)
    pallas_call x1, Pallas kernels, interpolate_kernel(): pl.pallas_call(_interp_kernel, grid_spec=pltpu.PrefetchScalarGridSpec(num...  111 us
    all_to_all x1, blocking collectives, body(): lax.all_to_all(visible, 'stn', split_axis=2, concat_axis=0, tiled=True)  27.4 us
    all_gather x1, blocking collectives, body(): gathered = lax.all_gather(packed, 'stn', axis=0, tiled=True)  19.4 us
    pallas_call x1, Pallas kernels, scatter_kernel(): pl.pallas_call(_scatter_kernel, grid_spec=pltpu.PrefetchScalarGridSpec(nu...  12 us
    all_to_all x1, starting transfers between devices, body(): lax.all_to_all(coords, 'stn', split_axis=1, concat_axis=1, tiled=True)  7.39 us
    concatenate x2, other arithmetic, interpolate_kernel(): pair = jnp.concatenate([screen2d, jnp.roll(screen2d, -1, axis=0)], axis=1)  6.77 us
    all_to_all x1, starting transfers between devices, body(): lax.all_to_all(sampled, 'stn', split_axis=0, concat_axis=0, tiled=True)  6.01 us
    all_to_all x1, waiting for transfers between devices, body(): lax.all_to_all(sampled, 'stn', split_axis=0, concat_axis=0, tiled=True)  5.44 us
  transfers between devices with their start and end apart: 2, of which 1 were waited for; matrix products, arithmetic and copies ran while one was open for 7% of the time, Pallas kernels for 0%

profile of v5, /device:TPU:0, one launch (start us, length us, event | category | flops | bytes accessed | tf_op | source)
XLA Modules:
  0.0 229.4 jit_solution(15794195771552927394)
XLA Ops:
  0.0 1.7 copy.40
  1.7 7.4 %all-to-all-start = ((f32[2,16,1024]{2,0,1:T(2,128)}), f32[2,16,1024]{2,0,1:T(2,128)S(1)}, u32[]{:S(2)}, u32[]{:S(2)}) async-start(f32[2,16,1024]{2,0,1:T(2,128)} %bitcast.20), calls=%async_computation | async-start | bytes 262144 | tf_op jit(solution)/shard_map/all_to_all | solution.py:161
  9.1 0.0 copy-start
  9.1 3.3 %slice.60 = f32[1023,512]{1,0:T(8,128)} slice(f32[1024,512]{1,0:T(8,128)} %bitcast.21), slice={[1:1024], [0:512]} | slice | bytes 4190208 | tf_op jit(solution)/shard_map/jit(_roll_static)/slice | solution.py:73
  12.4 0.0 copy-done
  12.4 1.7 concatenate.28
  14.1 1.8 pad_maximum_fusion.1
  15.9 0.0 copy-start.8
  15.9 0.0 copy-start.5
  15.9 0.0 copy-start.6
  16.0 1.7 concatenate.30
  17.7 0.0 copy-done.8
  17.7 0.1 fusion.17
  17.8 0.0 copy-done.5
  17.8 0.0 copy-done.6
  17.8 0.1 multiply_multiply_fusion
  17.9 0.0 copy-start.4
  17.9 5.0 %pad_maximum_fusion.s_ref = f32[1024,8,128]{2,1,0:T(8,128)} fusion(f32[1024,4,128]{2,1,0:T(4,128)} %concatenate.30, f32[1024,4,128]{2,1,0:T(4,128)} %concatenate.28), kind=kLoop, calls=%fused_computation | loop fusion | flops 1048576 | bytes 8388608 | tf_op jit(solution)/shard_map/concatenate | solution.py:73
  22.9 0.0 copy-done.4
  22.9 0.0 all-to-all-done
  22.9 0.0 copy-start.1
  23.0 0.6 copy.28
  23.6 0.0 copy-done.1
  23.6 111.4 %shard_map.82 = f32[16384,1]{1,0:T(8,128)} custom-call(s32[16384]{0:T(1024)} %bitcast.26, f32[2,16384]{1,0:T(2,128)} %bitcast.25, f32[1024,8,128]{2,1,0:T(8,128)} %pad_maximum_fusion.s_ref), custom_call_target="tpu_custom_call" | custom-call | tf_op jit(solution)/shard_map/pallas_call | solution.py:75
  135.1 0.0 copy-start.3
  135.1 0.0 copy-start.7
  135.1 5.3 %reduce.1 = f32[16384]{0:T(1024)} reduce(f32[16384,1]{1,0:T(8,128)} %shard_map.82, f32[]{:T(128)} %constant.29), dimensions={1}, to_apply=%pallas_call.6.reduce_sub_computation | reduce | bytes 131076 | tf_op jit(solution)/shard_map/pallas_call | solution.py:75
  140.3 6.0 %all-to-all-start.1 = ((f32[16,1,1024]{2,1,0:T(1,128)}), f32[16,1,1024]{2,1,0:T(1,128)S(1)}, u32[]{:S(2)}, u32[]{:S(2)}) async-start(f32[16,1,1024]{2,1,0:T(1,128)} %bitcast.13), calls=%async_computation.1 | async-start | bytes 131072 | tf_op jit(solution)/shard_map/all_to_all | solution.py:165
  146.4 0.0 copy-done.3
  146.4 0.6 copy.27
  147.0 0.0 copy-done.7
  147.0 0.1 copy.23
  147.1 0.7 convert_reduce_fusion.n_ref
  147.8 5.4 %all-to-all-done.1 = f32[16,1,1024]{2,1,0:T(1,128)S(1)} async-done(((f32[16,1,1024]{2,1,0:T(1,128)}), f32[16,1,1024]{2,1,0:T(1,128)S(1)}, u32[]{:S(2)}, u32[]{:S(2)}) %all-to-all-start.1) | async-done | bytes 65568 | tf_op jit(solution)/shard_map/all_to_all | solution.py:165
  153.2 0.6 copy-done.2
  153.9 12.0 %shard_map.83 = f32[4097]{0:T(1024)} custom-call(s32[16]{0:T(128)} %convert_reduce_fusion.n_ref, s32[16384]{0:T(1024)} %bitcast.28, f32[16384]{0:T(1024)} %bitcast.27), custom_call_target="tpu_custom_call" | custom-call | tf_op jit(solution)/shard_map/pallas_call | solution.py:104
  165.9 0.7 slice.62
  166.6 4.4 %all_gather.6 = f32[16,512]{1,0:T(8,128)S(1)} all-gather(f32[16,256]{1,0:T(8,128)S(1)} %reshape.176), channel_id=1, replica_groups=mesh['stn'=16,'chan'=2] {'chan'}, dimensions={1}, use_global_device_ids=true | all-gather | bytes 49152 | tf_op jit(solution)/shard_map/all_gather | solution.py:177
  171.0 19.4 %all_gather.7 = f32[256,515]{1,0:T(8,128)S(1)} all-gather(f32[16,515]{1,0:T(8,128)S(1)} %pad_maximum_fusion.2), channel_id=1, replica_groups=mesh['stn'=16,'chan'=2] {'stn'}, dimensions={0}, use_global_device_ids=true | all-gather | bytes 560320 | tf_op jit(solution)/shard_map/all_gather | solution.py:179
  190.4 0.3 slice_reduce_fusion.2
  190.7 0.1 slice.66
  190.7 0.2 multiply_add_fusion
  190.9 3.9 %fusion.16 = (bf16[256,2,512]{2,0,1:T(8,128)(2,1)S(1)}, bf16[256,2,512]{2,0,1:T(8,128)(2,1)S(1)}, bf16[256,2,512]{2,0,1:T(8,128)(2,1)S(1)}) fusion(f32[2,512]{1,0:T(2,128)S(1)} %multiply_multiply_fusion, f32[2]{0:T(128)S(1)} %get-tuple-element.14, f32[256,512]{1,0:T(8,128)S(1)} %slice.66, f32[256,512]{1,0:T(8,128)S(1)} %multiply_add_fusion, ...), kind=kLoop, calls=%fused_computation.35 | loop fusion | flops 2621440 | bytes 2625552 | tf_op jit(solution)/shard_map/neg | solution.py:141
  194.9 3.9 %multiply_convert_fusion = (bf16[256,2,512]{2,0,1:T(8,128)(2,1)S(1)}, bf16[256,2,512]{2,0,1:T(8,128)(2,1)S(1)}) fusion(f32[2,512]{1,0:T(2,128)S(1)} %multiply_multiply_fusion, f32[2]{0:T(128)S(1)} %get-tuple-element.14, f32[256,512]{1,0:T(8,128)S(1)} %slice.66, f32[256,512]{1,0:T(8,128)S(1)} %multiply_add_fusion, f32[2]{0:T(128)S(1)} %broadcast_multiply_fusion), kind=kLoop, calls=%fused_computation.15 | loop fusion | flops 1835008 | bytes 2101264 | tf_op jit(solution)/shard_map/convert_element_type | solution.py:139
  198.8 1.0 fusion
  199.8 1.1 copy_select_fusion
  200.9 27.4 %all_to_all.33 = f32[2,2,256,256]{3,1,0,2:T(2,128)S(1)} all-to-all(f32[2,2,256,256]{3,1,0,2:T(2,128)S(1)} %copy_select_fusion), channel_id=1, replica_groups=mesh['stn'=16,'chan'=2] {'stn'}, dimensions={2} | all-to-all | bytes 2097152 | tf_op jit(solution)/shard_map/all_to_all | solution.py:192
  228.3 1.2 copy.25
  (9 shorter events, 0.1 us)
Async XLA Ops:
  1.7 21.2 %all-to-all-start = ((f32[2,16,1024]{2,0,1:T(2,128)}), f32[2,16,1024]{2,0,1:T(2,128)S(1)}, u32[]{:S(2)}, u32[]{:S(2)}) async-start(f32[2,16,1024]{2,0,1:T(2,128)} %bitcast.20), calls=%async_computation | async-start | bytes 262144 | tf_op jit(solution)/shard_map/all_to_all | solution.py:161
  9.1 3.3 %copy-start = (f32[2,512,512]{2,1,0:T(8,128)S(1)}, f32[2,512,512]{2,1,0:T(8,128)}, u32[]{:S(2)}) copy-start(f32[2,512,512]{2,1,0:T(8,128)} %param.8) | copy-start | bytes 6291460
  15.9 1.8 copy-start.8
  15.9 1.9 copy-start.5
  15.9 1.8 copy-start.6
  17.9 5.0 %copy-start.4 = (f32[3,512]{1,0:T(4,128)S(1)}, f32[3,512]{1,0:T(4,128)}, u32[]{:S(2)}) copy-start(f32[3,512]{1,0:T(4,128)} %param.12) | copy-start | bytes 18436
  22.9 0.7 copy-start.1
  135.1 11.3 %copy-start.3 = (s32[1,1,16,1024]{3,2,1,0:T(8,128)S(1)}, s32[1,1,16,1024]{3,2,1,0:T(8,128)}, u32[]{:S(2)}) copy-start(s32[1,1,16,1024]{3,2,1,0:T(8,128)} %param.10) | copy-start | bytes 196612
  135.1 12.0 %copy-start.7 = (f32[3,16]{1,0:T(4,128)S(1)}, f32[3,16]{1,0:T(4,128)}, u32[]{:S(2)}) copy-start(f32[3,16]{1,0:T(4,128)} %param.11) | copy-start | bytes 580
  140.3 12.9 %all-to-all-start.1 = ((f32[16,1,1024]{2,1,0:T(1,128)}), f32[16,1,1024]{2,1,0:T(1,128)S(1)}, u32[]{:S(2)}, u32[]{:S(2)}) async-start(f32[16,1,1024]{2,1,0:T(1,128)} %bitcast.13), calls=%async_computation.1 | async-start | bytes 131072 | tf_op jit(solution)/shard_map/all_to_all | solution.py:165
  153.2 0.6 copy-start.2

commit v6 on v5

--- a/solution.py
+++ b/solution.py
@@ -85,6 +85,73 @@
     return out[:, 0]
 
 
+def _balanced_kernel(n_ref, r_ref, c_ref, s_ref, o_ref):
+    rows = s_ref.shape[1]
+    two_nb = s_ref.shape[2]
+    nb = two_nb // 2
+    cols = nb * 128
+    senders = n_ref.shape[0] // 2
+    seg = o_ref.shape[0] // senders
+    unroll = min(UNROLL, seg)
+    h = pl.program_id(0)
+    sub = lax.broadcasted_iota(jnp.int32, (two_nb, 128), 0)
+    lane = lax.broadcasted_iota(jnp.int32, (two_nb, 128), 1)
+    col = ((sub % nb) * 128 + lane).astype(jnp.float32)
+    upper = sub >= nb
+    rowid = lax.broadcasted_iota(jnp.int32, (8, 128), 0)
+
+    def segment(s, carry):
+        def group(g, carry2):
+            for part in range(unroll // 8):
+                acc = jnp.zeros((8, 128), jnp.float32)
+                first = s * seg + g * unroll + part * 8
+                for u in range(8):
+                    j = h * senders * seg + first + u
+                    t = s_ref[0, r_ref[j]]
+                    y = jnp.full((two_nb, 128), c_ref[0, j], jnp.float32) * (rows - 1)
+                    x = jnp.full((two_nb, 128), c_ref[1, j], jnp.float32) * (cols - 1)
+                    ry = jnp.clip(jnp.floor(y), 0.0, rows - 2.0)
+                    kx = jnp.clip(jnp.floor(x), 0.0, cols - 2.0)
+                    fy = y - ry
+                    fx = x - kx
+                    wy = jnp.where(upper, fy, 1.0 - fy)
+                    wx = jnp.where(col == kx, 1.0 - fx, jnp.where(col == kx + 1.0, fx, 0.0))
+                    row = jnp.sum(t * (wy * wx), axis=0, keepdims=True)
+                    acc = jnp.where(rowid == u, row, acc)
+                o_ref[pl.ds(pl.multiple_of(first, 8), 8), :] = jnp.sum(acc, axis=1, keepdims=True)
+            return carry2
+
+        trips = (n_ref[h * senders + s] + unroll - 1) // unroll
+        lax.fori_loop(0, trips, group, 0)
+        return carry
+
+    lax.fori_loop(0, senders, segment, 0)
+
+
+def pair_table(screen2d):
+    rows, cols = screen2d.shape
+    pair = jnp.concatenate([screen2d, jnp.roll(screen2d, -1, axis=0)], axis=1)
+    return pair.reshape(rows, 2 * (cols // 128), 128)
+
+
+def interpolate_balanced(tables, coords, live):
+    _, rows, two_nb, _ = tables.shape
+    _, halves, senders, seg = coords.shape
+    flat = coords.reshape(2, halves * senders * seg)
+    r = jnp.clip(jnp.floor(flat[0] * (rows - 1)), 0.0, rows - 2.0).astype(jnp.int32)
+    out = pl.pallas_call(
+        _balanced_kernel,
+        grid_spec=pltpu.PrefetchScalarGridSpec(
+            num_scalar_prefetch=3,
+            grid=(halves,),
+            in_specs=[pl.BlockSpec((1, rows, two_nb, 128), lambda i, n, rr, cc: (i, 0, 0, 0))],
+            out_specs=pl.BlockSpec((senders * seg, 1), lambda i, n, rr, cc: (i, 0)),
+        ),
+        out_shape=jax.ShapeDtypeStruct((halves * senders * seg, 1), jnp.float32),
+    )(live, r, flat, tables)
+    return out.reshape(halves, senders, seg)
+
+
 def _scatter_kernel(n_ref, d_ref, v_ref, o_ref):
     rows = n_ref.shape[0]
     width = d_ref.shape[0] // rows
@@ -157,15 +224,24 @@
     strip_rows = screen.shape[0] * screen.shape[1]
     values = screen.reshape(-1)
     capacity = query_dest.shape[3]
-    coords = pierce_coords.reshape(2, groups, capacity)
-    received = lax.all_to_all(coords, "stn", split_axis=1, concat_axis=1, tiled=True)
-    sampled = interpolate_kernel(
-        values.reshape(strip_rows, tile_cols), received.reshape(2, groups * capacity)
-    ).reshape(groups, capacity)
-    returned = lax.all_to_all(sampled, "stn", split_axis=0, concat_axis=0, tiled=True)
     stations_local = positions.shape[1]
     local_sources = source_flux.shape[0] // lax.axis_size("chan")
     queries = stations_local * local_sources
+    half = capacity // 2
+    coords = pierce_coords.reshape(2, groups, capacity)
+    dead = query_dest.reshape(groups, capacity) >= queries
+    coords = jnp.where(dead[None], -1.0, coords).reshape(2, groups, half, 2)
+    swap = lambda a: a.reshape(a.shape[0], groups // 2, 2, half)[:, :, ::-1, :].reshape(a.shape[0], groups, half)
+    send = jnp.stack([coords[..., 0], swap(coords[..., 1])], axis=2)
+    received = lax.all_to_all(send, "stn", split_axis=1, concat_axis=1, tiled=True)
+    kin = received.transpose(0, 2, 1, 3)
+    live = jnp.sum((kin[0] >= 0.0).astype(jnp.int32), axis=2).reshape(-1)
+    screen2d = values.reshape(strip_rows, tile_cols)
+    partner = lax.ppermute(screen2d, "stn", [(i, i ^ 1) for i in range(groups)])
+    tables = jnp.stack([pair_table(screen2d), pair_table(partner)])
+    sampled = interpolate_balanced(tables, kin, live).transpose(1, 0, 2)
+    back = lax.all_to_all(sampled, "stn", split_axis=0, concat_axis=0, tiled=True)
+    returned = jnp.stack([back[:, 0, :], swap(back[None, :, 1, :])[0]], axis=-1).reshape(groups, capacity)
     buffer = scatter_kernel(query_dest.reshape(groups, capacity), returned, queries + 1)
     own_iono = buffer[:queries].reshape(stations_local, local_sources)
     station_rows = positions.T

time: 231 us -> 209 us (0.905)
  Pallas kernels: 123 us -> 85.4 us
  local copies, waits for them, and re-layouts: 12.8 us -> 27.8 us
  other arithmetic: 22 us -> 25.3 us
  starting transfers between devices: 13.4 us -> 11 us
    pallas_call x1, Pallas kernels: 111 us -> 73.4 us  [interpolate_balanced(): pl.pallas_call(_balanced_kernel, grid_spec=pltpu.PrefetchScalarGridSpec(n...]
    another operation x0 -> x5, local copies, waits for them, and re-layouts: none -> 9.18 us  [the longest x1 4.52 us: scatter_kernel(): vals.reshape(-1)]
    concatenate x2 -> x0, other arithmetic: 6.77 us -> none  [interpolate_kernel(): pair = jnp.concatenate([screen2d, jnp.roll(screen2d, -1, axis=0)], axis=1)]
    another operation x0 -> x3, other arithmetic: none -> 5.1 us  [the longest x1 3.76 us: body(): tables = jnp.stack([pair_table(screen2d), pair_table(partner)])]
    unnamed x22 -> x23, local copies, waits for them, and re-layouts: 3.68 us -> 8.51 us
    unnamed x1 -> x2, other arithmetic: 0.02 us -> 4.05 us
    concatenate x2 -> x0, local copies, waits for them, and re-layouts: 3.48 us -> none  [interpolate_kernel(): pair = jnp.concatenate([screen2d, jnp.roll(screen2d, -1, axis=0)], axis=1)]
    slice x3 -> x6, local copies, waits for them, and re-layouts: 3.36 us -> 6.02 us  [the longest x4 4.15 us: pair_table(): pair = jnp.concatenate([screen2d, jnp.roll(screen2d, -1, axis=0)], axis=1)]
  transfers between devices with their start and end apart: 2 -> 3, of which waited for: 1 -> 2; matrix products, arithmetic and copies ran while one was open for 7% -> 9% of each run, Pallas kernels for 0% -> 0%
where the time goes in v6:
time: 209 us
  Pallas kernels  85.4 us (41%)
  blocking collectives  51.4 us (25%)
  local copies, waits for them, and re-layouts  27.8 us (13%)
  other arithmetic  25.3 us (12%)
  starting transfers between devices  11 us (5%)
  waiting for transfers between devices  6.57 us (3%)
    pallas_call x1, Pallas kernels, interpolate_balanced(): pl.pallas_call(_balanced_kernel, grid_spec=pltpu.PrefetchScalarGridSpec(n...  73.4 us
    all_to_all x1, blocking collectives, body(): lax.all_to_all(visible, 'stn', split_axis=2, concat_axis=0, tiled=True)  27.3 us
    all_gather x1, blocking collectives, body(): gathered = lax.all_gather(packed, 'stn', axis=0, tiled=True)  19.7 us
    pallas_call x1, Pallas kernels, scatter_kernel(): pl.pallas_call(_scatter_kernel, grid_spec=pltpu.PrefetchScalarGridSpec(nu...  12 us
    unnamed x23, local copies, waits for them, and re-layouts  8.51 us
    all_to_all x1, starting transfers between devices, body(): lax.all_to_all(send, 'stn', split_axis=1, concat_axis=1, tiled=True)  7.01 us
    all_to_all x1, waiting for transfers between devices, body(): lax.all_to_all(sampled, 'stn', split_axis=0, concat_axis=0, tiled=True)  5.45 us
    pallas_call x1, other arithmetic, interpolate_balanced(): pl.pallas_call(_balanced_kernel, grid_spec=pltpu.PrefetchScalarGridSpec(n...  4.65 us
  transfers between devices with their start and end apart: 3, of which 2 were waited for; matrix products, arithmetic and copies ran while one was open for 9% of the time, Pallas kernels for 0%

profile of v6, /device:TPU:0, one launch (start us, length us, event | category | flops | bytes accessed | tf_op | source)
XLA Modules:
  0.0 208.8 jit_solution(11022577059432560713)
XLA Ops:
  0.0 0.5 collective-permute-start
  0.5 0.8 broadcast_compare_fusion
  1.3 1.2 copy.69
  2.6 0.3 copy.68
  2.9 0.2 ge.18
  3.1 0.7 broadcast_select_fusion
  3.8 1.6 fusion.14
  5.4 0.3 copy.70
  5.7 1.0 copy.71
  6.7 1.3 pad_maximum_fusion.1
  8.0 1.0 copy.72
  9.0 7.0 %all-to-all-start = ((f32[2,16,2,512]{3,2,0,1:T(2,128)}), f32[2,16,2,512]{3,2,0,1:T(2,128)S(1)}, u32[]{:S(2)}, u32[]{:S(2)}) async-start(f32[2,16,2,512]{3,2,0,1:T(2,128)} %copy.72), calls=%async_computation | async-start | bytes 262144 | tf_op jit(solution)/shard_map/all_to_all | solution.py:236
  16.0 1.6 slice.87
  17.8 2.0 maximum_bitcast_fusion
  19.8 2.9 %copy.85 = f32[128,8,8,128]{3,2,1,0:T(8,128)} copy(f32[128,8,8,128]{3,1,2,0:T(8,128)S(1)} %maximum_bitcast_fusion) | data formatting | bytes 8388608
  22.8 1.1 all-to-all-done
  24.0 0.6 copy.83
  24.6 0.1 convert_reduce_fusion
  24.7 0.6 reshape.184.n_ref
  25.3 0.8 copy.84
  26.1 1.8 slice.89
  27.9 0.7 slice.90
  28.6 2.0 maximum_bitcast_fusion.1
  30.7 1.0 copy.86
  31.7 1.1 copy-done
  32.8 3.8 %pad_maximum_fusion.s_ref = f32[2,1024,8,128]{3,2,1,0:T(8,128)} fusion(f32[1,1024,8,128]{3,2,1,0:T(8,128)S(1)} %bitcast.41, f32[1,1024,8,128]{3,2,1,0:T(8,128)S(1)} %bitcast.40), kind=kLoop, calls=%fused_computation | loop fusion | flops 2097152 | bytes 16777216 | tf_op jit(solution)/shard_map/stack | solution.py:241
  36.6 73.4 %shard_map.82 = f32[16384,1]{1,0:T(8,128)} custom-call(s32[32]{0:T(128)} %reshape.184.n_ref, s32[16384]{0:T(1024)} %bitcast.55, f32[2,16384]{1,0:T(2,128)} %bitcast.54, f32[2,1024,8,128]{3,2,1,0:T(8,128)} %pad_maximum_fusion.s_ref), custom_call_target="tpu_custom_call" | custom-call | tf_op jit(solution)/shard_map/pallas_call | solution.py:142
  110.0 4.6 %reduce.2 = f32[16384]{0:T(1024)S(1)} reduce(f32[16384,1]{1,0:T(8,128)} %shard_map.82, f32[]{:T(128)} %constant.32), dimensions={1}, to_apply=%pallas_call.6.reduce_sub_computation | reduce | bytes 131076 | tf_op jit(solution)/shard_map/pallas_call | solution.py:142
  114.7 0.7 copy.76
  115.4 3.5 %all-to-all-start.1 = ((f32[16,2,512]{2,1,0:T(2,128)}), f32[16,2,512]{2,1,0:T(2,128)S(1)}, u32[]{:S(2)}, u32[]{:S(2)}) async-start(f32[16,2,512]{2,1,0:T(2,128)} %copy.76), calls=%async_computation.1 | async-start | bytes 131072 | tf_op jit(solution)/shard_map/all_to_all | solution.py:243
  118.9 0.6 copy.82
  119.5 0.1 copy.78
  119.6 0.6 convert_reduce_fusion.1.n_ref
  120.3 5.4 %all-to-all-done.1 = f32[16,2,512]{2,1,0:T(2,128)S(1)} async-done(((f32[16,2,512]{2,1,0:T(2,128)}), f32[16,2,512]{2,1,0:T(2,128)S(1)}, u32[]{:S(2)}, u32[]{:S(2)}) %all-to-all-start.1) | async-done | bytes 65568 | tf_op jit(solution)/shard_map/all_to_all | solution.py:243
  125.9 2.6 %copy.77 = f32[16,512,2]{2,1,0:T(8,128)} copy(f32[16,512,2]{1,2,0:T(2,128)S(1)} %pad_maximum_fusion.2) | data formatting | bytes 131072 | tf_op jit(solution)/shard_map/stack | solution.py:244
  128.5 4.5 %reshape_reshape.11.v_ref = f32[16384]{0:T(1024)} reshape(f32[16,512,2]{2,1,0:T(8,128)} %copy.77) | data formatting | bytes 131072 | tf_op jit(solution)/shard_map/reshape;reshape | solution.py:180
  133.0 12.0 %shard_map.83 = f32[4097]{0:T(1024)} custom-call(s32[16]{0:T(128)} %convert_reduce_fusion.1.n_ref, s32[16384]{0:T(1024)} %bitcast.58, f32[16384]{0:T(1024)} %reshape_reshape.11.v_ref), custom_call_target="tpu_custom_call" | custom-call | tf_op jit(solution)/shard_map/pallas_call | solution.py:171
  145.0 0.7 slice.93
  145.7 4.4 %all_gather.6 = f32[16,512]{1,0:T(8,128)S(1)} all-gather(f32[16,256]{1,0:T(8,128)S(1)} %reshape.187), channel_id=1, replica_groups=mesh['stn'=16,'chan'=2] {'chan'}, dimensions={1}, use_global_device_ids=true | all-gather | bytes 49152 | tf_op jit(solution)/shard_map/all_gather | solution.py:253
  150.1 19.7 %all_gather.7 = f32[256,515]{1,0:T(8,128)S(1)} all-gather(f32[16,515]{1,0:T(8,128)S(1)} %pad_maximum_fusion.3), channel_id=1, replica_groups=mesh['stn'=16,'chan'=2] {'stn'}, dimensions={0}, use_global_device_ids=true | all-gather | bytes 560320 | tf_op jit(solution)/shard_map/all_gather | solution.py:255
  169.8 0.3 slice_reduce_fusion.2
  170.2 0.2 multiply_add_fusion
  170.4 3.9 %multiply_convert_fusion = (bf16[256,2,512]{2,0,1:T(8,128)(2,1)S(1)}, bf16[256,2,512]{2,0,1:T(8,128)(2,1)S(1)}) fusion(f32[2,512]{1,0:T(2,128)S(1)} %multiply_multiply_fusion, f32[2]{0:T(128)S(1)} %get-tuple-element.14, f32[256,512]{1,0:T(8,128)S(1)} %slice.97, f32[256,512]{1,0:T(8,128)S(1)} %multiply_add_fusion, f32[2]{0:T(128)S(1)} %broadcast_multiply_fusion), kind=kLoop, calls=%fused_computation.17 | loop fusion | flops 1835008 | bytes 2101264 | tf_op jit(solution)/shard_map/convert_element_type | solution.py:206
  174.3 3.9 %fusion.12 = (bf16[256,2,512]{2,0,1:T(8,128)(2,1)S(1)}, bf16[256,2,512]{2,0,1:T(8,128)(2,1)S(1)}, bf16[256,2,512]{2,0,1:T(8,128)(2,1)S(1)}) fusion(f32[2,512]{1,0:T(2,128)S(1)} %multiply_multiply_fusion, f32[2]{0:T(128)S(1)} %get-tuple-element.14, f32[256,512]{1,0:T(8,128)S(1)} %slice.97, f32[256,512]{1,0:T(8,128)S(1)} %multiply_add_fusion, ...), kind=kLoop, calls=%fused_computation.38 | loop fusion | flops 2621440 | bytes 2625552 | tf_op jit(solution)/shard_map/neg | solution.py:208
  178.2 1.0 fusion
  179.2 1.1 copy_select_fusion
  180.3 27.3 %all_to_all.28 = f32[2,2,256,256]{3,1,0,2:T(2,128)S(1)} all-to-all(f32[2,2,256,256]{3,1,0,2:T(2,128)S(1)} %copy_select_fusion), channel_id=1, replica_groups=mesh['stn'=16,'chan'=2] {'stn'}, dimensions={2} | all-to-all | bytes 2097152 | tf_op jit(solution)/shard_map/all_to_all | solution.py:268
  207.6 1.2 copy.80
  (32 shorter events, 0.5 us)
Async XLA Ops:
  0.0 26.1 %collective-permute-start = (f32[1024,512]{1,0:T(8,128)}, f32[1024,512]{1,0:T(8,128)}, u32[]{:S(2)}, u32[]{:S(2)}) collective-permute-start(f32[1024,512]{1,0:T(8,128)} %bitcast.42), channel_id=1, source_target_pairs={{0,2},{2,0},{4,6},{6,4},{8,10},{10,8},{12,14},{14,12},{16,18},{18,... | collective-permute-start | bytes 6291464 | tf_op jit(solution)/shard_map/ppermute | solution.py:240
  3.1 12.9 %copy-start.1 = (f32[2,512,512]{2,1,0:T(8,128)S(1)}, f32[2,512,512]{2,1,0:T(8,128)}, u32[]{:S(2)}) copy-start(f32[2,512,512]{2,1,0:T(8,128)} %param.8) | copy-start | bytes 6291460
  5.7 11.9 %copy-start.7 = (f32[32]{0:T(128)S(1)}, f32[32]{0:T(128)}, u32[]{:S(2)}) copy-start(f32[32]{0:T(128)} %param.13) | copy-start | bytes 388
  5.7 12.0 %copy-start.4 = (f32[512]{0:T(512)S(1)}, f32[512]{0:T(512)}, u32[]{:S(2)}) copy-start(f32[512]{0:T(512)} %param.15) | copy-start | bytes 6148
  5.7 12.0 %copy-start.5 = (f32[512]{0:T(512)S(1)}, f32[512]{0:T(512)}, u32[]{:S(2)}) copy-start(f32[512]{0:T(512)} %param.14) | copy-start | bytes 6148
  9.0 14.9 %all-to-all-start = ((f32[2,16,2,512]{3,2,0,1:T(2,128)}), f32[2,16,2,512]{3,2,0,1:T(2,128)S(1)}, u32[]{:S(2)}, u32[]{:S(2)}) async-start(f32[2,16,2,512]{3,2,0,1:T(2,128)} %copy.72), calls=%async_computation | async-start | bytes 262144 | tf_op jit(solution)/shard_map/all_to_all | solution.py:236
  19.8 3.0 %copy-start.3 = (f32[3,512]{1,0:T(4,128)S(1)}, f32[3,512]{1,0:T(4,128)}, u32[]{:S(2)}) copy-start(f32[3,512]{1,0:T(4,128)} %param.12) | copy-start | bytes 18436
  30.7 2.2 %copy-start = (f32[128,8,8,128]{3,2,1,0:T(8,128)S(1)}, f32[128,8,8,128]{3,2,1,0:T(8,128)}, u32[]{:S(2)}) copy-start(f32[128,8,8,128]{3,2,1,0:T(8,128)} %copy.85) | copy-start | bytes 12582916
  110.0 8.9 %copy-start.2 = (s32[1,1,16,1024]{3,2,1,0:T(8,128)S(1)}, s32[1,1,16,1024]{3,2,1,0:T(8,128)}, u32[]{:S(2)}) copy-start(s32[1,1,16,1024]{3,2,1,0:T(8,128)} %param.10) | copy-start | bytes 196612
  110.0 9.5 %copy-start.6 = (f32[3,16]{1,0:T(4,128)S(1)}, f32[3,16]{1,0:T(4,128)}, u32[]{:S(2)}) copy-start(f32[3,16]{1,0:T(4,128)} %param.11) | copy-start | bytes 580
  115.4 10.4 %all-to-all-start.1 = ((f32[16,2,512]{2,1,0:T(2,128)}), f32[16,2,512]{2,1,0:T(2,128)S(1)}, u32[]{:S(2)}, u32[]{:S(2)}) async-start(f32[16,2,512]{2,1,0:T(2,128)} %copy.76), calls=%async_computation.1 | async-start | bytes 131072 | tf_op jit(solution)/shard_map/all_to_all | solution.py:243

commit v7 on v6

--- a/solution.py
+++ b/solution.py
@@ -265,7 +265,8 @@
     ids = jnp.arange(total_stations, dtype=jnp.int32)
     cross_only = ids[:, None] != ids[None, :]
     visible = jnp.where(cross_only[None, None], visible, jnp.zeros_like(visible))
-    return lax.all_to_all(visible, "stn", split_axis=2, concat_axis=0, tiled=True)
+    moved = lax.all_to_all(visible.astype(jnp.bfloat16), "stn", split_axis=2, concat_axis=0, tiled=True)
+    return moved.astype(jnp.float32)
 
 
 def _rows_path(own_iono, station_rows, directions, freq_ratio, source_flux, spectral_index):

time: 209 us -> 199 us (0.952); the launches traced: 209 us -> 196 us
  Pallas kernels: 85.4 us -> 41.6 us
  starting transfers between devices: 11 us -> 52.6 us
  blocking collectives: 51.4 us -> 41.2 us
    pallas_call x1, Pallas kernels: 73.4 us -> 29.7 us  [interpolate_balanced(): pl.pallas_call(_balanced_kernel, grid_spec=pltpu.PrefetchScalarGridSpec(n...]
    all_to_all x1, starting transfers between devices: 3.49 us -> 45.1 us  [body(): lax.all_to_all(sampled, 'stn', split_axis=0, concat_axis=0, tiled=True)]
    all_to_all x1, blocking collectives: 27.3 us -> 16.9 us  [body(): lax.all_to_all(visible.astype(jnp.bfloat16), 'stn', split_axis=2, concat_...]
  transfers between devices with their start and end apart: 3 -> 3, of which waited for: 2 -> 2; matrix products, arithmetic and copies ran while one was open for 9% -> 10% of each run, Pallas kernels for 0% -> 0%
where the time goes in v7:
time: 199 us; the launch traced here: 196 us
  starting transfers between devices  52.6 us (26%)
  Pallas kernels  41.6 us (21%)
  blocking collectives  41.2 us (21%)
  local copies, waits for them, and re-layouts  27.8 us (14%)
  other arithmetic  25.5 us (13%)
  waiting for transfers between devices  6.61 us (3%)
    all_to_all x1, starting transfers between devices, body(): lax.all_to_all(sampled, 'stn', split_axis=0, concat_axis=0, tiled=True)  45.1 us
    pallas_call x1, Pallas kernels, interpolate_balanced(): pl.pallas_call(_balanced_kernel, grid_spec=pltpu.PrefetchScalarGridSpec(n...  29.7 us
    all_gather x1, blocking collectives, body(): gathered = lax.all_gather(packed, 'stn', axis=0, tiled=True)  19.9 us
    all_to_all x1, blocking collectives, body(): lax.all_to_all(visible.astype(jnp.bfloat16), 'stn', split_axis=2, concat_...  16.9 us
    pallas_call x1, Pallas kernels, scatter_kernel(): pl.pallas_call(_scatter_kernel, grid_spec=pltpu.PrefetchScalarGridSpec(nu...  11.9 us
    unnamed x23, local copies, waits for them, and re-layouts  8.51 us
    all_to_all x1, starting transfers between devices, body(): lax.all_to_all(send, 'stn', split_axis=1, concat_axis=1, tiled=True)  7.01 us
    all_to_all x1, waiting for transfers between devices, body(): lax.all_to_all(sampled, 'stn', split_axis=0, concat_axis=0, tiled=True)  5.48 us
  transfers between devices with their start and end apart: 3, of which 2 were waited for; matrix products, arithmetic and copies ran while one was open for 10% of the time, Pallas kernels for 0%

profile of v7, /device:TPU:0, one launch (start us, length us, event | category | flops | bytes accessed | tf_op | source)
XLA Modules:
  0.0 196.3 jit_solution(10432850374654596588)
XLA Ops:
  0.0 0.5 collective-permute-start
  0.5 0.8 broadcast_compare_fusion
  1.3 1.2 copy.69
  2.6 0.3 copy.68
  2.9 0.2 ge.18
  3.1 0.7 broadcast_select_fusion
  3.8 1.6 fusion.15
  5.4 0.3 copy.70
  5.7 1.0 copy.71
  6.7 1.3 pad_maximum_fusion.1
  8.0 1.0 copy.72
  9.0 7.0 %all-to-all-start = ((f32[2,16,2,512]{3,2,0,1:T(2,128)}), f32[2,16,2,512]{3,2,0,1:T(2,128)S(1)}, u32[]{:S(2)}, u32[]{:S(2)}) async-start(f32[2,16,2,512]{3,2,0,1:T(2,128)} %copy.72), calls=%async_computation | async-start | bytes 262144 | tf_op jit(solution)/shard_map/all_to_all | solution.py:236
  16.0 1.6 slice.87
  17.8 2.0 %maximum_bitcast_fusion = f32[128,8,8,128]{3,1,2,0:T(8,128)S(1)} fusion(f32[1,512]{1,0:T(1,128)S(1)} %slice.88, f32[1023,512]{1,0:T(8,128)} %slice.87, f32[1024,512]{1,0:T(8,128)S(1)} %bitcast.46), kind=kLoop, calls=%fused_computation.1 | loop fusion | flops 2097152 | bytes 8388608
  19.8 2.9 %copy.85 = f32[128,8,8,128]{3,2,1,0:T(8,128)} copy(f32[128,8,8,128]{3,1,2,0:T(8,128)S(1)} %maximum_bitcast_fusion) | data formatting | bytes 8388608
  22.8 1.1 all-to-all-done
  24.0 0.6 copy.83
  24.6 0.1 convert_reduce_fusion
  24.7 0.6 reshape.188.n_ref
  25.3 0.8 copy.84
  26.1 1.8 slice.89
  27.9 0.7 slice.90
  28.6 2.0 %maximum_bitcast_fusion.1 = f32[128,8,8,128]{3,1,2,0:T(8,128)S(1)} fusion(f32[1,512]{1,0:T(1,128)S(1)} %slice.90, f32[1023,512]{1,0:T(8,128)S(1)} %slice.89, f32[1024,512]{1,0:T(8,128)} %collective-permute-done), kind=kLoop, calls=%fused_computation.2 | loop fusion | flops 2097152 | bytes 8388608
  30.7 1.0 copy.86
  31.7 1.1 copy-done
  32.8 3.8 %pad_maximum_fusion.s_ref = f32[2,1024,8,128]{3,2,1,0:T(8,128)} fusion(f32[1,1024,8,128]{3,2,1,0:T(8,128)S(1)} %bitcast.42, f32[1,1024,8,128]{3,2,1,0:T(8,128)S(1)} %bitcast.41), kind=kLoop, calls=%fused_computation | loop fusion | flops 2097152 | bytes 16777216 | tf_op jit(solution)/shard_map/stack | solution.py:241
  36.6 29.7 %shard_map.82 = f32[16384,1]{1,0:T(8,128)} custom-call(s32[32]{0:T(128)} %reshape.188.n_ref, s32[16384]{0:T(1024)} %bitcast.56, f32[2,16384]{1,0:T(2,128)} %bitcast.54, f32[2,1024,8,128]{3,2,1,0:T(8,128)} %pad_maximum_fusion.s_ref), custom_call_target="tpu_custom_call" | custom-call | tf_op jit(solution)/shard_map/pallas_call | solution.py:142
  66.3 4.6 %reduce.2 = f32[16384]{0:T(1024)S(1)} reduce(f32[16384,1]{1,0:T(8,128)} %shard_map.82, f32[]{:T(128)} %constant.32), dimensions={1}, to_apply=%pallas_call.6.reduce_sub_computation | reduce | bytes 131076 | tf_op jit(solution)/shard_map/pallas_call | solution.py:142
  71.0 0.7 copy.76
  71.7 45.1 %all-to-all-start.1 = ((f32[16,2,512]{2,1,0:T(2,128)}), f32[16,2,512]{2,1,0:T(2,128)S(1)}, u32[]{:S(2)}, u32[]{:S(2)}) async-start(f32[16,2,512]{2,1,0:T(2,128)} %copy.76), calls=%async_computation.1 | async-start | bytes 131072 | tf_op jit(solution)/shard_map/all_to_all | solution.py:243
  116.8 0.6 copy.82
  117.5 0.6 convert_reduce_fusion.1.n_ref
  118.2 5.5 %all-to-all-done.1 = f32[16,2,512]{2,1,0:T(2,128)S(1)} async-done(((f32[16,2,512]{2,1,0:T(2,128)}), f32[16,2,512]{2,1,0:T(2,128)S(1)}, u32[]{:S(2)}, u32[]{:S(2)}) %all-to-all-start.1) | async-done | bytes 65568 | tf_op jit(solution)/shard_map/all_to_all | solution.py:243
  123.8 2.6 %copy.77 = f32[16,512,2]{2,1,0:T(8,128)} copy(f32[16,512,2]{1,2,0:T(2,128)S(1)} %pad_maximum_fusion.2) | data formatting | bytes 131072 | tf_op jit(solution)/shard_map/stack | solution.py:244
  126.4 4.5 %reshape_reshape.11.v_ref = f32[16384]{0:T(1024)} reshape(f32[16,512,2]{2,1,0:T(8,128)} %copy.77) | data formatting | bytes 131072 | tf_op jit(solution)/shard_map/reshape;reshape | solution.py:180
  130.9 11.9 %shard_map.83 = f32[4097]{0:T(1024)} custom-call(s32[16]{0:T(128)} %convert_reduce_fusion.1.n_ref, s32[16384]{0:T(1024)} %bitcast.59, f32[16384]{0:T(1024)} %reshape_reshape.11.v_ref), custom_call_target="tpu_custom_call" | custom-call | tf_op jit(solution)/shard_map/pallas_call | solution.py:171
  142.8 0.7 slice.93
  143.5 4.4 %all_gather.6 = f32[16,512]{1,0:T(8,128)S(1)} all-gather(f32[16,256]{1,0:T(8,128)S(1)} %reshape.191), channel_id=1, replica_groups=mesh['stn'=16,'chan'=2] {'chan'}, dimensions={1}, use_global_device_ids=true | all-gather | bytes 49152 | tf_op jit(solution)/shard_map/all_gather | solution.py:253
  147.9 19.9 %all_gather.7 = f32[256,515]{1,0:T(8,128)S(1)} all-gather(f32[16,515]{1,0:T(8,128)S(1)} %pad_maximum_fusion.3), channel_id=1, replica_groups=mesh['stn'=16,'chan'=2] {'stn'}, dimensions={0}, use_global_device_ids=true | all-gather | bytes 560320 | tf_op jit(solution)/shard_map/all_gather | solution.py:255
  167.8 0.3 slice_reduce_fusion.2
  168.2 0.2 multiply_add_fusion
  168.3 3.9 %multiply_convert_fusion = (bf16[256,2,512]{2,0,1:T(8,128)(2,1)S(1)}, bf16[256,2,512]{2,0,1:T(8,128)(2,1)S(1)}) fusion(f32[2,512]{1,0:T(2,128)S(1)} %multiply_multiply_fusion, f32[2]{0:T(128)S(1)} %get-tuple-element.14, f32[256,512]{1,0:T(8,128)S(1)} %slice.97, f32[256,512]{1,0:T(8,128)S(1)} %multiply_add_fusion, f32[2]{0:T(128)S(1)} %broadcast_multiply_fusion), kind=kLoop, calls=%fused_computation.19 | loop fusion | flops 1835008 | bytes 2101264 | tf_op jit(solution)/shard_map/convert_element_type | solution.py:206
  172.3 3.9 %fusion.13 = (bf16[256,2,512]{2,0,1:T(8,128)(2,1)S(1)}, bf16[256,2,512]{2,0,1:T(8,128)(2,1)S(1)}, bf16[256,2,512]{2,0,1:T(8,128)(2,1)S(1)}) fusion(f32[2,512]{1,0:T(2,128)S(1)} %multiply_multiply_fusion, f32[2]{0:T(128)S(1)} %get-tuple-element.14, f32[256,512]{1,0:T(8,128)S(1)} %slice.97, f32[256,512]{1,0:T(8,128)S(1)} %multiply_add_fusion, ...), kind=kLoop, calls=%fused_computation.40 | loop fusion | flops 2621440 | bytes 2625552 | tf_op jit(solution)/shard_map/neg | solution.py:208
  176.2 0.7 fusion
  177.0 0.9 fusion.11
  177.8 16.9 %all_to_all.19 = bf16[2,2,256,256]{3,1,0,2:T(2,128)(2,1)S(1)} all-to-all(bf16[2,2,256,256]{3,1,0,2:T(2,128)(2,1)S(1)} %fusion.11), channel_id=1, replica_groups=mesh['stn'=16,'chan'=2] {'stn'}, dimensions={2} | all-to-all | bytes 1048576 | tf_op jit(solution)/shard_map/all_to_all | solution.py:268
  194.7 0.4 convert_bitcast_fusion
  195.2 1.2 copy.80
  (33 shorter events, 0.6 us)
Async XLA Ops:
  0.0 26.1 %collective-permute-start = (f32[1024,512]{1,0:T(8,128)}, f32[1024,512]{1,0:T(8,128)}, u32[]{:S(2)}, u32[]{:S(2)}) collective-permute-start(f32[1024,512]{1,0:T(8,128)} %bitcast.43), channel_id=1, source_target_pairs={{0,2},{2,0},{4,6},{6,4},{8,10},{10,8},{12,14},{14,12},{16,18},{18,... | collective-permute-start | bytes 6291464 | tf_op jit(solution)/shard_map/ppermute | solution.py:240
  3.1 12.9 %copy-start.1 = (f32[2,512,512]{2,1,0:T(8,128)S(1)}, f32[2,512,512]{2,1,0:T(8,128)}, u32[]{:S(2)}) copy-start(f32[2,512,512]{2,1,0:T(8,128)} %param.8) | copy-start | bytes 6291460
  5.7 11.9 %copy-start.7 = (f32[32]{0:T(128)S(1)}, f32[32]{0:T(128)}, u32[]{:S(2)}) copy-start(f32[32]{0:T(128)} %param.13) | copy-start | bytes 388
  5.7 12.0 %copy-start.4 = (f32[512]{0:T(512)S(1)}, f32[512]{0:T(512)}, u32[]{:S(2)}) copy-start(f32[512]{0:T(512)} %param.15) | copy-start | bytes 6148
  5.7 12.0 %copy-start.5 = (f32[512]{0:T(512)S(1)}, f32[512]{0:T(512)}, u32[]{:S(2)}) copy-start(f32[512]{0:T(512)} %param.14) | copy-start | bytes 6148
  9.0 14.9 %all-to-all-start = ((f32[2,16,2,512]{3,2,0,1:T(2,128)}), f32[2,16,2,512]{3,2,0,1:T(2,128)S(1)}, u32[]{:S(2)}, u32[]{:S(2)}) async-start(f32[2,16,2,512]{3,2,0,1:T(2,128)} %copy.72), calls=%async_computation | async-start | bytes 262144 | tf_op jit(solution)/shard_map/all_to_all | solution.py:236
  19.8 3.0 %copy-start.3 = (f32[3,512]{1,0:T(4,128)S(1)}, f32[3,512]{1,0:T(4,128)}, u32[]{:S(2)}) copy-start(f32[3,512]{1,0:T(4,128)} %param.12) | copy-start | bytes 18436
  30.7 2.2 %copy-start = (f32[128,8,8,128]{3,2,1,0:T(8,128)S(1)}, f32[128,8,8,128]{3,2,1,0:T(8,128)}, u32[]{:S(2)}) copy-start(f32[128,8,8,128]{3,2,1,0:T(8,128)} %copy.85) | copy-start | bytes 12582916
  66.3 50.5 %copy-start.2 = (s32[1,1,16,1024]{3,2,1,0:T(8,128)S(1)}, s32[1,1,16,1024]{3,2,1,0:T(8,128)}, u32[]{:S(2)}) copy-start(s32[1,1,16,1024]{3,2,1,0:T(8,128)} %param.10) | copy-start | bytes 196612
  66.3 51.1 %copy-start.6 = (f32[3,16]{1,0:T(4,128)S(1)}, f32[3,16]{1,0:T(4,128)}, u32[]{:S(2)}) copy-start(f32[3,16]{1,0:T(4,128)} %param.11) | copy-start | bytes 580
  71.7 52.0 %all-to-all-start.1 = ((f32[16,2,512]{2,1,0:T(2,128)}), f32[16,2,512]{2,1,0:T(2,128)S(1)}, u32[]{:S(2)}, u32[]{:S(2)}) async-start(f32[16,2,512]{2,1,0:T(2,128)} %copy.76), calls=%async_computation.1 | async-start | bytes 131072 | tf_op jit(solution)/shard_map/all_to_all | solution.py:243

commit v8 on v7

--- a/solution.py
+++ b/solution.py
@@ -155,12 +155,15 @@
 def _scatter_kernel(n_ref, d_ref, v_ref, o_ref):
     rows = n_ref.shape[0]
     width = d_ref.shape[0] // rows
-    step = 8 if width % 8 == 0 else 1
+    half = width // 2
+    step = 8 if width % 8 == 0 else 2
     for row in range(rows):
         def body(i, carry, row=row):
             for u in range(step):
                 slot = row * width + i * step + u
-                o_ref[d_ref[slot]] = v_ref[slot]
+                parity = u % 2
+                source = ((row ^ parity) * 2 + parity) * half + i * (step // 2) + u // 2
+                o_ref[d_ref[slot]] = v_ref[source]
             return carry
 
         lax.fori_loop(0, (n_ref[row] + step - 1) // step, body, 0)
@@ -241,8 +244,7 @@
     tables = jnp.stack([pair_table(screen2d), pair_table(partner)])
     sampled = interpolate_balanced(tables, kin, live).transpose(1, 0, 2)
     back = lax.all_to_all(sampled, "stn", split_axis=0, concat_axis=0, tiled=True)
-    returned = jnp.stack([back[:, 0, :], swap(back[None, :, 1, :])[0]], axis=-1).reshape(groups, capacity)
-    buffer = scatter_kernel(query_dest.reshape(groups, capacity), returned, queries + 1)
+    buffer = scatter_kernel(query_dest.reshape(groups, capacity), back, queries + 1)
     own_iono = buffer[:queries].reshape(stations_local, local_sources)
     station_rows = positions.T
     total_stations = stations_local * groups

time: 199 us -> 192 us (0.965)
  local copies, waits for them, and re-layouts: 27.8 us -> 21.3 us
  Pallas kernels: 41.6 us -> 45 us
  starting transfers between devices: 52.6 us -> 49.7 us
    another operation x3 -> x0, local copies, waits for them, and re-layouts: 7.21 us -> none  [the longest x1 4.52 us: scatter_kernel(): vals.reshape(-1)]
    pallas_call x1, Pallas kernels: 29.7 us -> 32.8 us  [interpolate_balanced(): pl.pallas_call(_balanced_kernel, grid_spec=pltpu.PrefetchScalarGridSpec(n...]
    all_to_all x1, starting transfers between devices: 45.1 us -> 42.2 us  [body(): lax.all_to_all(sampled, 'stn', split_axis=0, concat_axis=0, tiled=True)]
    unnamed x23 -> x24, local copies, waits for them, and re-layouts: 8.51 us -> 9.14 us
where the time goes in v8:
time: 192 us; the launch traced here: 190 us
  starting transfers between devices  49.7 us (26%)
  Pallas kernels  45 us (23%)
  blocking collectives  41.1 us (21%)
  other arithmetic  25.4 us (13%)
  local copies, waits for them, and re-layouts  21.3 us (11%)
  waiting for transfers between devices  6.62 us (3%)
    all_to_all x1, starting transfers between devices, body(): lax.all_to_all(sampled, 'stn', split_axis=0, concat_axis=0, tiled=True)  42.2 us
    pallas_call x1, Pallas kernels, interpolate_balanced(): pl.pallas_call(_balanced_kernel, grid_spec=pltpu.PrefetchScalarGridSpec(n...  32.8 us
    all_gather x1, blocking collectives, body(): gathered = lax.all_gather(packed, 'stn', axis=0, tiled=True)  19.8 us
    all_to_all x1, blocking collectives, body(): lax.all_to_all(visible.astype(jnp.bfloat16), 'stn', split_axis=2, concat_...  16.9 us
    pallas_call x1, Pallas kernels, scatter_kernel(): pl.pallas_call(_scatter_kernel, grid_spec=pltpu.PrefetchScalarGridSpec(nu...  12.2 us
    unnamed x24, local copies, waits for them, and re-layouts  9.14 us
    all_to_all x1, starting transfers between devices, body(): lax.all_to_all(send, 'stn', split_axis=1, concat_axis=1, tiled=True)  7.01 us
    all_to_all x1, waiting for transfers between devices, body(): lax.all_to_all(sampled, 'stn', split_axis=0, concat_axis=0, tiled=True)  5.5 us
  transfers between devices with their start and end apart: 3, of which 2 were waited for; matrix products, arithmetic and copies ran while one was open for 10% of the time, Pallas kernels for 0%

profile of v8, /device:TPU:0, one launch (start us, length us, event | category | flops | bytes accessed | tf_op | source)
XLA Modules:
  0.0 190.2 jit_solution(3605710796785413143)
XLA Ops:
  0.0 0.5 collective-permute-start
  0.5 0.8 broadcast_compare_fusion
  1.3 1.2 copy.66
  2.6 0.3 copy.65
  2.9 0.2 ge.18
  3.1 0.7 broadcast_select_fusion
  3.8 1.6 fusion.15
  5.4 0.3 copy.67
  5.7 1.0 copy.68
  6.7 1.3 pad_maximum_fusion.1
  8.0 1.0 copy.69
  9.0 7.0 %all-to-all-start = ((f32[2,16,2,512]{3,2,0,1:T(2,128)}), f32[2,16,2,512]{3,2,0,1:T(2,128)S(1)}, u32[]{:S(2)}, u32[]{:S(2)}) async-start(f32[2,16,2,512]{3,2,0,1:T(2,128)} %copy.69), calls=%async_computation | async-start | bytes 262144 | tf_op jit(solution)/shard_map/all_to_all | solution.py:239
  16.0 1.6 slice.79
  17.8 2.0 %maximum_bitcast_fusion = f32[128,8,8,128]{3,1,2,0:T(8,128)S(1)} fusion(f32[1,512]{1,0:T(1,128)S(1)} %slice.80, f32[1023,512]{1,0:T(8,128)} %slice.79, f32[1024,512]{1,0:T(8,128)S(1)} %bitcast.44), kind=kLoop, calls=%fused_computation.1 | loop fusion | flops 2097152 | bytes 8388608
  19.8 2.9 %copy.81 = f32[128,8,8,128]{3,2,1,0:T(8,128)} copy(f32[128,8,8,128]{3,1,2,0:T(8,128)S(1)} %maximum_bitcast_fusion) | data formatting | bytes 8388608
  22.8 1.1 all-to-all-done
  23.9 0.6 copy.79
  24.6 0.1 convert_reduce_fusion
  24.7 0.7 reshape.191.n_ref
  25.4 0.8 copy.80
  26.1 1.8 slice.81
  28.0 0.7 slice.82
  28.7 2.0 %maximum_bitcast_fusion.1 = f32[128,8,8,128]{3,1,2,0:T(8,128)S(1)} fusion(f32[1,512]{1,0:T(1,128)S(1)} %slice.82, f32[1023,512]{1,0:T(8,128)S(1)} %slice.81, f32[1024,512]{1,0:T(8,128)} %collective-permute-done), kind=kLoop, calls=%fused_computation.2 | loop fusion | flops 2097152 | bytes 8388608
  30.7 1.0 copy.82
  31.8 1.1 copy-done
  32.9 3.8 %pad_maximum_fusion.s_ref = f32[2,1024,8,128]{3,2,1,0:T(8,128)} fusion(f32[1,1024,8,128]{3,2,1,0:T(8,128)S(1)} %bitcast.40, f32[1,1024,8,128]{3,2,1,0:T(8,128)S(1)} %bitcast.39), kind=kLoop, calls=%fused_computation | loop fusion | flops 2097152 | bytes 16777216 | tf_op jit(solution)/shard_map/stack | solution.py:244
  36.7 32.8 %shard_map.82 = f32[16384,1]{1,0:T(8,128)} custom-call(s32[32]{0:T(128)} %reshape.191.n_ref, s32[16384]{0:T(1024)} %bitcast.54, f32[2,16384]{1,0:T(2,128)} %bitcast.52, f32[2,1024,8,128]{3,2,1,0:T(8,128)} %pad_maximum_fusion.s_ref), custom_call_target="tpu_custom_call" | custom-call | tf_op jit(solution)/shard_map/pallas_call | solution.py:142
  69.4 4.6 %reduce.2 = f32[16384]{0:T(1024)S(1)} reduce(f32[16384,1]{1,0:T(8,128)} %shard_map.82, f32[]{:T(128)} %constant.32), dimensions={1}, to_apply=%pallas_call.6.reduce_sub_computation | reduce | bytes 131076 | tf_op jit(solution)/shard_map/pallas_call | solution.py:142
  74.1 0.7 copy.73
  74.8 42.2 %all-to-all-start.1 = ((f32[16,2,512]{2,1,0:T(2,128)}), f32[16,2,512]{2,1,0:T(2,128)S(1)}, u32[]{:S(2)}, u32[]{:S(2)}) async-start(f32[16,2,512]{2,1,0:T(2,128)} %copy.73), calls=%async_computation.1 | async-start | bytes 131072 | tf_op jit(solution)/shard_map/all_to_all | solution.py:246
  117.1 0.6 copy.78
  117.7 0.1 copy.74
  117.8 0.6 convert_reduce_fusion.1.n_ref
  118.4 5.5 %all-to-all-done.1 = f32[16,2,512]{2,1,0:T(2,128)S(1)} async-done(((f32[16,2,512]{2,1,0:T(2,128)}), f32[16,2,512]{2,1,0:T(2,128)S(1)}, u32[]{:S(2)}, u32[]{:S(2)}) %all-to-all-start.1) | async-done | bytes 65568 | tf_op jit(solution)/shard_map/all_to_all | solution.py:246
  123.9 0.6 copy.83
  124.5 12.2 %shard_map.83 = f32[4097]{0:T(1024)} custom-call(s32[16]{0:T(128)} %convert_reduce_fusion.1.n_ref, s32[16384]{0:T(1024)} %bitcast.57, f32[16384]{0:T(1024)} %bitcast.58), custom_call_target="tpu_custom_call" | custom-call | tf_op jit(solution)/shard_map/pallas_call | solution.py:174
  136.8 0.7 slice.83
  137.5 4.4 %all_gather.6 = f32[16,512]{1,0:T(8,128)S(1)} all-gather(f32[16,256]{1,0:T(8,128)S(1)} %reshape.195), channel_id=1, replica_groups=mesh['stn'=16,'chan'=2] {'chan'}, dimensions={1}, use_global_device_ids=true | all-gather | bytes 49152 | tf_op jit(solution)/shard_map/all_gather | solution.py:255
  141.9 19.8 %all_gather.7 = f32[256,515]{1,0:T(8,128)S(1)} all-gather(f32[16,515]{1,0:T(8,128)S(1)} %pad_maximum_fusion.2), channel_id=1, replica_groups=mesh['stn'=16,'chan'=2] {'stn'}, dimensions={0}, use_global_device_ids=true | all-gather | bytes 560320 | tf_op jit(solution)/shard_map/all_gather | solution.py:257
  161.7 0.3 slice_reduce_fusion.2
  162.1 0.2 multiply_add_fusion
  162.3 3.9 %multiply_convert_fusion = (bf16[256,2,512]{2,0,1:T(8,128)(2,1)S(1)}, bf16[256,2,512]{2,0,1:T(8,128)(2,1)S(1)}) fusion(f32[2,512]{1,0:T(2,128)S(1)} %multiply_multiply_fusion, f32[2]{0:T(128)S(1)} %get-tuple-element.14, f32[256,512]{1,0:T(8,128)S(1)} %slice.87, f32[256,512]{1,0:T(8,128)S(1)} %multiply_add_fusion, f32[2]{0:T(128)S(1)} %broadcast_multiply_fusion), kind=kLoop, calls=%fused_computation.19 | loop fusion | flops 1835008 | bytes 2101264 | tf_op jit(solution)/shard_map/convert_element_type | solution.py:209
  166.2 3.9 %fusion.13 = (bf16[256,2,512]{2,0,1:T(8,128)(2,1)S(1)}, bf16[256,2,512]{2,0,1:T(8,128)(2,1)S(1)}, bf16[256,2,512]{2,0,1:T(8,128)(2,1)S(1)}) fusion(f32[2,512]{1,0:T(2,128)S(1)} %multiply_multiply_fusion, f32[2]{0:T(128)S(1)} %get-tuple-element.14, f32[256,512]{1,0:T(8,128)S(1)} %slice.87, f32[256,512]{1,0:T(8,128)S(1)} %multiply_add_fusion, ...), kind=kLoop, calls=%fused_computation.38 | loop fusion | flops 2621440 | bytes 2625552 | tf_op jit(solution)/shard_map/neg | solution.py:211
  170.1 0.7 fusion
  170.9 0.9 fusion.11
  171.7 16.9 %all_to_all.19 = bf16[2,2,256,256]{3,1,0,2:T(2,128)(2,1)S(1)} all-to-all(bf16[2,2,256,256]{3,1,0,2:T(2,128)(2,1)S(1)} %fusion.11), channel_id=1, replica_groups=mesh['stn'=16,'chan'=2] {'stn'}, dimensions={2} | all-to-all | bytes 1048576 | tf_op jit(solution)/shard_map/all_to_all | solution.py:270
  188.6 0.4 convert_bitcast_fusion
  189.1 1.2 copy.76
  (29 shorter events, 0.4 us)
Async XLA Ops:
  0.0 26.1 %collective-permute-start = (f32[1024,512]{1,0:T(8,128)}, f32[1024,512]{1,0:T(8,128)}, u32[]{:S(2)}, u32[]{:S(2)}) collective-permute-start(f32[1024,512]{1,0:T(8,128)} %bitcast.41), channel_id=1, source_target_pairs={{0,2},{2,0},{4,6},{6,4},{8,10},{10,8},{12,14},{14,12},{16,18},{18,... | collective-permute-start | bytes 6291464 | tf_op jit(solution)/shard_map/ppermute | solution.py:243
  3.1 12.9 %copy-start.1 = (f32[2,512,512]{2,1,0:T(8,128)S(1)}, f32[2,512,512]{2,1,0:T(8,128)}, u32[]{:S(2)}) copy-start(f32[2,512,512]{2,1,0:T(8,128)} %param.8) | copy-start | bytes 6291460
  5.7 11.9 %copy-start.7 = (f32[32]{0:T(128)S(1)}, f32[32]{0:T(128)}, u32[]{:S(2)}) copy-start(f32[32]{0:T(128)} %param.13) | copy-start | bytes 388
  5.7 12.0 %copy-start.4 = (f32[512]{0:T(512)S(1)}, f32[512]{0:T(512)}, u32[]{:S(2)}) copy-start(f32[512]{0:T(512)} %param.15) | copy-start | bytes 6148
  5.7 12.0 %copy-start.5 = (f32[512]{0:T(512)S(1)}, f32[512]{0:T(512)}, u32[]{:S(2)}) copy-start(f32[512]{0:T(512)} %param.14) | copy-start | bytes 6148
  9.0 14.9 %all-to-all-start = ((f32[2,16,2,512]{3,2,0,1:T(2,128)}), f32[2,16,2,512]{3,2,0,1:T(2,128)S(1)}, u32[]{:S(2)}, u32[]{:S(2)}) async-start(f32[2,16,2,512]{3,2,0,1:T(2,128)} %copy.69), calls=%async_computation | async-start | bytes 262144 | tf_op jit(solution)/shard_map/all_to_all | solution.py:239
  19.8 3.0 %copy-start.3 = (f32[3,512]{1,0:T(4,128)S(1)}, f32[3,512]{1,0:T(4,128)}, u32[]{:S(2)}) copy-start(f32[3,512]{1,0:T(4,128)} %param.12) | copy-start | bytes 18436
  30.7 2.2 %copy-start = (f32[128,8,8,128]{3,2,1,0:T(8,128)S(1)}, f32[128,8,8,128]{3,2,1,0:T(8,128)}, u32[]{:S(2)}) copy-start(f32[128,8,8,128]{3,2,1,0:T(8,128)} %copy.81) | copy-start | bytes 12582916
  69.4 47.6 %copy-start.2 = (s32[1,1,16,1024]{3,2,1,0:T(8,128)S(1)}, s32[1,1,16,1024]{3,2,1,0:T(8,128)}, u32[]{:S(2)}) copy-start(s32[1,1,16,1024]{3,2,1,0:T(8,128)} %param.10) | copy-start | bytes 196612
  69.4 48.3 %copy-start.6 = (f32[3,16]{1,0:T(4,128)S(1)}, f32[3,16]{1,0:T(4,128)}, u32[]{:S(2)}) copy-start(f32[3,16]{1,0:T(4,128)} %param.11) | copy-start | bytes 580
  74.8 49.1 %all-to-all-start.1 = ((f32[16,2,512]{2,1,0:T(2,128)}), f32[16,2,512]{2,1,0:T(2,128)S(1)}, u32[]{:S(2)}, u32[]{:S(2)}) async-start(f32[16,2,512]{2,1,0:T(2,128)} %copy.73), calls=%async_computation.1 | async-start | bytes 131072 | tf_op jit(solution)/shard_map/all_to_all | solution.py:246

commit v9 on v5

--- a/solution.py
+++ b/solution.py
@@ -85,15 +85,81 @@
     return out[:, 0]
 
 
+def _balanced_kernel(n_ref, r_ref, c_ref, own_ref, partner_ref, o_ref):
+    rows = own_ref.shape[0]
+    nb = own_ref.shape[1]
+    cols = nb * 128
+    senders = n_ref.shape[0] // 2
+    seg = o_ref.shape[0] // (2 * senders)
+    unroll = min(UNROLL, seg)
+    sub = lax.broadcasted_iota(jnp.int32, (nb, 128), 0)
+    lane = lax.broadcasted_iota(jnp.int32, (nb, 128), 1)
+    col = (sub * 128 + lane).astype(jnp.float32)
+    rowid = lax.broadcasted_iota(jnp.int32, (8, 128), 0)
+
+    for h, s_ref in enumerate((own_ref, partner_ref)):
+        def segment(s, carry, h=h, s_ref=s_ref):
+            def group(g, carry2):
+                for part in range(unroll // 8):
+                    acc = jnp.zeros((8, 128), jnp.float32)
+                    first = (h * senders + s) * seg + g * unroll + part * 8
+                    for u in range(8):
+                        j = first + u
+                        r = r_ref[j]
+                        lower = s_ref[r]
+                        upper = s_ref[r + 1]
+                        y = jnp.full((nb, 128), c_ref[0, j], jnp.float32) * (rows - 1)
+                        x = jnp.full((nb, 128), c_ref[1, j], jnp.float32) * (cols - 1)
+                        ry = jnp.clip(jnp.floor(y), 0.0, rows - 2.0)
+                        kx = jnp.clip(jnp.floor(x), 0.0, cols - 2.0)
+                        fy = y - ry
+                        fx = x - kx
+                        blend = (1.0 - fy) * lower + fy * upper
+                        wx = jnp.where(col == kx, 1.0 - fx, jnp.where(col == kx + 1.0, fx, 0.0))
+                        row = jnp.sum(blend * wx, axis=0, keepdims=True)
+                        acc = jnp.where(rowid == u, row, acc)
+                    o_ref[pl.ds(pl.multiple_of(first, 8), 8), :] = jnp.sum(acc, axis=1, keepdims=True)
+                return carry2
+
+            trips = (n_ref[h * senders + s] + unroll - 1) // unroll
+            lax.fori_loop(0, trips, group, 0)
+            return carry
+
+        lax.fori_loop(0, senders, segment, 0)
+
+
+def interpolate_balanced(own, partner, coords, live):
+    rows, cols = own.shape
+    nb = cols // 128
+    _, halves, senders, seg = coords.shape
+    flat = coords.reshape(2, halves * senders * seg)
+    r = jnp.clip(jnp.floor(flat[0] * (rows - 1)), 0.0, rows - 2.0).astype(jnp.int32)
+    spec = pl.BlockSpec((rows, nb, 128), lambda i, n, rr, cc: (0, 0, 0))
+    out = pl.pallas_call(
+        _balanced_kernel,
+        grid_spec=pltpu.PrefetchScalarGridSpec(
+            num_scalar_prefetch=3,
+            grid=(1,),
+            in_specs=[spec, spec],
+            out_specs=pl.BlockSpec((halves * senders * seg, 1), lambda i, n, rr, cc: (0, 0)),
+        ),
+        out_shape=jax.ShapeDtypeStruct((halves * senders * seg, 1), jnp.float32),
+    )(live, r, flat, own.reshape(rows, nb, 128), partner.reshape(rows, nb, 128))
+    return out.reshape(halves, senders, seg)
+
+
 def _scatter_kernel(n_ref, d_ref, v_ref, o_ref):
     rows = n_ref.shape[0]
     width = d_ref.shape[0] // rows
-    step = 8 if width % 8 == 0 else 1
+    half = width // 2
+    step = 8 if width % 8 == 0 else 2
     for row in range(rows):
         def body(i, carry, row=row):
             for u in range(step):
                 slot = row * width + i * step + u
-                o_ref[d_ref[slot]] = v_ref[slot]
+                parity = u % 2
+                source = ((row ^ parity) * 2 + parity) * half + i * (step // 2) + u // 2
+                o_ref[d_ref[slot]] = v_ref[source]
             return carry
 
         lax.fori_loop(0, (n_ref[row] + step - 1) // step, body, 0)
@@ -157,16 +223,23 @@
     strip_rows = screen.shape[0] * screen.shape[1]
     values = screen.reshape(-1)
     capacity = query_dest.shape[3]
-    coords = pierce_coords.reshape(2, groups, capacity)
-    received = lax.all_to_all(coords, "stn", split_axis=1, concat_axis=1, tiled=True)
-    sampled = interpolate_kernel(
-        values.reshape(strip_rows, tile_cols), received.reshape(2, groups * capacity)
-    ).reshape(groups, capacity)
-    returned = lax.all_to_all(sampled, "stn", split_axis=0, concat_axis=0, tiled=True)
     stations_local = positions.shape[1]
     local_sources = source_flux.shape[0] // lax.axis_size("chan")
     queries = stations_local * local_sources
-    buffer = scatter_kernel(query_dest.reshape(groups, capacity), returned, queries + 1)
+    half = capacity // 2
+    coords = pierce_coords.reshape(2, groups, capacity)
+    dead = query_dest.reshape(groups, capacity) >= queries
+    coords = jnp.where(dead[None], -1.0, coords).reshape(2, groups, half, 2)
+    swap = lambda a: a.reshape(a.shape[0], groups // 2, 2, half)[:, :, ::-1, :].reshape(a.shape[0], groups, half)
+    send = jnp.stack([coords[..., 0], swap(coords[..., 1])], axis=2)
+    received = lax.all_to_all(send, "stn", split_axis=1, concat_axis=1, tiled=True)
+    kin = received.transpose(0, 2, 1, 3)
+    live = jnp.sum((kin[0] >= 0.0).astype(jnp.int32), axis=2).reshape(-1)
+    screen2d = values.reshape(strip_rows, tile_cols)
+    partner = lax.ppermute(screen2d, "stn", [(i, i ^ 1) for i in range(groups)])
+    sampled = interpolate_balanced(screen2d, partner, kin, live).transpose(1, 0, 2)
+    back = lax.all_to_all(sampled, "stn", split_axis=0, concat_axis=0, tiled=True)
+    buffer = scatter_kernel(query_dest.reshape(groups, capacity), back, queries + 1)
     own_iono = buffer[:queries].reshape(stations_local, local_sources)
     station_rows = positions.T
     total_stations = stations_local * groups
@@ -189,7 +262,8 @@
     ids = jnp.arange(total_stations, dtype=jnp.int32)
     cross_only = ids[:, None] != ids[None, :]
     visible = jnp.where(cross_only[None, None], visible, jnp.zeros_like(visible))
-    return lax.all_to_all(visible, "stn", split_axis=2, concat_axis=0, tiled=True)
+    moved = lax.all_to_all(visible.astype(jnp.bfloat16), "stn", split_axis=2, concat_axis=0, tiled=True)
+    return moved.astype(jnp.float32)
 
 
 def _rows_path(own_iono, station_rows, directions, freq_ratio, source_flux, spectral_index):

time: 231 us -> 187 us (0.81)
  Pallas kernels: 123 us -> 45.1 us
  starting transfers between devices: 13.4 us -> 53.4 us
  blocking collectives: 51.2 us -> 41 us
  waiting for transfers between devices: 5.44 us -> 11.3 us
  other arithmetic: 22 us -> 17.7 us
  local copies, waits for them, and re-layouts: 12.8 us -> 16.7 us
    pallas_call x1, Pallas kernels: 111 us -> 32.8 us  [interpolate_balanced(): pl.pallas_call(_balanced_kernel, grid_spec=pltpu.PrefetchScalarGridSpec(n...]
    all_to_all x1, starting transfers between devices: 6.01 us -> 45.9 us  [body(): lax.all_to_all(sampled, 'stn', split_axis=0, concat_axis=0, tiled=True)]
    all_to_all x1, blocking collectives: 27.4 us -> 16.9 us  [body(): lax.all_to_all(visible.astype(jnp.bfloat16), 'stn', split_axis=2, concat_...]
    concatenate x2 -> x0, other arithmetic: 6.77 us -> none  [interpolate_kernel(): pair = jnp.concatenate([screen2d, jnp.roll(screen2d, -1, axis=0)], axis=1)]
    all_to_all x1, waiting for transfers between devices: 0.01 us -> 5.91 us  [body(): lax.all_to_all(send, 'stn', split_axis=1, concat_axis=1, tiled=True)]
    another operation x0 -> x3, local copies, waits for them, and re-layouts: none -> 3.75 us  [the longest x2 1.98 us: body(): send = jnp.stack([coords[..., 0], swap(coords[..., 1])], axis=2)]
    reshape x0 -> x3, local copies, waits for them, and re-layouts: none -> 3.51 us  [the longest x1 2.89 us: interpolate_balanced(): partner.reshape(rows, nb, 128)]
    concatenate x2 -> x0, local copies, waits for them, and re-layouts: 3.48 us -> none  [interpolate_kernel(): pair = jnp.concatenate([screen2d, jnp.roll(screen2d, -1, axis=0)], axis=1)]
  transfers between devices with their start and end apart: 2 -> 3, of which waited for: 1 -> 2; matrix products, arithmetic and copies ran while one was open for 7% -> 8% of each run, Pallas kernels for 0% -> 0%
where the time goes in v9:
time: 187 us; the launch traced here: 186 us
  starting transfers between devices  53.4 us (29%)
  Pallas kernels  45.1 us (24%)
  blocking collectives  41 us (22%)
  other arithmetic  17.7 us (9%)
  local copies, waits for them, and re-layouts  16.7 us (9%)
  waiting for transfers between devices  11.3 us (6%)
    all_to_all x1, starting transfers between devices, body(): lax.all_to_all(sampled, 'stn', split_axis=0, concat_axis=0, tiled=True)  45.9 us
    pallas_call x1, Pallas kernels, interpolate_balanced(): pl.pallas_call(_balanced_kernel, grid_spec=pltpu.PrefetchScalarGridSpec(n...  32.8 us
    all_gather x1, blocking collectives, body(): gathered = lax.all_gather(packed, 'stn', axis=0, tiled=True)  19.7 us
    all_to_all x1, blocking collectives, body(): lax.all_to_all(visible.astype(jnp.bfloat16), 'stn', split_axis=2, concat_...  16.9 us
    pallas_call x1, Pallas kernels, scatter_kernel(): pl.pallas_call(_scatter_kernel, grid_spec=pltpu.PrefetchScalarGridSpec(nu...  12.3 us
    all_to_all x1, starting transfers between devices, body(): lax.all_to_all(send, 'stn', split_axis=1, concat_axis=1, tiled=True)  7.01 us
    all_to_all x1, waiting for transfers between devices, body(): lax.all_to_all(send, 'stn', split_axis=1, concat_axis=1, tiled=True)  5.91 us
    all_to_all x1, waiting for transfers between devices, body(): lax.all_to_all(sampled, 'stn', split_axis=0, concat_axis=0, tiled=True)  5.41 us
  transfers between devices with their start and end apart: 3, of which 2 were waited for; matrix products, arithmetic and copies ran while one was open for 8% of the time, Pallas kernels for 0%

profile of v9, /device:TPU:0, one launch (start us, length us, event | category | flops | bytes accessed | tf_op | source)
XLA Modules:
  0.0 186.2 jit_solution(5189028263540046570)
XLA Ops:
  0.0 0.5 collective-permute-start
  0.5 1.2 copy.66
  1.7 0.9 broadcast_compare_fusion
  2.6 0.3 copy.65
  2.9 0.2 ge.18
  3.1 0.7 broadcast_select_fusion
  3.8 1.6 fusion.15
  5.4 0.3 copy.67
  5.7 0.0 copy-start.6
  5.7 0.0 copy-start.3
  5.7 0.0 copy-start.4
  5.7 1.0 copy.68
  6.7 1.3 pad_maximum_fusion
  8.0 1.0 copy.69
  9.0 7.0 %all-to-all-start = ((f32[2,16,2,512]{3,2,0,1:T(2,128)}), f32[2,16,2,512]{3,2,0,1:T(2,128)S(1)}, u32[]{:S(2)}, u32[]{:S(2)}) async-start(f32[2,16,2,512]{3,2,0,1:T(2,128)} %copy.69), calls=%async_computation | async-start | bytes 262144 | tf_op jit(solution)/shard_map/all_to_all | solution.py:235
  16.0 0.1 fusion.14
  16.1 0.1 multiply_multiply_fusion
  16.2 0.0 copy-start.2
  16.2 1.8 reshape_reshape_reshape.3.own_ref
  18.0 5.9 %all-to-all-done = f32[2,16,2,512]{3,2,0,1:T(2,128)S(1)} async-done(((f32[2,16,2,512]{3,2,0,1:T(2,128)}), f32[2,16,2,512]{3,2,0,1:T(2,128)S(1)}, u32[]{:S(2)}, u32[]{:S(2)}) %all-to-all-start) | async-done | bytes 131104 | tf_op jit(solution)/shard_map/all_to_all | solution.py:235
  24.0 0.7 copy.79
  24.6 0.1 convert_reduce_fusion
  24.7 0.6 reshape.194.n_ref
  25.3 0.8 copy.80
  26.1 2.9 %reshape.196.partner_ref = f32[1024,4,128]{2,1,0:T(4,128)} reshape(f32[1024,512]{1,0:T(8,128)} %collective-permute-done) | data formatting | bytes 4194304 | tf_op jit(solution)/shard_map/reshape | solution.py:147
  29.0 32.8 %shard_map.82 = f32[16384,1]{1,0:T(8,128)} custom-call(s32[32]{0:T(128)} %reshape.194.n_ref, s32[16384]{0:T(1024)} %bitcast.41, f32[2,16384]{1,0:T(2,128)} %bitcast.39, f32[1024,4,128]{2,1,0:T(4,128)} %reshape_reshape_reshape.3.own_ref, f32[1024,4,128]{2,1,0:T(4,128)} %reshape.196.partner_ref), custom_call_target="tpu_custom_call" | custom-call | tf_op jit(solution)/shard_map/pallas_call | solution.py:138
  61.8 4.6 %reduce.2 = f32[16384]{0:T(1024)S(1)} reduce(f32[16384,1]{1,0:T(8,128)} %shard_map.82, f32[]{:T(128)} %constant.32), dimensions={1}, to_apply=%pallas_call.6.reduce_sub_computation | reduce | bytes 131076 | tf_op jit(solution)/shard_map/pallas_call | solution.py:138
  66.5 0.7 copy.73
  67.2 45.9 %all-to-all-start.1 = ((f32[16,2,512]{2,1,0:T(2,128)}), f32[16,2,512]{2,1,0:T(2,128)S(1)}, u32[]{:S(2)}, u32[]{:S(2)}) async-start(f32[16,2,512]{2,1,0:T(2,128)} %copy.73), calls=%async_computation.1 | async-start | bytes 131072 | tf_op jit(solution)/shard_map/all_to_all | solution.py:241
  113.1 0.6 copy.78
  113.8 0.1 copy.74
  113.9 0.7 convert_reduce_fusion.1.n_ref
  114.6 5.4 %all-to-all-done.1 = f32[16,2,512]{2,1,0:T(2,128)S(1)} async-done(((f32[16,2,512]{2,1,0:T(2,128)}), f32[16,2,512]{2,1,0:T(2,128)S(1)}, u32[]{:S(2)}, u32[]{:S(2)}) %all-to-all-start.1) | async-done | bytes 65568 | tf_op jit(solution)/shard_map/all_to_all | solution.py:241
  120.0 0.6 copy.81
  120.6 12.3 %shard_map.83 = f32[4097]{0:T(1024)} custom-call(s32[16]{0:T(128)} %convert_reduce_fusion.1.n_ref, s32[16384]{0:T(1024)} %bitcast.44, f32[16384]{0:T(1024)} %bitcast.45), custom_call_target="tpu_custom_call" | custom-call | tf_op jit(solution)/shard_map/pallas_call | solution.py:170
  132.9 0.7 slice.61
  133.6 4.4 %all_gather.6 = f32[16,512]{1,0:T(8,128)S(1)} all-gather(f32[16,256]{1,0:T(8,128)S(1)} %reshape.199), channel_id=1, replica_groups=mesh['stn'=16,'chan'=2] {'chan'}, dimensions={1}, use_global_device_ids=true | all-gather | bytes 49152 | tf_op jit(solution)/shard_map/all_gather | solution.py:250
  138.0 19.7 %all_gather.7 = f32[256,515]{1,0:T(8,128)S(1)} all-gather(f32[16,515]{1,0:T(8,128)S(1)} %pad_maximum_fusion.1), channel_id=1, replica_groups=mesh['stn'=16,'chan'=2] {'stn'}, dimensions={0}, use_global_device_ids=true | all-gather | bytes 560320 | tf_op jit(solution)/shard_map/all_gather | solution.py:252
  157.7 0.3 slice_reduce_fusion.2
  158.0 0.1 slice.65
  158.1 0.2 multiply_add_fusion
  158.2 3.9 %fusion.13 = (bf16[256,2,512]{2,0,1:T(8,128)(2,1)S(1)}, bf16[256,2,512]{2,0,1:T(8,128)(2,1)S(1)}, bf16[256,2,512]{2,0,1:T(8,128)(2,1)S(1)}) fusion(f32[2,512]{1,0:T(2,128)S(1)} %multiply_multiply_fusion, f32[2]{0:T(128)S(1)} %get-tuple-element.14, f32[256,512]{1,0:T(8,128)S(1)} %slice.65, f32[256,512]{1,0:T(8,128)S(1)} %multiply_add_fusion, ...), kind=kLoop, calls=%fused_computation.35 | loop fusion | flops 2621440 | bytes 2625552 | tf_op jit(solution)/shard_map/neg | solution.py:207
  162.2 3.9 %multiply_convert_fusion = (bf16[256,2,512]{2,0,1:T(8,128)(2,1)S(1)}, bf16[256,2,512]{2,0,1:T(8,128)(2,1)S(1)}) fusion(f32[2,512]{1,0:T(2,128)S(1)} %multiply_multiply_fusion, f32[2]{0:T(128)S(1)} %get-tuple-element.14, f32[256,512]{1,0:T(8,128)S(1)} %slice.65, f32[256,512]{1,0:T(8,128)S(1)} %multiply_add_fusion, f32[2]{0:T(128)S(1)} %broadcast_multiply_fusion), kind=kLoop, calls=%fused_computation.16 | loop fusion | flops 1835008 | bytes 2101264 | tf_op jit(solution)/shard_map/convert_element_type | solution.py:205
  166.1 0.7 fusion
  166.9 0.9 fusion.11
  167.7 16.9 %all_to_all.19 = bf16[2,2,256,256]{3,1,0,2:T(2,128)(2,1)S(1)} all-to-all(bf16[2,2,256,256]{3,1,0,2:T(2,128)(2,1)S(1)} %fusion.11), channel_id=1, replica_groups=mesh['stn'=16,'chan'=2] {'stn'}, dimensions={2} | all-to-all | bytes 1048576 | tf_op jit(solution)/shard_map/all_to_all | solution.py:265
  184.6 0.4 convert_bitcast_fusion
  185.1 1.2 copy.76
  (20 shorter events, 0.2 us)
Async XLA Ops:
  0.0 26.1 %collective-permute-start = (f32[1024,512]{1,0:T(8,128)}, f32[1024,512]{1,0:T(8,128)}, u32[]{:S(2)}, u32[]{:S(2)}) collective-permute-start(f32[1024,512]{1,0:T(8,128)} %bitcast.33), channel_id=1, source_target_pairs={{0,2},{2,0},{4,6},{6,4},{8,10},{10,8},{12,14},{14,12},{16,18},{18,... | collective-permute-start | bytes 6291464 | tf_op jit(solution)/shard_map/ppermute | solution.py:239
  5.7 10.3 %copy-start.6 = (f32[32]{0:T(128)S(1)}, f32[32]{0:T(128)}, u32[]{:S(2)}) copy-start(f32[32]{0:T(128)} %param.13) | copy-start | bytes 388
  5.7 10.4 %copy-start.3 = (f32[512]{0:T(512)S(1)}, f32[512]{0:T(512)}, u32[]{:S(2)}) copy-start(f32[512]{0:T(512)} %param.15) | copy-start | bytes 6148
  5.7 10.4 %copy-start.4 = (f32[512]{0:T(512)S(1)}, f32[512]{0:T(512)}, u32[]{:S(2)}) copy-start(f32[512]{0:T(512)} %param.14) | copy-start | bytes 6148
  5.7 10.5 %copy-start = (f32[2,512,512]{2,1,0:T(8,128)S(1)}, f32[2,512,512]{2,1,0:T(8,128)}, u32[]{:S(2)}) copy-start(f32[2,512,512]{2,1,0:T(8,128)} %param.8) | copy-start | bytes 6291460
  9.0 14.9 %all-to-all-start = ((f32[2,16,2,512]{3,2,0,1:T(2,128)}), f32[2,16,2,512]{3,2,0,1:T(2,128)S(1)}, u32[]{:S(2)}, u32[]{:S(2)}) async-start(f32[2,16,2,512]{3,2,0,1:T(2,128)} %copy.69), calls=%async_computation | async-start | bytes 262144 | tf_op jit(solution)/shard_map/all_to_all | solution.py:235
  16.2 1.8 copy-start.2
  61.8 51.3 %copy-start.1 = (s32[1,1,16,1024]{3,2,1,0:T(8,128)S(1)}, s32[1,1,16,1024]{3,2,1,0:T(8,128)}, u32[]{:S(2)}) copy-start(s32[1,1,16,1024]{3,2,1,0:T(8,128)} %param.10) | copy-start | bytes 196612
  61.8 51.9 %copy-start.5 = (f32[3,16]{1,0:T(4,128)S(1)}, f32[3,16]{1,0:T(4,128)}, u32[]{:S(2)}) copy-start(f32[3,16]{1,0:T(4,128)} %param.11) | copy-start | bytes 580
  67.2 52.8 %all-to-all-start.1 = ((f32[16,2,512]{2,1,0:T(2,128)}), f32[16,2,512]{2,1,0:T(2,128)S(1)}, u32[]{:S(2)}, u32[]{:S(2)}) async-start(f32[16,2,512]{2,1,0:T(2,128)} %copy.73), calls=%async_computation.1 | async-start | bytes 131072 | tf_op jit(solution)/shard_map/all_to_all | solution.py:241

commit v10 on v9

--- a/solution.py
+++ b/solution.py
@@ -26,6 +26,7 @@
 
 
 UNROLL = 32
+KBITS = 12
 
 
 def _interp_kernel(r_ref, c_ref, s_ref, o_ref):
@@ -94,7 +95,7 @@
     unroll = min(UNROLL, seg)
     sub = lax.broadcasted_iota(jnp.int32, (nb, 128), 0)
     lane = lax.broadcasted_iota(jnp.int32, (nb, 128), 1)
-    col = (sub * 128 + lane).astype(jnp.float32)
+    col = sub * 128 + lane
     rowid = lax.broadcasted_iota(jnp.int32, (8, 128), 0)
 
     for h, s_ref in enumerate((own_ref, partner_ref)):
@@ -105,17 +106,15 @@
                     first = (h * senders + s) * seg + g * unroll + part * 8
                     for u in range(8):
                         j = first + u
-                        r = r_ref[j]
+                        rk = r_ref[j]
+                        r = rk >> KBITS
+                        k = rk & ((1 << KBITS) - 1)
                         lower = s_ref[r]
                         upper = s_ref[r + 1]
-                        y = jnp.full((nb, 128), c_ref[0, j], jnp.float32) * (rows - 1)
-                        x = jnp.full((nb, 128), c_ref[1, j], jnp.float32) * (cols - 1)
-                        ry = jnp.clip(jnp.floor(y), 0.0, rows - 2.0)
-                        kx = jnp.clip(jnp.floor(x), 0.0, cols - 2.0)
-                        fy = y - ry
-                        fx = x - kx
+                        fy = c_ref[0, j]
+                        fx = c_ref[1, j]
                         blend = (1.0 - fy) * lower + fy * upper
-                        wx = jnp.where(col == kx, 1.0 - fx, jnp.where(col == kx + 1.0, fx, 0.0))
+                        wx = jnp.where(col == k, 1.0 - fx, jnp.where(col == k + 1, fx, 0.0))
                         row = jnp.sum(blend * wx, axis=0, keepdims=True)
                         acc = jnp.where(rowid == u, row, acc)
                     o_ref[pl.ds(pl.multiple_of(first, 8), 8), :] = jnp.sum(acc, axis=1, keepdims=True)
@@ -133,7 +132,12 @@
     nb = cols // 128
     _, halves, senders, seg = coords.shape
     flat = coords.reshape(2, halves * senders * seg)
-    r = jnp.clip(jnp.floor(flat[0] * (rows - 1)), 0.0, rows - 2.0).astype(jnp.int32)
+    y = flat[0] * (rows - 1)
+    x = flat[1] * (cols - 1)
+    r = jnp.clip(jnp.floor(y), 0.0, rows - 2.0)
+    k = jnp.clip(jnp.floor(x), 0.0, cols - 2.0)
+    rk = (r.astype(jnp.int32) << KBITS) | k.astype(jnp.int32)
+    frac = jnp.stack([y - r, x - k])
     spec = pl.BlockSpec((rows, nb, 128), lambda i, n, rr, cc: (0, 0, 0))
     out = pl.pallas_call(
         _balanced_kernel,
@@ -144,7 +148,7 @@
             out_specs=pl.BlockSpec((halves * senders * seg, 1), lambda i, n, rr, cc: (0, 0)),
         ),
         out_shape=jax.ShapeDtypeStruct((halves * senders * seg, 1), jnp.float32),
-    )(live, r, flat, own.reshape(rows, nb, 128), partner.reshape(rows, nb, 128))
+    )(live, rk, frac, own.reshape(rows, nb, 128), partner.reshape(rows, nb, 128))
     return out.reshape(halves, senders, seg)
 
 

time: 187 us -> 193 us (1.032)
  Pallas kernels: 45.1 us -> 93.3 us
  starting transfers between devices: 53.4 us -> 11.3 us
    pallas_call x1, Pallas kernels: 32.8 us -> 81 us  [interpolate_balanced(): pl.pallas_call(_balanced_kernel, grid_spec=pltpu.PrefetchScalarGridSpec(n...]
    all_to_all x1, starting transfers between devices: 45.9 us -> 3.49 us  [body(): lax.all_to_all(sampled, 'stn', split_axis=0, concat_axis=0, tiled=True)]
    unnamed x20 -> x21, local copies, waits for them, and re-layouts: 4.05 us -> 3.4 us
  transfers between devices with their start and end apart: 3 -> 3, of which waited for: 2 -> 2; matrix products, arithmetic and copies ran while one was open for 8% -> 3% of each run, Pallas kernels for 0% -> 0%
where the time goes in v10:
time: 193 us; the launch traced here: 192 us
  Pallas kernels  93.3 us (48%)
  blocking collectives  40.8 us (21%)
  other arithmetic  18.6 us (10%)
  local copies, waits for them, and re-layouts  16 us (8%)
  starting transfers between devices  11.3 us (6%)
  waiting for transfers between devices  10.9 us (6%)
    pallas_call x1, Pallas kernels, interpolate_balanced(): pl.pallas_call(_balanced_kernel, grid_spec=pltpu.PrefetchScalarGridSpec(n...  81 us
    all_gather x1, blocking collectives, body(): gathered = lax.all_gather(packed, 'stn', axis=0, tiled=True)  19.6 us
    all_to_all x1, blocking collectives, body(): lax.all_to_all(visible.astype(jnp.bfloat16), 'stn', split_axis=2, concat_...  16.9 us
    pallas_call x1, Pallas kernels, scatter_kernel(): pl.pallas_call(_scatter_kernel, grid_spec=pltpu.PrefetchScalarGridSpec(nu...  12.2 us
    all_to_all x1, starting transfers between devices, body(): lax.all_to_all(send, 'stn', split_axis=1, concat_axis=1, tiled=True)  7.39 us
    all_to_all x1, waiting for transfers between devices, body(): lax.all_to_all(send, 'stn', split_axis=1, concat_axis=1, tiled=True)  5.49 us
    all_to_all x1, waiting for transfers between devices, body(): lax.all_to_all(sampled, 'stn', split_axis=0, concat_axis=0, tiled=True)  5.4 us
    pallas_call x1, other arithmetic, interpolate_balanced(): pl.pallas_call(_balanced_kernel, grid_spec=pltpu.PrefetchScalarGridSpec(n...  4.65 us
  transfers between devices with their start and end apart: 3, of which 2 were waited for; matrix products, arithmetic and copies ran while one was open for 3% of the time, Pallas kernels for 0%

profile of v10, /device:TPU:0, one launch (start us, length us, event | category | flops | bytes accessed | tf_op | source)
XLA Modules:
  0.0 192.0 jit_solution(13762070141766568599)
XLA Ops:
  0.0 1.2 copy.71
  1.2 0.9 broadcast_compare_fusion
  2.1 0.3 copy.70
  2.4 0.2 ge.18
  2.6 0.7 broadcast_select_fusion
  3.3 1.6 fusion.15
  4.9 0.3 copy.72
  5.2 0.0 copy-start
  5.2 1.0 copy.73
  6.2 1.3 pad_maximum_fusion
  7.5 1.0 copy.74
  8.5 7.4 %all-to-all-start = ((f32[2,16,2,512]{3,2,0,1:T(2,128)}), f32[2,16,2,512]{3,2,0,1:T(2,128)S(1)}, u32[]{:S(2)}, u32[]{:S(2)}) async-start(f32[2,16,2,512]{3,2,0,1:T(2,128)} %copy.74), calls=%async_computation | async-start | bytes 262144 | tf_op jit(solution)/shard_map/all_to_all | solution.py:239
  15.9 0.5 collective-permute-start
  16.4 0.1 fusion.14
  16.4 0.1 multiply_multiply_fusion
  16.5 1.7 reshape_reshape_reshape.3.own_ref
  18.3 5.5 %all-to-all-done = f32[2,16,2,512]{3,2,0,1:T(2,128)S(1)} async-done(((f32[2,16,2,512]{3,2,0,1:T(2,128)}), f32[2,16,2,512]{3,2,0,1:T(2,128)S(1)}, u32[]{:S(2)}, u32[]{:S(2)}) %all-to-all-start) | async-done | bytes 131104 | tf_op jit(solution)/shard_map/all_to_all | solution.py:239
  23.8 0.1 copy.85
  23.9 0.1 copy.86
  24.0 0.1 clamp_subtract_fusion
  24.1 0.1 shift-left_or_fusion
  24.3 0.6 copy.84
  24.9 0.6 reshape.243.n_ref
  25.5 0.8 pad_maximum_fusion.1.c_ref
  26.3 2.9 %reshape.244.partner_ref = f32[1024,4,128]{2,1,0:T(4,128)} reshape(f32[1024,512]{1,0:T(8,128)} %collective-permute-done) | data formatting | bytes 4194304 | tf_op jit(solution)/shard_map/reshape | solution.py:151
  29.2 81.0 %shard_map.82 = f32[16384,1]{1,0:T(8,128)} custom-call(s32[32]{0:T(128)} %reshape.243.n_ref, s32[16384]{0:T(1024)} %bitcast.43, f32[2,16384]{1,0:T(2,128)} %pad_maximum_fusion.1.c_ref, f32[1024,4,128]{2,1,0:T(4,128)} %reshape_reshape_reshape.3.own_ref, f32[1024,4,128]{2,1,0:T(4,128)} %reshape.244.partner_ref), custom_call_target="tpu_custom_call" | custom-call | tf_op jit(solution)/shard_map/pallas_call | solution.py:142
  110.2 4.6 %reduce.2 = f32[16384]{0:T(1024)S(1)} reduce(f32[16384,1]{1,0:T(8,128)} %shard_map.82, f32[]{:T(128)} %constant.38), dimensions={1}, to_apply=%pallas_call.6.reduce_sub_computation | reduce | bytes 131076 | tf_op jit(solution)/shard_map/pallas_call | solution.py:142
  114.9 0.7 copy.78
  115.6 3.5 %all-to-all-start.1 = ((f32[16,2,512]{2,1,0:T(2,128)}), f32[16,2,512]{2,1,0:T(2,128)S(1)}, u32[]{:S(2)}, u32[]{:S(2)}) async-start(f32[16,2,512]{2,1,0:T(2,128)} %copy.78), calls=%async_computation.1 | async-start | bytes 131072 | tf_op jit(solution)/shard_map/all_to_all | solution.py:245
  119.1 0.6 copy.83
  119.8 0.1 copy.79
  119.8 0.7 convert_reduce_fusion.1.n_ref
  120.5 5.4 %all-to-all-done.1 = f32[16,2,512]{2,1,0:T(2,128)S(1)} async-done(((f32[16,2,512]{2,1,0:T(2,128)}), f32[16,2,512]{2,1,0:T(2,128)S(1)}, u32[]{:S(2)}, u32[]{:S(2)}) %all-to-all-start.1) | async-done | bytes 65568 | tf_op jit(solution)/shard_map/all_to_all | solution.py:245
  125.9 0.6 copy.87
  126.6 12.2 %shard_map.83 = f32[4097]{0:T(1024)} custom-call(s32[16]{0:T(128)} %convert_reduce_fusion.1.n_ref, s32[16384]{0:T(1024)} %bitcast.47, f32[16384]{0:T(1024)} %bitcast.48), custom_call_target="tpu_custom_call" | custom-call | tf_op jit(solution)/shard_map/pallas_call | solution.py:174
  138.8 0.7 slice.67
  139.5 4.4 %all_gather.6 = f32[16,512]{1,0:T(8,128)S(1)} all-gather(f32[16,256]{1,0:T(8,128)S(1)} %reshape.247), channel_id=1, replica_groups=mesh['stn'=16,'chan'=2] {'chan'}, dimensions={1}, use_global_device_ids=true | all-gather | bytes 49152 | tf_op jit(solution)/shard_map/all_gather | solution.py:254
  143.9 19.6 %all_gather.7 = f32[256,515]{1,0:T(8,128)S(1)} all-gather(f32[16,515]{1,0:T(8,128)S(1)} %pad_maximum_fusion.2), channel_id=1, replica_groups=mesh['stn'=16,'chan'=2] {'stn'}, dimensions={0}, use_global_device_ids=true | all-gather | bytes 560320 | tf_op jit(solution)/shard_map/all_gather | solution.py:256
  163.5 0.3 slice_reduce_fusion.2
  163.8 0.1 slice.71
  163.8 0.2 multiply_add_fusion
  164.0 3.9 %multiply_convert_fusion = (bf16[256,2,512]{2,0,1:T(8,128)(2,1)S(1)}, bf16[256,2,512]{2,0,1:T(8,128)(2,1)S(1)}) fusion(f32[2,512]{1,0:T(2,128)S(1)} %multiply_multiply_fusion, f32[2]{0:T(128)S(1)} %get-tuple-element.14, f32[256,512]{1,0:T(8,128)S(1)} %slice.71, f32[256,512]{1,0:T(8,128)S(1)} %multiply_add_fusion, f32[2]{0:T(128)S(1)} %broadcast_multiply_fusion), kind=kLoop, calls=%fused_computation.16 | loop fusion | flops 1835008 | bytes 2101264 | tf_op jit(solution)/shard_map/convert_element_type | solution.py:209
  167.9 3.9 %fusion.13 = (bf16[256,2,512]{2,0,1:T(8,128)(2,1)S(1)}, bf16[256,2,512]{2,0,1:T(8,128)(2,1)S(1)}, bf16[256,2,512]{2,0,1:T(8,128)(2,1)S(1)}) fusion(f32[2,512]{1,0:T(2,128)S(1)} %multiply_multiply_fusion, f32[2]{0:T(128)S(1)} %get-tuple-element.14, f32[256,512]{1,0:T(8,128)S(1)} %slice.71, f32[256,512]{1,0:T(8,128)S(1)} %multiply_add_fusion, ...), kind=kLoop, calls=%fused_computation.40 | loop fusion | flops 2621440 | bytes 2625552 | tf_op jit(solution)/shard_map/neg | solution.py:211
  171.9 0.7 fusion
  172.6 0.9 fusion.11
  173.5 16.9 %all_to_all.19 = bf16[2,2,256,256]{3,1,0,2:T(2,128)(2,1)S(1)} all-to-all(bf16[2,2,256,256]{3,1,0,2:T(2,128)(2,1)S(1)} %fusion.11), channel_id=1, replica_groups=mesh['stn'=16,'chan'=2] {'stn'}, dimensions={2} | all-to-all | bytes 1048576 | tf_op jit(solution)/shard_map/all_to_all | solution.py:269
  190.4 0.4 convert_bitcast_fusion
  190.8 1.2 copy.81
  (23 shorter events, 0.2 us)
Async XLA Ops:
  5.2 10.7 %copy-start = (f32[2,512,512]{2,1,0:T(8,128)S(1)}, f32[2,512,512]{2,1,0:T(8,128)}, u32[]{:S(2)}) copy-start(f32[2,512,512]{2,1,0:T(8,128)} %param.8) | copy-start | bytes 6291460
  5.2 11.2 %copy-start.6 = (f32[32]{0:T(128)S(1)}, f32[32]{0:T(128)}, u32[]{:S(2)}) copy-start(f32[32]{0:T(128)} %param.13) | copy-start | bytes 388
  5.2 11.2 %copy-start.3 = (f32[512]{0:T(512)S(1)}, f32[512]{0:T(512)}, u32[]{:S(2)}) copy-start(f32[512]{0:T(512)} %param.15) | copy-start | bytes 6148
  5.2 11.2 %copy-start.4 = (f32[512]{0:T(512)S(1)}, f32[512]{0:T(512)}, u32[]{:S(2)}) copy-start(f32[512]{0:T(512)} %param.14) | copy-start | bytes 6148
  8.5 15.3 %all-to-all-start = ((f32[2,16,2,512]{3,2,0,1:T(2,128)}), f32[2,16,2,512]{3,2,0,1:T(2,128)S(1)}, u32[]{:S(2)}, u32[]{:S(2)}) async-start(f32[2,16,2,512]{3,2,0,1:T(2,128)} %copy.74), calls=%async_computation | async-start | bytes 262144 | tf_op jit(solution)/shard_map/all_to_all | solution.py:239
  15.9 10.4 %collective-permute-start = (f32[1024,512]{1,0:T(8,128)S(1)}, f32[1024,512]{1,0:T(8,128)}, u32[]{:S(2)}, u32[]{:S(2)}) collective-permute-start(f32[1024,512]{1,0:T(8,128)S(1)} %bitcast.37), channel_id=1, source_target_pairs={{0,2},{2,0},{4,6},{6,4},{8,10},{10,8},{12,14},{14,12},{16,18},{18,... | collective-permute-start | bytes 6291464 | tf_op jit(solution)/shard_map/ppermute | solution.py:243
  16.5 1.7 copy-start.2
  110.2 8.9 %copy-start.1 = (s32[1,1,16,1024]{3,2,1,0:T(8,128)S(1)}, s32[1,1,16,1024]{3,2,1,0:T(8,128)}, u32[]{:S(2)}) copy-start(s32[1,1,16,1024]{3,2,1,0:T(8,128)} %param.10) | copy-start | bytes 196612
  110.2 9.5 %copy-start.5 = (f32[3,16]{1,0:T(4,128)S(1)}, f32[3,16]{1,0:T(4,128)}, u32[]{:S(2)}) copy-start(f32[3,16]{1,0:T(4,128)} %param.11) | copy-start | bytes 580
  115.6 10.4 %all-to-all-start.1 = ((f32[16,2,512]{2,1,0:T(2,128)}), f32[16,2,512]{2,1,0:T(2,128)S(1)}, u32[]{:S(2)}, u32[]{:S(2)}) async-start(f32[16,2,512]{2,1,0:T(2,128)} %copy.78), calls=%async_computation.1 | async-start | bytes 131072 | tf_op jit(solution)/shard_map/all_to_all | solution.py:245

commit v11 on v10

--- a/solution.py
+++ b/solution.py
@@ -128,8 +128,8 @@
 
 
 def interpolate_balanced(own, partner, coords, live):
-    rows, cols = own.shape
-    nb = cols // 128
+    rows, nb, _ = own.shape
+    cols = nb * 128
     _, halves, senders, seg = coords.shape
     flat = coords.reshape(2, halves * senders * seg)
     y = flat[0] * (rows - 1)
@@ -148,7 +148,7 @@
             out_specs=pl.BlockSpec((halves * senders * seg, 1), lambda i, n, rr, cc: (0, 0)),
         ),
         out_shape=jax.ShapeDtypeStruct((halves * senders * seg, 1), jnp.float32),
-    )(live, rk, frac, own.reshape(rows, nb, 128), partner.reshape(rows, nb, 128))
+    )(live, rk, frac, own, partner)
     return out.reshape(halves, senders, seg)
 
 
@@ -239,9 +239,9 @@
     received = lax.all_to_all(send, "stn", split_axis=1, concat_axis=1, tiled=True)
     kin = received.transpose(0, 2, 1, 3)
     live = jnp.sum((kin[0] >= 0.0).astype(jnp.int32), axis=2).reshape(-1)
-    screen2d = values.reshape(strip_rows, tile_cols)
-    partner = lax.ppermute(screen2d, "stn", [(i, i ^ 1) for i in range(groups)])
-    sampled = interpolate_balanced(screen2d, partner, kin, live).transpose(1, 0, 2)
+    own = screen.reshape(strip_rows, tile_cols // 128, 128)
+    partner = lax.ppermute(own, "stn", [(i, i ^ 1) for i in range(groups)])
+    sampled = interpolate_balanced(own, partner, kin, live).transpose(1, 0, 2)
     back = lax.all_to_all(sampled, "stn", split_axis=0, concat_axis=0, tiled=True)
     buffer = scatter_kernel(query_dest.reshape(groups, capacity), back, queries + 1)
     own_iono = buffer[:queries].reshape(stations_local, local_sources)

time: 193 us -> 185 us (0.959)
  Pallas kernels: 93.3 us -> 46.3 us
  starting transfers between devices: 11.3 us -> 57.3 us
  local copies, waits for them, and re-layouts: 16 us -> 11.7 us
    pallas_call x1, Pallas kernels: 81 us -> 34.1 us  [interpolate_balanced(): pl.pallas_call(_balanced_kernel, grid_spec=pltpu.PrefetchScalarGridSpec(n...]
    all_to_all x1, starting transfers between devices: 3.49 us -> 49.4 us  [body(): lax.all_to_all(sampled, 'stn', split_axis=0, concat_axis=0, tiled=True)]
where the time goes in v11:
time: 185 us
  starting transfers between devices  57.3 us (31%)
  Pallas kernels  46.3 us (25%)
  blocking collectives  40.9 us (22%)
  other arithmetic  17.4 us (9%)
  local copies, waits for them, and re-layouts  11.7 us (6%)
  waiting for transfers between devices  10.7 us (6%)
    all_to_all x1, starting transfers between devices, body(): lax.all_to_all(sampled, 'stn', split_axis=0, concat_axis=0, tiled=True)  49.4 us
    pallas_call x1, Pallas kernels, interpolate_balanced(): pl.pallas_call(_balanced_kernel, grid_spec=pltpu.PrefetchScalarGridSpec(n...  34.1 us
    all_gather x1, blocking collectives, body(): gathered = lax.all_gather(packed, 'stn', axis=0, tiled=True)  19.6 us
    all_to_all x1, blocking collectives, body(): lax.all_to_all(visible.astype(jnp.bfloat16), 'stn', split_axis=2, concat_...  16.9 us
    pallas_call x1, Pallas kernels, scatter_kernel(): pl.pallas_call(_scatter_kernel, grid_spec=pltpu.PrefetchScalarGridSpec(nu...  12.3 us
    all_to_all x1, starting transfers between devices, body(): lax.all_to_all(send, 'stn', split_axis=1, concat_axis=1, tiled=True)  7.39 us
    all_to_all x1, waiting for transfers between devices, body(): lax.all_to_all(sampled, 'stn', split_axis=0, concat_axis=0, tiled=True)  5.44 us
    all_to_all x1, waiting for transfers between devices, body(): lax.all_to_all(send, 'stn', split_axis=1, concat_axis=1, tiled=True)  5.22 us
  transfers between devices with their start and end apart: 3, of which 2 were waited for; matrix products, arithmetic and copies ran while one was open for 3% of the time, Pallas kernels for 0%

profile of v11, /device:TPU:0, one launch (start us, length us, event | category | flops | bytes accessed | tf_op | source)
XLA Modules:
  0.0 185.4 jit_solution(1887439352509184217)
XLA Ops:
  0.0 1.2 copy.71
  1.2 0.9 broadcast_compare_fusion
  2.1 0.3 copy.70
  2.4 0.2 ge.18
  2.6 0.7 broadcast_select_fusion
  3.3 0.8 fusion.15
  4.1 0.3 copy.72
  4.4 0.2 copy.73
  4.6 0.1 pad_maximum_fusion
  4.7 1.0 copy.74
  5.7 7.4 %all-to-all-start = ((f32[2,16,2,512]{3,2,0,1:T(2,128)}), f32[2,16,2,512]{3,2,0,1:T(2,128)S(1)}, u32[]{:S(2)}, u32[]{:S(2)}) async-start(f32[2,16,2,512]{3,2,0,1:T(2,128)} %copy.74), calls=%async_computation | async-start | bytes 262144 | tf_op jit(solution)/shard_map/all_to_all | solution.py:239
  13.1 0.0 copy-start.4
  13.1 0.0 copy-start.2
  13.1 1.9 %reshape.244.own_ref = f32[1024,4,128]{2,1,0:T(4,128)S(1)} reshape(f32[2,512,512]{2,1,0:T(8,128)} %param.8) | data formatting | bytes 4194304 | tf_op jit(solution)/shard_map/reshape | solution.py:242
  15.1 0.5 collective-permute-start
  15.5 0.1 fusion.14
  15.6 0.1 multiply_multiply_fusion
  15.7 5.2 %all-to-all-done = f32[2,16,2,512]{3,2,0,1:T(2,128)S(1)} async-done(((f32[2,16,2,512]{3,2,0,1:T(2,128)}), f32[2,16,2,512]{3,2,0,1:T(2,128)S(1)}, u32[]{:S(2)}, u32[]{:S(2)}) %all-to-all-start) | async-done | bytes 131104 | tf_op jit(solution)/shard_map/all_to_all | solution.py:239
  21.0 0.1 copy.85
  21.1 0.1 copy.86
  21.2 0.1 clamp_subtract_fusion
  21.3 0.1 shift-left_or_fusion
  21.5 0.6 copy.84
  22.1 0.6 reshape.243.n_ref
  22.7 0.8 pad_maximum_fusion.1.c_ref
  23.5 34.1 %shard_map.82 = f32[16384,1]{1,0:T(8,128)} custom-call(s32[32]{0:T(128)} %reshape.243.n_ref, s32[16384]{0:T(1024)} %bitcast.41, f32[2,16384]{1,0:T(2,128)} %pad_maximum_fusion.1.c_ref, f32[1024,4,128]{2,1,0:T(4,128)} %copy-done, f32[1024,4,128]{2,1,0:T(4,128)} %collective-permute-done.partner_ref), custom_call_target="tpu_custom_call" | custom-call | tf_op jit(solution)/shard_map/pallas_call | solution.py:142
  57.6 4.6 %reduce.2 = f32[16384]{0:T(1024)S(1)} reduce(f32[16384,1]{1,0:T(8,128)} %shard_map.82, f32[]{:T(128)} %constant.38), dimensions={1}, to_apply=%pallas_call.6.reduce_sub_computation | reduce | bytes 131076 | tf_op jit(solution)/shard_map/pallas_call | solution.py:142
  62.2 0.7 copy.78
  62.9 49.4 %all-to-all-start.1 = ((f32[16,2,512]{2,1,0:T(2,128)}), f32[16,2,512]{2,1,0:T(2,128)S(1)}, u32[]{:S(2)}, u32[]{:S(2)}) async-start(f32[16,2,512]{2,1,0:T(2,128)} %copy.78), calls=%async_computation.1 | async-start | bytes 131072 | tf_op jit(solution)/shard_map/all_to_all | solution.py:245
  112.4 0.6 copy.83
  113.0 0.1 copy.79
  113.1 0.7 convert_reduce_fusion.1.n_ref
  113.8 5.4 %all-to-all-done.1 = f32[16,2,512]{2,1,0:T(2,128)S(1)} async-done(((f32[16,2,512]{2,1,0:T(2,128)}), f32[16,2,512]{2,1,0:T(2,128)S(1)}, u32[]{:S(2)}, u32[]{:S(2)}) %all-to-all-start.1) | async-done | bytes 65568 | tf_op jit(solution)/shard_map/all_to_all | solution.py:245
  119.2 0.6 copy.87
  119.9 12.3 %shard_map.83 = f32[4097]{0:T(1024)} custom-call(s32[16]{0:T(128)} %convert_reduce_fusion.1.n_ref, s32[16384]{0:T(1024)} %bitcast.45, f32[16384]{0:T(1024)} %bitcast.46), custom_call_target="tpu_custom_call" | custom-call | tf_op jit(solution)/shard_map/pallas_call | solution.py:174
  132.2 0.7 slice.67
  132.9 4.4 %all_gather.6 = f32[16,512]{1,0:T(8,128)S(1)} all-gather(f32[16,256]{1,0:T(8,128)S(1)} %reshape.247), channel_id=1, replica_groups=mesh['stn'=16,'chan'=2] {'chan'}, dimensions={1}, use_global_device_ids=true | all-gather | bytes 49152 | tf_op jit(solution)/shard_map/all_gather | solution.py:254
  137.3 19.6 %all_gather.7 = f32[256,515]{1,0:T(8,128)S(1)} all-gather(f32[16,515]{1,0:T(8,128)S(1)} %pad_maximum_fusion.2), channel_id=1, replica_groups=mesh['stn'=16,'chan'=2] {'stn'}, dimensions={0}, use_global_device_ids=true | all-gather | bytes 560320 | tf_op jit(solution)/shard_map/all_gather | solution.py:256
  156.9 0.3 slice_reduce_fusion.2
  157.2 0.1 slice.71
  157.2 0.2 multiply_add_fusion
  157.4 3.9 %multiply_convert_fusion = (bf16[256,2,512]{2,0,1:T(8,128)(2,1)S(1)}, bf16[256,2,512]{2,0,1:T(8,128)(2,1)S(1)}) fusion(f32[2,512]{1,0:T(2,128)S(1)} %multiply_multiply_fusion, f32[2]{0:T(128)S(1)} %get-tuple-element.14, f32[256,512]{1,0:T(8,128)S(1)} %slice.71, f32[256,512]{1,0:T(8,128)S(1)} %multiply_add_fusion, f32[2]{0:T(128)S(1)} %broadcast_multiply_fusion), kind=kLoop, calls=%fused_computation.16 | loop fusion | flops 1835008 | bytes 2101264 | tf_op jit(solution)/shard_map/convert_element_type | solution.py:209
  161.3 3.9 %fusion.13 = (bf16[256,2,512]{2,0,1:T(8,128)(2,1)S(1)}, bf16[256,2,512]{2,0,1:T(8,128)(2,1)S(1)}, bf16[256,2,512]{2,0,1:T(8,128)(2,1)S(1)}) fusion(f32[2,512]{1,0:T(2,128)S(1)} %multiply_multiply_fusion, f32[2]{0:T(128)S(1)} %get-tuple-element.14, f32[256,512]{1,0:T(8,128)S(1)} %slice.71, f32[256,512]{1,0:T(8,128)S(1)} %multiply_add_fusion, ...), kind=kLoop, calls=%fused_computation.40 | loop fusion | flops 2621440 | bytes 2625552 | tf_op jit(solution)/shard_map/neg | solution.py:211
  165.3 0.7 fusion
  166.0 0.9 fusion.11
  166.9 16.9 %all_to_all.19 = bf16[2,2,256,256]{3,1,0,2:T(2,128)(2,1)S(1)} all-to-all(bf16[2,2,256,256]{3,1,0,2:T(2,128)(2,1)S(1)} %fusion.11), channel_id=1, replica_groups=mesh['stn'=16,'chan'=2] {'stn'}, dimensions={2} | all-to-all | bytes 1048576 | tf_op jit(solution)/shard_map/all_to_all | solution.py:269
  183.8 0.4 convert_bitcast_fusion
  184.2 1.2 copy.81
  (22 shorter events, 0.2 us)
Async XLA Ops:
  5.7 15.3 %all-to-all-start = ((f32[2,16,2,512]{3,2,0,1:T(2,128)}), f32[2,16,2,512]{3,2,0,1:T(2,128)S(1)}, u32[]{:S(2)}, u32[]{:S(2)}) async-start(f32[2,16,2,512]{3,2,0,1:T(2,128)} %copy.74), calls=%async_computation | async-start | bytes 262144 | tf_op jit(solution)/shard_map/all_to_all | solution.py:239
  13.1 2.5 %copy-start.6 = (f32[32]{0:T(128)S(1)}, f32[32]{0:T(128)}, u32[]{:S(2)}) copy-start(f32[32]{0:T(128)} %param.13) | copy-start | bytes 388
  13.1 2.6 %copy-start.3 = (f32[512]{0:T(512)S(1)}, f32[512]{0:T(512)}, u32[]{:S(2)}) copy-start(f32[512]{0:T(512)} %param.15) | copy-start | bytes 6148
  13.1 2.5 %copy-start.4 = (f32[512]{0:T(512)S(1)}, f32[512]{0:T(512)}, u32[]{:S(2)}) copy-start(f32[512]{0:T(512)} %param.14) | copy-start | bytes 6148
  13.1 2.6 %copy-start.2 = (f32[3,512]{1,0:T(4,128)S(1)}, f32[3,512]{1,0:T(4,128)}, u32[]{:S(2)}) copy-start(f32[3,512]{1,0:T(4,128)} %param.12) | copy-start | bytes 18436
  15.1 8.4 %copy-start = (f32[1024,4,128]{2,1,0:T(4,128)}, f32[1024,4,128]{2,1,0:T(4,128)S(1)}, u32[]{:S(2)}) copy-start(f32[1024,4,128]{2,1,0:T(4,128)S(1)} %reshape.244.own_ref) | copy-start | bytes 6291460
  15.1 8.4 %collective-permute-start = (f32[1024,4,128]{2,1,0:T(4,128)S(1)}, f32[1024,4,128]{2,1,0:T(4,128)}, u32[]{:S(2)}, u32[]{:S(2)}) collective-permute-start(f32[1024,4,128]{2,1,0:T(4,128)S(1)} %reshape.244.own_ref), channel_id=1, source_target_pairs={{0,2},{2,0},{4,6},{6,4},{8,10},{10,8},{12,14},{14,12},{16,18},{18,... | collective-permute-start | bytes 6291464 | tf_op jit(solution)/shard_map/ppermute | solution.py:243
  57.5 54.8 %copy-start.1 = (s32[1,1,16,1024]{3,2,1,0:T(8,128)S(1)}, s32[1,1,16,1024]{3,2,1,0:T(8,128)}, u32[]{:S(2)}) copy-start(s32[1,1,16,1024]{3,2,1,0:T(8,128)} %param.10) | copy-start | bytes 196612
  57.6 55.5 %copy-start.5 = (f32[3,16]{1,0:T(4,128)S(1)}, f32[3,16]{1,0:T(4,128)}, u32[]{:S(2)}) copy-start(f32[3,16]{1,0:T(4,128)} %param.11) | copy-start | bytes 580
  62.9 56.4 %all-to-all-start.1 = ((f32[16,2,512]{2,1,0:T(2,128)}), f32[16,2,512]{2,1,0:T(2,128)S(1)}, u32[]{:S(2)}, u32[]{:S(2)}) async-start(f32[16,2,512]{2,1,0:T(2,128)} %copy.78), calls=%async_computation.1 | async-start | bytes 131072 | tf_op jit(solution)/shard_map/all_to_all | solution.py:245

commit v12 on v11

--- a/solution.py
+++ b/solution.py
@@ -1,3 +1,4 @@
+import functools
 import math
 
 import jax
@@ -86,26 +87,30 @@
     return out[:, 0]
 
 
-def _balanced_kernel(n_ref, r_ref, c_ref, own_ref, partner_ref, o_ref):
-    rows = own_ref.shape[0]
-    nb = own_ref.shape[1]
-    cols = nb * 128
-    senders = n_ref.shape[0] // 2
-    seg = o_ref.shape[0] // (2 * senders)
+def _balanced_kernel(first_part, n_ref, r_ref, c_ref, *refs):
+    screens, o_ref = refs[:-1], refs[-1]
+    rows = screens[0].shape[0]
+    nb = screens[0].shape[1]
+    parts_here = len(screens)
+    seg = SEG[0]
+    senders = o_ref.shape[0] // (parts_here * seg)
     unroll = min(UNROLL, seg)
     sub = lax.broadcasted_iota(jnp.int32, (nb, 128), 0)
     lane = lax.broadcasted_iota(jnp.int32, (nb, 128), 1)
     col = sub * 128 + lane
     rowid = lax.broadcasted_iota(jnp.int32, (8, 128), 0)
 
-    for h, s_ref in enumerate((own_ref, partner_ref)):
-        def segment(s, carry, h=h, s_ref=s_ref):
+    for h, s_ref in enumerate(screens):
+        part = first_part + h
+
+        def segment(s, carry, h=h, part=part, s_ref=s_ref):
             def group(g, carry2):
-                for part in range(unroll // 8):
+                for piece in range(unroll // 8):
                     acc = jnp.zeros((8, 128), jnp.float32)
-                    first = (h * senders + s) * seg + g * unroll + part * 8
+                    local = (h * senders + s) * seg + g * unroll + piece * 8
+                    start = (part * senders + s) * seg + g * unroll + piece * 8
                     for u in range(8):
-                        j = first + u
+                        j = start + u
                         rk = r_ref[j]
                         r = rk >> KBITS
                         k = rk & ((1 << KBITS) - 1)
@@ -117,21 +122,25 @@
                         wx = jnp.where(col == k, 1.0 - fx, jnp.where(col == k + 1, fx, 0.0))
                         row = jnp.sum(blend * wx, axis=0, keepdims=True)
                         acc = jnp.where(rowid == u, row, acc)
-                    o_ref[pl.ds(pl.multiple_of(first, 8), 8), :] = jnp.sum(acc, axis=1, keepdims=True)
+                    o_ref[pl.ds(pl.multiple_of(local, 8), 8), :] = jnp.sum(acc, axis=1, keepdims=True)
                 return carry2
 
-            trips = (n_ref[h * senders + s] + unroll - 1) // unroll
+            trips = (n_ref[part * senders + s] + unroll - 1) // unroll
             lax.fori_loop(0, trips, group, 0)
             return carry
 
         lax.fori_loop(0, senders, segment, 0)
 
 
-def interpolate_balanced(own, partner, coords, live):
-    rows, nb, _ = own.shape
+SEG = [0]
+
+
+def interpolate_parts(screens, coords, live, split):
+    rows, nb, _ = screens[0].shape
     cols = nb * 128
-    _, halves, senders, seg = coords.shape
-    flat = coords.reshape(2, halves * senders * seg)
+    _, parts, senders, seg = coords.shape
+    SEG[0] = seg
+    flat = coords.reshape(2, parts * senders * seg)
     y = flat[0] * (rows - 1)
     x = flat[1] * (cols - 1)
     r = jnp.clip(jnp.floor(y), 0.0, rows - 2.0)
@@ -139,30 +148,40 @@
     rk = (r.astype(jnp.int32) << KBITS) | k.astype(jnp.int32)
     frac = jnp.stack([y - r, x - k])
     spec = pl.BlockSpec((rows, nb, 128), lambda i, n, rr, cc: (0, 0, 0))
-    out = pl.pallas_call(
-        _balanced_kernel,
-        grid_spec=pltpu.PrefetchScalarGridSpec(
-            num_scalar_prefetch=3,
-            grid=(1,),
-            in_specs=[spec, spec],
-            out_specs=pl.BlockSpec((halves * senders * seg, 1), lambda i, n, rr, cc: (0, 0)),
-        ),
-        out_shape=jax.ShapeDtypeStruct((halves * senders * seg, 1), jnp.float32),
-    )(live, rk, frac, own, partner)
-    return out.reshape(halves, senders, seg)
+    outs = []
+    for lo, hi in ((0, split), (split, parts)):
+        if lo == hi:
+            continue
+        size = (hi - lo) * senders * seg
+        out = pl.pallas_call(
+            functools.partial(_balanced_kernel, lo),
+            grid_spec=pltpu.PrefetchScalarGridSpec(
+                num_scalar_prefetch=3,
+                grid=(1,),
+                in_specs=[spec] * (hi - lo),
+                out_specs=pl.BlockSpec((size, 1), lambda i, n, rr, cc: (0, 0)),
+            ),
+            out_shape=jax.ShapeDtypeStruct((size, 1), jnp.float32),
+        )(live, rk, frac, *screens[lo:hi])
+        outs.append(out)
+    return jnp.concatenate(outs, axis=0).reshape(parts, senders, seg)
+
+
+PARTS = [2]
 
 
 def _scatter_kernel(n_ref, d_ref, v_ref, o_ref):
     rows = n_ref.shape[0]
     width = d_ref.shape[0] // rows
-    half = width // 2
-    step = 8 if width % 8 == 0 else 2
+    parts = PARTS[0]
+    part_len = width // parts
+    step = 8 if width % 8 == 0 else parts
     for row in range(rows):
         def body(i, carry, row=row):
             for u in range(step):
                 slot = row * width + i * step + u
-                parity = u % 2
-                source = ((row ^ parity) * 2 + parity) * half + i * (step // 2) + u // 2
+                q = u % parts
+                source = ((row ^ q) * parts + q) * part_len + i * (step // parts) + u // parts
                 o_ref[d_ref[slot]] = v_ref[source]
             return carry
 
@@ -230,19 +249,27 @@
     stations_local = positions.shape[1]
     local_sources = source_flux.shape[0] // lax.axis_size("chan")
     queries = stations_local * local_sources
-    half = capacity // 2
+    parts = 4 if groups % 4 == 0 and capacity % (4 * 8) == 0 else 2
+    part_len = capacity // parts
     coords = pierce_coords.reshape(2, groups, capacity)
     dead = query_dest.reshape(groups, capacity) >= queries
-    coords = jnp.where(dead[None], -1.0, coords).reshape(2, groups, half, 2)
-    swap = lambda a: a.reshape(a.shape[0], groups // 2, 2, half)[:, :, ::-1, :].reshape(a.shape[0], groups, half)
-    send = jnp.stack([coords[..., 0], swap(coords[..., 1])], axis=2)
+    coords = jnp.where(dead[None], -1.0, coords).reshape(2, groups // parts, parts, part_len, parts)
+
+    def to_dest(q):
+        piece = coords[..., q]
+        return jnp.stack([piece[:, :, d ^ q, :] for d in range(parts)], axis=2)
+
+    send = jnp.stack([to_dest(q) for q in range(parts)], axis=3).reshape(2, groups, parts, part_len)
     received = lax.all_to_all(send, "stn", split_axis=1, concat_axis=1, tiled=True)
     kin = received.transpose(0, 2, 1, 3)
     live = jnp.sum((kin[0] >= 0.0).astype(jnp.int32), axis=2).reshape(-1)
     own = screen.reshape(strip_rows, tile_cols // 128, 128)
-    partner = lax.ppermute(own, "stn", [(i, i ^ 1) for i in range(groups)])
-    sampled = interpolate_balanced(own, partner, kin, live).transpose(1, 0, 2)
+    screens = [own] + [
+        lax.ppermute(own, "stn", [(i, i ^ q) for i in range(groups)]) for q in range(1, parts)
+    ]
+    sampled = interpolate_parts(screens, kin, live, 2).transpose(1, 0, 2)
     back = lax.all_to_all(sampled, "stn", split_axis=0, concat_axis=0, tiled=True)
+    PARTS[0] = parts
     buffer = scatter_kernel(query_dest.reshape(groups, capacity), back, queries + 1)
     own_iono = buffer[:queries].reshape(stations_local, local_sources)
     station_rows = positions.T

time: 185 us -> 251 us (1.36)
  waiting for transfers between devices: 10.7 us -> 68.8 us
  starting transfers between devices: 57.3 us -> 12.8 us
  Pallas kernels: 46.3 us -> 75.8 us
  local copies, waits for them, and re-layouts: 11.7 us -> 33.3 us
  other arithmetic: 17.4 us -> 14.1 us
    all_to_all x1, waiting for transfers between devices: 5.22 us -> 63.3 us  [body(): lax.all_to_all(send, 'stn', split_axis=1, concat_axis=1, tiled=True)]
    all_to_all x1, starting transfers between devices: 49.4 us -> 3.5 us  [body(): lax.all_to_all(sampled, 'stn', split_axis=0, concat_axis=0, tiled=True)]
    pallas_call x1 -> x2, Pallas kernels: 34.1 us -> 63.5 us  [interpolate_parts(): pl.pallas_call(functools.partial(_balanced_kernel, lo), grid_spec=pltpu.P...]
    slice x2 -> x4, local copies, waits for them, and re-layouts: 1.08 us -> 11.1 us  [the longest x2 11.1 us: to_dest(): piece = coords[..., q]]
    pallas_call x0 -> x2, local copies, waits for them, and re-layouts: none -> 5.68 us  [interpolate_parts(): pl.pallas_call(functools.partial(_balanced_kernel, lo), grid_spec=pltpu.P...]
    reshape x1 -> x2, local copies, waits for them, and re-layouts: 0.01 us -> 5.64 us  [the longest x1 5.62 us: body(): coords = pierce_coords.reshape(2, groups, capacity)]
    pallas_call x1 -> x0, other arithmetic: 4.65 us -> none  [interpolate_balanced(): pl.pallas_call(_balanced_kernel, grid_spec=pltpu.PrefetchScalarGridSpec(n...]
    ppermute x1 -> x3, starting transfers between devices: 0.47 us -> 3.15 us  [body(): lax.ppermute(own, 'stn', [(i, i ^ q) for i in range(groups)])]
  transfers between devices with their start and end apart: 3 -> 5, of which waited for: 2 -> 2; matrix products, arithmetic and copies ran while one was open for 3% -> 12% of each run, Pallas kernels for 0% -> 17%
where the time goes in v12:
time: 251 us; the launch traced here: 249 us
  Pallas kernels  75.8 us (30%)
  waiting for transfers between devices  68.8 us (27%)
  blocking collectives  43.4 us (17%)
  local copies, waits for them, and re-layouts  33.3 us (13%)
  other arithmetic  14.1 us (6%)
  starting transfers between devices  12.8 us (5%)
    pallas_call x2, Pallas kernels, interpolate_parts(): pl.pallas_call(functools.partial(_balanced_kernel, lo), grid_spec=pltpu.P...  63.5 us
    all_to_all x1, waiting for transfers between devices, body(): lax.all_to_all(send, 'stn', split_axis=1, concat_axis=1, tiled=True)  63.3 us
    all_gather x1, blocking collectives, body(): gathered = lax.all_gather(packed, 'stn', axis=0, tiled=True)  19.5 us
    all_to_all x1, blocking collectives, body(): lax.all_to_all(visible.astype(jnp.bfloat16), 'stn', split_axis=2, concat_...  17.1 us
    pallas_call x1, Pallas kernels, scatter_kernel(): pl.pallas_call(_scatter_kernel, grid_spec=pltpu.PrefetchScalarGridSpec(nu...  12.3 us
    slice x2, local copies, waits for them, and re-layouts, to_dest(): piece = coords[..., q]  11.1 us
    all_gather x1, blocking collectives, body(): iono_phase = lax.all_gather(own_iono, 'chan', axis=1, tiled=True)  6.84 us
    all_to_all x1, starting transfers between devices, body(): lax.all_to_all(send, 'stn', split_axis=1, concat_axis=1, tiled=True)  6.16 us
  transfers between devices with their start and end apart: 5, of which 2 were waited for; matrix products, arithmetic and copies ran while one was open for 12% of the time, Pallas kernels for 17%

profile of v12, /device:TPU:0, one launch (start us, length us, event | category | flops | bytes accessed | tf_op | source)
XLA Modules:
  0.0 249.3 jit_solution(4663242717410976073)
XLA Ops:
  0.0 2.0 reshape.254.refs_0_
  2.0 0.6 collective-permute-start
  2.6 2.6 %collective-permute-start.1 = (f32[1024,4,128]{2,1,0:T(4,128)S(1)}, f32[1024,4,128]{2,1,0:T(4,128)}, u32[]{:S(2)}, u32[]{:S(2)}) collective-permute-start(f32[1024,4,128]{2,1,0:T(4,128)S(1)} %reshape.254.refs_0_), channel_id=1, source_target_pairs={{0,4},{2,6},{4,0},{6,2},{8,12},{10,14},{12,8},{14,10},{16,20},{18,... | collective-permute-start | bytes 6291464 | tf_op jit(solution)/shard_map/ppermute | solution.py:268
  5.1 5.6 %reshape.252 = f32[2,4,4,256,4]{4,3,2,1,0:T(8,128)} reshape(f32[2,1,1,16,1024]{4,3,2,1,0:T(8,128)S(1)} %copy-done.2) | data formatting | bytes 262144 | tf_op jit(solution)/shard_map/reshape | solution.py:254
  10.8 2.3 ge.18
  13.1 2.6 %broadcast_select_fusion = f32[2,4,4,256,4]{4,3,2,1,0:T(8,128)S(1)} fusion(f32[2,4,4,256,4]{4,3,2,1,0:T(8,128)} %reshape.252, pred[4,4,256,4]{3,2,1,0:T(8,128)(4,1)S(1)} %ge.18), kind=kLoop, calls=%fused_computation.11 | loop fusion | flops 32768 | bytes 278528 | tf_op jit(solution)/shard_map/jit(_where)/select_n | solution.py:256
  15.7 8.2 %slice_reduce_fusion.2 = (f32[2,4,4,256]{3,2,1,0:T(4,128)S(1)}, f32[2,4,4,256]{3,2,1,0:T(4,128)S(1)}, f32[2,4,4,256]{3,2,1,0:T(4,128)S(1)}, f32[2,4,4,256,1]{4,3,2,1,0:T(8,128)}) fusion(f32[2,4,4,256,4]{4,3,2,1,0:T(8,128)S(1)} %broadcast_select_fusion), kind=kLoop, calls=%fused_computation.2 | loop fusion | bytes 262144 | tf_op jit(solution)/shard_map/slice | solution.py:259
  24.3 2.9 %copy.67 = f32[2,4,4,256,1]{3,0,2,1,4:T(2,128)S(1)} copy(f32[2,4,4,256,1]{4,3,2,1,0:T(8,128)} %get-tuple-element.18) | data formatting | bytes 65536 | tf_op jit(solution)/shard_map/slice | solution.py:259
  27.1 0.1 pad_maximum_fusion
  27.2 0.7 copy.71
  27.9 6.2 %all-to-all-start = ((f32[2,16,4,256]{3,0,2,1:T(2,128)}), f32[2,16,4,256]{3,0,2,1:T(2,128)S(1)}, u32[]{:S(2)}, u32[]{:S(2)}) async-start(f32[2,16,4,256]{3,0,2,1:T(2,128)} %copy.71), calls=%async_computation | async-start | bytes 262144 | tf_op jit(solution)/shard_map/all_to_all | solution.py:263
  34.1 0.1 fusion.14
  34.1 0.1 multiply_multiply_fusion
  34.3 63.3 %all-to-all-done = f32[2,16,4,256]{3,0,2,1:T(2,128)S(1)} async-done(((f32[2,16,4,256]{3,0,2,1:T(2,128)}), f32[2,16,4,256]{3,0,2,1:T(2,128)S(1)}, u32[]{:S(2)}, u32[]{:S(2)}) %all-to-all-start) | async-done | bytes 131104 | tf_op jit(solution)/shard_map/all_to_all | solution.py:263
  97.7 0.1 copy.85
  97.7 0.1 clamp_subtract_fusion
  97.8 0.1 copy.84
  97.9 0.1 clamp_subtract_fusion.1
  97.9 0.2 shift-left_or_fusion
  98.1 0.7 copy.83
  98.8 0.6 reshape.253.n_ref
  99.4 0.8 pad_maximum_fusion.1.c_ref
  100.2 43.3 %shard_map.82 = f32[8192,1]{1,0:T(8,128)} custom-call(s32[64]{0:T(128)} %reshape.253.n_ref, s32[16384]{0:T(1024)} %bitcast.37, f32[2,16384]{1,0:T(2,128)} %pad_maximum_fusion.1.c_ref, f32[1024,4,128]{2,1,0:T(4,128)} %copy-done, f32[1024,4,128]{2,1,0:T(4,128)} %collective-permute-done.refs_1_), custom_call_target="tpu_custom_call" | custom-call | tf_op jit(solution)/shard_map/pallas_call | solution.py:156
  143.5 2.8 %copy.75 = f32[8192,1]{0,1:T(1,128)S(1)} copy(f32[8192,1]{1,0:T(8,128)} %shard_map.82) | data formatting | bytes 65536 | tf_op jit(solution)/shard_map/pallas_call | solution.py:156
  146.3 20.2 %shard_map.83 = f32[8192,1]{1,0:T(8,128)} custom-call(s32[64]{0:T(128)} %reshape.253.n_ref, s32[16384]{0:T(1024)} %bitcast.38, f32[2,16384]{1,0:T(2,128)} %pad_maximum_fusion.1.c_ref, f32[1024,4,128]{2,1,0:T(4,128)} %collective-permute-done.1.refs_0_, f32[1024,4,128]{2,1,0:T(4,128)} %collective-permute-done.2.refs_1_), custom_call_target="tpu_custom_call" | custom-call | tf_op jit(solution)/shard_map/pallas_call | solution.py:156
  166.5 2.8 %copy.76 = f32[8192,1]{0,1:T(1,128)S(1)} copy(f32[8192,1]{1,0:T(8,128)} %shard_map.83) | data formatting | bytes 65536 | tf_op jit(solution)/shard_map/pallas_call | solution.py:156
  169.4 0.2 maximum_reduce_fusion
  169.6 0.7 copy.77
  170.3 3.5 %all-to-all-start.1 = ((f32[16,4,256]{2,1,0:T(4,128)}), f32[16,4,256]{2,1,0:T(4,128)S(1)}, u32[]{:S(2)}, u32[]{:S(2)}) async-start(f32[16,4,256]{2,1,0:T(4,128)} %copy.77), calls=%async_computation.1 | async-start | bytes 131072 | tf_op jit(solution)/shard_map/all_to_all | solution.py:271
  173.8 0.6 copy.82
  174.5 0.1 copy.78
  174.5 0.6 convert_reduce_fusion.1.n_ref
  175.2 5.5 %all-to-all-done.1 = f32[16,4,256]{2,1,0:T(4,128)S(1)} async-done(((f32[16,4,256]{2,1,0:T(4,128)}), f32[16,4,256]{2,1,0:T(4,128)S(1)}, u32[]{:S(2)}, u32[]{:S(2)}) %all-to-all-start.1) | async-done | bytes 65568 | tf_op jit(solution)/shard_map/all_to_all | solution.py:271
  180.6 0.7 copy.86
  181.3 12.3 %shard_map.84 = f32[4097]{0:T(1024)} custom-call(s32[16]{0:T(128)} %convert_reduce_fusion.1.n_ref, s32[16384]{0:T(1024)} %bitcast.42, f32[16384]{0:T(1024)} %bitcast.43), custom_call_target="tpu_custom_call" | custom-call | tf_op jit(solution)/shard_map/pallas_call | solution.py:193
  193.6 0.7 slice.136
  194.3 6.8 %all_gather.6 = f32[16,512]{1,0:T(8,128)S(1)} all-gather(f32[16,256]{1,0:T(8,128)S(1)} %reshape.257), channel_id=1, replica_groups=mesh['stn'=16,'chan'=2] {'chan'}, dimensions={1}, use_global_device_ids=true | all-gather | bytes 49152 | tf_op jit(solution)/shard_map/all_gather | solution.py:281
  201.1 19.5 %all_gather.7 = f32[256,515]{1,0:T(8,128)S(1)} all-gather(f32[16,515]{1,0:T(8,128)S(1)} %pad_maximum_fusion.2), channel_id=1, replica_groups=mesh['stn'=16,'chan'=2] {'stn'}, dimensions={0}, use_global_device_ids=true | all-gather | bytes 560320 | tf_op jit(solution)/shard_map/all_gather | solution.py:283
  220.6 0.3 slice_reduce_fusion.5
  220.9 0.1 slice.140
  221.0 0.2 multiply_add_fusion
  221.2 3.9 %multiply_convert_fusion = (bf16[256,2,512]{2,0,1:T(8,128)(2,1)S(1)}, bf16[256,2,512]{2,0,1:T(8,128)(2,1)S(1)}) fusion(f32[2,512]{1,0:T(2,128)S(1)} %multiply_multiply_fusion, f32[2]{0:T(128)S(1)} %get-tuple-element.17, f32[256,512]{1,0:T(8,128)S(1)} %slice.140, f32[256,512]{1,0:T(8,128)S(1)} %multiply_add_fusion, f32[2]{0:T(128)S(1)} %broadcast_multiply_fusion), kind=kLoop, calls=%fused_computation.19 | loop fusion | flops 1835008 | bytes 2101264 | tf_op jit(solution)/shard_map/convert_element_type | solution.py:228
  225.1 3.9 %fusion.13 = (bf16[256,2,512]{2,0,1:T(8,128)(2,1)S(1)}, bf16[256,2,512]{2,0,1:T(8,128)(2,1)S(1)}, bf16[256,2,512]{2,0,1:T(8,128)(2,1)S(1)}) fusion(f32[2,512]{1,0:T(2,128)S(1)} %multiply_multiply_fusion, f32[2]{0:T(128)S(1)} %get-tuple-element.17, f32[256,512]{1,0:T(8,128)S(1)} %slice.140, f32[256,512]{1,0:T(8,128)S(1)} %multiply_add_fusion, ...), kind=kLoop, calls=%fused_computation.47 | loop fusion | flops 2621440 | bytes 2625552 | tf_op jit(solution)/shard_map/neg | solution.py:230
  229.0 0.7 fusion
  229.8 0.9 fusion.11
  230.6 17.1 %all_to_all.19 = bf16[2,2,256,256]{3,1,0,2:T(2,128)(2,1)S(1)} all-to-all(bf16[2,2,256,256]{3,1,0,2:T(2,128)(2,1)S(1)} %fusion.11), channel_id=1, replica_groups=mesh['stn'=16,'chan'=2] {'stn'}, dimensions={2} | all-to-all | bytes 1048576 | tf_op jit(solution)/shard_map/all_to_all | solution.py:296
  247.7 0.4 convert_bitcast_fusion
  248.2 1.2 copy.80
  (37 shorter events, 0.5 us)
Async XLA Ops:
  0.0 5.1 %copy-start.2 = (f32[2,1,1,16,1024]{4,3,2,1,0:T(8,128)S(1)}, f32[2,1,1,16,1024]{4,3,2,1,0:T(8,128)}, u32[]{:S(2)}) copy-start(f32[2,1,1,16,1024]{4,3,2,1,0:T(8,128)} %param.9) | copy-start | bytes 393220
  0.0 10.8 %copy-start.1 = (s32[1,1,16,1024]{3,2,1,0:T(8,128)S(1)}, s32[1,1,16,1024]{3,2,1,0:T(8,128)}, u32[]{:S(2)}) copy-start(s32[1,1,16,1024]{3,2,1,0:T(8,128)} %param.10) | copy-start | bytes 196612
  2.0 13.7 %copy-start = (f32[1024,4,128]{2,1,0:T(4,128)}, f32[1024,4,128]{2,1,0:T(4,128)S(1)}, u32[]{:S(2)}) copy-start(f32[1024,4,128]{2,1,0:T(4,128)S(1)} %reshape.254.refs_0_) | copy-start | bytes 6291460
  2.0 98.2 %collective-permute-start = (f32[1024,4,128]{2,1,0:T(4,128)S(1)}, f32[1024,4,128]{2,1,0:T(4,128)}, u32[]{:S(2)}, u32[]{:S(2)}) collective-permute-start(f32[1024,4,128]{2,1,0:T(4,128)S(1)} %reshape.254.refs_0_), channel_id=1, source_target_pairs={{0,2},{2,0},{4,6},{6,4},{8,10},{10,8},{12,14},{14,12},{16,18},{18,... | collective-permute-start | bytes 6291464 | tf_op jit(solution)/shard_map/ppermute | solution.py:268
  2.6 143.8 %collective-permute-start.1 = (f32[1024,4,128]{2,1,0:T(4,128)S(1)}, f32[1024,4,128]{2,1,0:T(4,128)}, u32[]{:S(2)}, u32[]{:S(2)}) collective-permute-start(f32[1024,4,128]{2,1,0:T(4,128)S(1)} %reshape.254.refs_0_), channel_id=1, source_target_pairs={{0,4},{2,6},{4,0},{6,2},{8,12},{10,14},{12,8},{14,10},{16,20},{18,... | collective-permute-start | bytes 6291464 | tf_op jit(solution)/shard_map/ppermute | solution.py:268
  5.1 141.2 %collective-permute-start.2 = (f32[1024,4,128]{2,1,0:T(4,128)S(1)}, f32[1024,4,128]{2,1,0:T(4,128)}, u32[]{:S(2)}, u32[]{:S(2)}) collective-permute-start(f32[1024,4,128]{2,1,0:T(4,128)S(1)} %reshape.254.refs_0_), channel_id=1, source_target_pairs={{0,6},{2,4},{4,2},{6,0},{8,14},{10,12},{12,10},{14,8},{16,22},{18,... | collective-permute-start | bytes 6291464 | tf_op jit(solution)/shard_map/ppermute | solution.py:268
  23.9 10.1 %copy-start.7 = (f32[32]{0:T(128)S(1)}, f32[32]{0:T(128)}, u32[]{:S(2)}) copy-start(f32[32]{0:T(128)} %param.13) | copy-start | bytes 388
  23.9 10.2 %copy-start.4 = (f32[512]{0:T(512)S(1)}, f32[512]{0:T(512)}, u32[]{:S(2)}) copy-start(f32[512]{0:T(512)} %param.15) | copy-start | bytes 6148
  23.9 10.2 %copy-start.5 = (f32[512]{0:T(512)S(1)}, f32[512]{0:T(512)}, u32[]{:S(2)}) copy-start(f32[512]{0:T(512)} %param.14) | copy-start | bytes 6148
  24.0 10.3 %copy-start.3 = (f32[3,512]{1,0:T(4,128)S(1)}, f32[3,512]{1,0:T(4,128)}, u32[]{:S(2)}) copy-start(f32[3,512]{1,0:T(4,128)} %param.12) | copy-start | bytes 18436
  27.9 69.7 %all-to-all-start = ((f32[2,16,4,256]{3,0,2,1:T(2,128)}), f32[2,16,4,256]{3,0,2,1:T(2,128)S(1)}, u32[]{:S(2)}, u32[]{:S(2)}) async-start(f32[2,16,4,256]{3,0,2,1:T(2,128)} %copy.71), calls=%async_computation | async-start | bytes 262144 | tf_op jit(solution)/shard_map/all_to_all | solution.py:263
  166.5 7.9 %copy-start.6 = (f32[3,16]{1,0:T(4,128)S(1)}, f32[3,16]{1,0:T(4,128)}, u32[]{:S(2)}) copy-start(f32[3,16]{1,0:T(4,128)} %param.11) | copy-start | bytes 580
  170.3 10.4 %all-to-all-start.1 = ((f32[16,4,256]{2,1,0:T(4,128)}), f32[16,4,256]{2,1,0:T(4,128)S(1)}, u32[]{:S(2)}, u32[]{:S(2)}) async-start(f32[16,4,256]{2,1,0:T(4,128)} %copy.77), calls=%async_computation.1 | async-start | bytes 131072 | tf_op jit(solution)/shard_map/all_to_all | solution.py:271

commit v13 on v11

--- a/solution.py
+++ b/solution.py
@@ -156,7 +156,7 @@
     rows = n_ref.shape[0]
     width = d_ref.shape[0] // rows
     half = width // 2
-    step = 8 if width % 8 == 0 else 2
+    step = 16 if width % 16 == 0 else 2
     for row in range(rows):
         def body(i, carry, row=row):
             for u in range(step):
@@ -251,11 +251,10 @@
     n_chan = lax.axis_size("chan")
     if channels % groups:
         return _rows_path(own_iono, station_rows, directions, freq_ratio, source_flux, spectral_index)
-    iono_phase = lax.all_gather(own_iono, "chan", axis=1, tiled=True)
-    packed = jnp.concatenate([iono_phase, station_rows], axis=1)
+    packed = jnp.concatenate([own_iono, station_rows], axis=1)
     gathered = lax.all_gather(packed, "stn", axis=0, tiled=True)
-    all_iono = gathered[:, : n_chan * local_sources]
-    all_rows = gathered[:, n_chan * local_sources :]
+    all_rows = gathered[:, local_sources:]
+    all_iono = lax.all_gather(gathered[:, :local_sources], "chan", axis=1, tiled=True)
     per_dev = channels // groups
     my_freq = lax.dynamic_slice_in_dim(freq_ratio, lax.axis_index("stn") * per_dev, per_dev)
     phasors = make_phasors(all_rows, all_iono, directions, my_freq)

time: 185 us -> 188 us (1.016)
  blocking collectives: 40.9 us -> 46.6 us
  starting transfers between devices: 57.3 us -> 53.3 us
    all_gather x1, blocking collectives: 4.39 us -> 10.6 us  [body(): lax.all_gather(gathered[:, :local_sources], 'chan', axis=1, tiled=True)]
    all_to_all x1, starting transfers between devices: 49.4 us -> 45.5 us  [body(): lax.all_to_all(sampled, 'stn', split_axis=0, concat_axis=0, tiled=True)]
where the time goes in v13:
time: 188 us
  starting transfers between devices  53.3 us (28%)
  Pallas kernels  47.3 us (25%)
  blocking collectives  46.6 us (25%)
  other arithmetic  17.4 us (9%)
  local copies, waits for them, and re-layouts  11.7 us (6%)
  waiting for transfers between devices  10.7 us (6%)
    all_to_all x1, starting transfers between devices, body(): lax.all_to_all(sampled, 'stn', split_axis=0, concat_axis=0, tiled=True)  45.5 us
    pallas_call x1, Pallas kernels, interpolate_balanced(): pl.pallas_call(_balanced_kernel, grid_spec=pltpu.PrefetchScalarGridSpec(n...  35.6 us
    all_gather x1, blocking collectives, body(): gathered = lax.all_gather(packed, 'stn', axis=0, tiled=True)  18.9 us
    all_to_all x1, blocking collectives, body(): lax.all_to_all(visible.astype(jnp.bfloat16), 'stn', split_axis=2, concat_...  17.2 us
    pallas_call x1, Pallas kernels, scatter_kernel(): pl.pallas_call(_scatter_kernel, grid_spec=pltpu.PrefetchScalarGridSpec(nu...  11.7 us
    all_gather x1, blocking collectives, body(): lax.all_gather(gathered[:, :local_sources], 'chan', axis=1, tiled=True)  10.6 us
    all_to_all x1, starting transfers between devices, body(): lax.all_to_all(send, 'stn', split_axis=1, concat_axis=1, tiled=True)  7.39 us
    all_to_all x1, waiting for transfers between devices, body(): lax.all_to_all(sampled, 'stn', split_axis=0, concat_axis=0, tiled=True)  5.44 us
  transfers between devices with their start and end apart: 3, of which 2 were waited for; matrix products, arithmetic and copies ran while one was open for 3% of the time, Pallas kernels for 0%

profile of v13, /device:TPU:0, one launch (start us, length us, event | category | flops | bytes accessed | tf_op | source)
XLA Modules:
  0.0 188.1 jit_solution(15382594262393417523)
XLA Ops:
  0.0 1.2 copy.71
  1.2 0.9 broadcast_compare_fusion
  2.1 0.3 copy.70
  2.4 0.2 ge.18
  2.6 0.7 broadcast_select_fusion
  3.3 0.8 fusion.15
  4.1 0.3 copy.72
  4.4 0.2 copy.73
  4.6 0.1 pad_maximum_fusion
  4.7 1.0 copy.74
  5.7 7.4 %all-to-all-start = ((f32[2,16,2,512]{3,2,0,1:T(2,128)}), f32[2,16,2,512]{3,2,0,1:T(2,128)S(1)}, u32[]{:S(2)}, u32[]{:S(2)}) async-start(f32[2,16,2,512]{3,2,0,1:T(2,128)} %copy.74), calls=%async_computation | async-start | bytes 262144 | tf_op jit(solution)/shard_map/all_to_all | solution.py:239
  13.1 0.0 copy-start.6
  13.1 0.0 copy-start.4
  13.1 0.0 copy-start.2
  13.1 1.9 %reshape.244.own_ref = f32[1024,4,128]{2,1,0:T(4,128)S(1)} reshape(f32[2,512,512]{2,1,0:T(8,128)} %param.8) | data formatting | bytes 4194304 | tf_op jit(solution)/shard_map/reshape | solution.py:242
  15.1 0.5 collective-permute-start
  15.5 0.1 fusion.14
  15.6 0.1 multiply_multiply_fusion
  15.7 5.2 %all-to-all-done = f32[2,16,2,512]{3,2,0,1:T(2,128)S(1)} async-done(((f32[2,16,2,512]{3,2,0,1:T(2,128)}), f32[2,16,2,512]{3,2,0,1:T(2,128)S(1)}, u32[]{:S(2)}, u32[]{:S(2)}) %all-to-all-start) | async-done | bytes 131104 | tf_op jit(solution)/shard_map/all_to_all | solution.py:239
  21.0 0.1 copy.85
  21.1 0.1 copy.86
  21.2 0.1 clamp_subtract_fusion
  21.3 0.1 shift-left_or_fusion
  21.5 0.6 copy.84
  22.1 0.6 reshape.243.n_ref
  22.7 0.8 pad_maximum_fusion.1.c_ref
  23.5 35.6 %shard_map.82 = f32[16384,1]{1,0:T(8,128)} custom-call(s32[32]{0:T(128)} %reshape.243.n_ref, s32[16384]{0:T(1024)} %bitcast.41, f32[2,16384]{1,0:T(2,128)} %pad_maximum_fusion.1.c_ref, f32[1024,4,128]{2,1,0:T(4,128)} %copy-done, f32[1024,4,128]{2,1,0:T(4,128)} %collective-permute-done.partner_ref), custom_call_target="tpu_custom_call" | custom-call | tf_op jit(solution)/shard_map/pallas_call | solution.py:142
  59.1 4.6 %reduce.2 = f32[16384]{0:T(1024)S(1)} reduce(f32[16384,1]{1,0:T(8,128)} %shard_map.82, f32[]{:T(128)} %constant.38), dimensions={1}, to_apply=%pallas_call.6.reduce_sub_computation | reduce | bytes 131076 | tf_op jit(solution)/shard_map/pallas_call | solution.py:142
  63.8 0.7 copy.78
  64.5 45.5 %all-to-all-start.1 = ((f32[16,2,512]{2,1,0:T(2,128)}), f32[16,2,512]{2,1,0:T(2,128)S(1)}, u32[]{:S(2)}, u32[]{:S(2)}) async-start(f32[16,2,512]{2,1,0:T(2,128)} %copy.78), calls=%async_computation.1 | async-start | bytes 131072 | tf_op jit(solution)/shard_map/all_to_all | solution.py:245
  110.0 0.6 copy.83
  110.6 0.1 copy.79
  110.7 0.7 convert_reduce_fusion.1.n_ref
  111.4 5.4 %all-to-all-done.1 = f32[16,2,512]{2,1,0:T(2,128)S(1)} async-done(((f32[16,2,512]{2,1,0:T(2,128)}), f32[16,2,512]{2,1,0:T(2,128)S(1)}, u32[]{:S(2)}, u32[]{:S(2)}) %all-to-all-start.1) | async-done | bytes 65568 | tf_op jit(solution)/shard_map/all_to_all | solution.py:245
  116.8 0.6 copy.87
  117.5 11.7 %shard_map.83 = f32[4097]{0:T(1024)} custom-call(s32[16]{0:T(128)} %convert_reduce_fusion.1.n_ref, s32[16384]{0:T(1024)} %bitcast.45, f32[16384]{0:T(1024)} %bitcast.46), custom_call_target="tpu_custom_call" | custom-call | tf_op jit(solution)/shard_map/pallas_call | solution.py:174
  129.2 0.7 slice.67
  129.9 18.9 %all_gather.6 = f32[256,259]{1,0:T(8,128)S(1)} all-gather(f32[16,259]{1,0:T(8,128)S(1)} %pad_maximum_fusion.2), channel_id=1, replica_groups=mesh['stn'=16,'chan'=2] {'stn'}, dimensions={0}, use_global_device_ids=true | all-gather | bytes 281792 | tf_op jit(solution)/shard_map/all_gather | solution.py:255
  148.8 0.3 slice_reduce_fusion.2
  149.1 10.6 %all_gather.7 = f32[256,512]{1,0:T(8,128)S(1)} all-gather(f32[256,256]{1,0:T(8,128)S(1)} %slice.71), channel_id=1, replica_groups=mesh['stn'=16,'chan'=2] {'chan'}, dimensions={1}, use_global_device_ids=true | all-gather | bytes 786432 | tf_op jit(solution)/shard_map/all_gather | solution.py:257
  159.7 0.2 multiply_add_fusion
  159.8 3.9 %multiply_convert_fusion = (bf16[256,2,512]{2,0,1:T(8,128)(2,1)S(1)}, bf16[256,2,512]{2,0,1:T(8,128)(2,1)S(1)}) fusion(f32[2,512]{1,0:T(2,128)S(1)} %multiply_multiply_fusion, f32[2]{0:T(128)S(1)} %get-tuple-element.14, f32[256,512]{1,0:T(8,128)S(1)} %all_gather.7, f32[256,512]{1,0:T(8,128)S(1)} %multiply_add_fusion, f32[2]{0:T(128)S(1)} %broadcast_multiply_fusion), kind=kLoop, calls=%fused_computation.16 | loop fusion | flops 1835008 | bytes 2101264 | tf_op jit(solution)/shard_map/convert_element_type | solution.py:209
  163.8 3.9 %fusion.13 = (bf16[256,2,512]{2,0,1:T(8,128)(2,1)S(1)}, bf16[256,2,512]{2,0,1:T(8,128)(2,1)S(1)}, bf16[256,2,512]{2,0,1:T(8,128)(2,1)S(1)}) fusion(f32[2,512]{1,0:T(2,128)S(1)} %multiply_multiply_fusion, f32[2]{0:T(128)S(1)} %get-tuple-element.14, f32[256,512]{1,0:T(8,128)S(1)} %all_gather.7, f32[256,512]{1,0:T(8,128)S(1)} %multiply_add_fusion, ...), kind=kLoop, calls=%fused_computation.40 | loop fusion | flops 2621440 | bytes 2625552 | tf_op jit(solution)/shard_map/neg | solution.py:211
  167.7 0.7 fusion
  168.5 0.9 fusion.11
  169.3 17.2 %all_to_all.19 = bf16[2,2,256,256]{3,1,0,2:T(2,128)(2,1)S(1)} all-to-all(bf16[2,2,256,256]{3,1,0,2:T(2,128)(2,1)S(1)} %fusion.11), channel_id=1, replica_groups=mesh['stn'=16,'chan'=2] {'stn'}, dimensions={2} | all-to-all | bytes 1048576 | tf_op jit(solution)/shard_map/all_to_all | solution.py:268
  186.5 0.4 convert_bitcast_fusion
  186.9 1.2 copy.81
  (22 shorter events, 0.2 us)
Async XLA Ops:
  5.7 15.3 %all-to-all-start = ((f32[2,16,2,512]{3,2,0,1:T(2,128)}), f32[2,16,2,512]{3,2,0,1:T(2,128)S(1)}, u32[]{:S(2)}, u32[]{:S(2)}) async-start(f32[2,16,2,512]{3,2,0,1:T(2,128)} %copy.74), calls=%async_computation | async-start | bytes 262144 | tf_op jit(solution)/shard_map/all_to_all | solution.py:239
  13.1 2.5 %copy-start.6 = (f32[32]{0:T(128)S(1)}, f32[32]{0:T(128)}, u32[]{:S(2)}) copy-start(f32[32]{0:T(128)} %param.13) | copy-start | bytes 388
  13.1 2.6 %copy-start.3 = (f32[512]{0:T(512)S(1)}, f32[512]{0:T(512)}, u32[]{:S(2)}) copy-start(f32[512]{0:T(512)} %param.15) | copy-start | bytes 6148
  13.1 2.5 %copy-start.4 = (f32[512]{0:T(512)S(1)}, f32[512]{0:T(512)}, u32[]{:S(2)}) copy-start(f32[512]{0:T(512)} %param.14) | copy-start | bytes 6148
  13.1 2.6 %copy-start.2 = (f32[3,512]{1,0:T(4,128)S(1)}, f32[3,512]{1,0:T(4,128)}, u32[]{:S(2)}) copy-start(f32[3,512]{1,0:T(4,128)} %param.12) | copy-start | bytes 18436
  15.1 8.4 %copy-start = (f32[1024,4,128]{2,1,0:T(4,128)}, f32[1024,4,128]{2,1,0:T(4,128)S(1)}, u32[]{:S(2)}) copy-start(f32[1024,4,128]{2,1,0:T(4,128)S(1)} %reshape.244.own_ref) | copy-start | bytes 6291460
  15.1 8.4 %collective-permute-start = (f32[1024,4,128]{2,1,0:T(4,128)S(1)}, f32[1024,4,128]{2,1,0:T(4,128)}, u32[]{:S(2)}, u32[]{:S(2)}) collective-permute-start(f32[1024,4,128]{2,1,0:T(4,128)S(1)} %reshape.244.own_ref), channel_id=1, source_target_pairs={{0,2},{2,0},{4,6},{6,4},{8,10},{10,8},{12,14},{14,12},{16,18},{18,... | collective-permute-start | bytes 6291464 | tf_op jit(solution)/shard_map/ppermute | solution.py:243
  59.1 50.9 %copy-start.1 = (s32[1,1,16,1024]{3,2,1,0:T(8,128)S(1)}, s32[1,1,16,1024]{3,2,1,0:T(8,128)}, u32[]{:S(2)}) copy-start(s32[1,1,16,1024]{3,2,1,0:T(8,128)} %param.10) | copy-start | bytes 196612
  59.1 51.5 %copy-start.5 = (f32[3,16]{1,0:T(4,128)S(1)}, f32[3,16]{1,0:T(4,128)}, u32[]{:S(2)}) copy-start(f32[3,16]{1,0:T(4,128)} %param.11) | copy-start | bytes 580
  64.5 52.4 %all-to-all-start.1 = ((f32[16,2,512]{2,1,0:T(2,128)}), f32[16,2,512]{2,1,0:T(2,128)S(1)}, u32[]{:S(2)}, u32[]{:S(2)}) async-start(f32[16,2,512]{2,1,0:T(2,128)} %copy.78), calls=%async_computation.1 | async-start | bytes 131072 | tf_op jit(solution)/shard_map/all_to_all | solution.py:245

commit v14 on v12

--- a/solution.py
+++ b/solution.py
@@ -135,7 +135,7 @@
 SEG = [0]
 
 
-def interpolate_parts(screens, coords, live, split):
+def interpolate_parts(screens, coords, live, later):
     rows, nb, _ = screens[0].shape
     cols = nb * 128
     _, parts, senders, seg = coords.shape
@@ -149,9 +149,11 @@
     frac = jnp.stack([y - r, x - k])
     spec = pl.BlockSpec((rows, nb, 128), lambda i, n, rr, cc: (0, 0, 0))
     outs = []
-    for lo, hi in ((0, split), (split, parts)):
-        if lo == hi:
-            continue
+    lo = 0
+    while lo < parts:
+        if lo:
+            screens = later(outs[-1])
+        hi = lo + len(screens)
         size = (hi - lo) * senders * seg
         out = pl.pallas_call(
             functools.partial(_balanced_kernel, lo),
@@ -162,8 +164,9 @@
                 out_specs=pl.BlockSpec((size, 1), lambda i, n, rr, cc: (0, 0)),
             ),
             out_shape=jax.ShapeDtypeStruct((size, 1), jnp.float32),
-        )(live, rk, frac, *screens[lo:hi])
+        )(live, rk, frac, *screens)
         outs.append(out)
+        lo = hi
     return jnp.concatenate(outs, axis=0).reshape(parts, senders, seg)
 
 
@@ -262,12 +265,19 @@
     send = jnp.stack([to_dest(q) for q in range(parts)], axis=3).reshape(2, groups, parts, part_len)
     received = lax.all_to_all(send, "stn", split_axis=1, concat_axis=1, tiled=True)
     kin = received.transpose(0, 2, 1, 3)
+    own = screen.reshape(strip_rows, tile_cols // 128, 128)
+    swap_core = [(i, i ^ 1) for i in range(groups)]
+    screens = [own, lax.ppermute(own, "stn", swap_core)]
+    later = None
+    if parts == 4:
+        late, kin = lax.optimization_barrier((own, kin))
+        far = lax.ppermute(late, "stn", [(i, i ^ 2) for i in range(groups)])
+
+        def later(first_out):
+            far_ready, _ = lax.optimization_barrier((far, first_out))
+            return [far_ready, lax.ppermute(far_ready, "stn", swap_core)]
     live = jnp.sum((kin[0] >= 0.0).astype(jnp.int32), axis=2).reshape(-1)
-    own = screen.reshape(strip_rows, tile_cols // 128, 128)
-    screens = [own] + [
-        lax.ppermute(own, "stn", [(i, i ^ q) for i in range(groups)]) for q in range(1, parts)
-    ]
-    sampled = interpolate_parts(screens, kin, live, 2).transpose(1, 0, 2)
+    sampled = interpolate_parts(screens, kin, live, later).transpose(1, 0, 2)
     back = lax.all_to_all(sampled, "stn", split_axis=0, concat_axis=0, tiled=True)
     PARTS[0] = parts
     buffer = scatter_kernel(query_dest.reshape(groups, capacity), back, queries + 1)

time: 251 us -> 217 us (0.86)
  waiting for transfers between devices: 68.8 us -> 35.5 us
  Pallas kernels: 75.8 us -> 56.4 us
  starting transfers between devices: 12.8 us -> 31.4 us
    all_to_all x1, waiting for transfers between devices: 63.3 us -> 5.48 us  [body(): lax.all_to_all(send, 'stn', split_axis=1, concat_axis=1, tiled=True)]
    ppermute x3, waiting for transfers between devices: 0.01 us -> 24.5 us  [the longest x1 23.2 us: body(): far = lax.ppermute(late, 'stn', [(i, i ^ 2) for i in range(groups)])]
    all_to_all x1, starting transfers between devices: 3.5 us -> 23.4 us  [body(): lax.all_to_all(sampled, 'stn', split_axis=0, concat_axis=0, tiled=True)]
    pallas_call x2, Pallas kernels: 63.5 us -> 44.1 us  [interpolate_parts(): pl.pallas_call(functools.partial(_balanced_kernel, lo), grid_spec=pltpu.P...]
    ppermute x3, starting transfers between devices: 3.15 us -> 0.55 us  [the longest x1 0.47 us: body(): screens = [own, lax.ppermute(own, 'stn', swap_core)]]
  transfers between devices with their start and end apart: 5 -> 5, of which waited for: 2 -> 4; matrix products, arithmetic and copies ran while one was open for 12% -> 4% of each run, Pallas kernels for 17% -> 10%
where the time goes in v14:
time: 217 us; the launch traced here: 215 us
  Pallas kernels  56.4 us (26%)
  blocking collectives  41.1 us (19%)
  local copies, waits for them, and re-layouts  35.5 us (16%)
  waiting for transfers between devices  35.5 us (16%)
  starting transfers between devices  31.4 us (14%)
  other arithmetic  14.1 us (6%)
    pallas_call x2, Pallas kernels, interpolate_parts(): pl.pallas_call(functools.partial(_balanced_kernel, lo), grid_spec=pltpu.P...  44.1 us
    all_to_all x1, starting transfers between devices, body(): lax.all_to_all(sampled, 'stn', split_axis=0, concat_axis=0, tiled=True)  23.4 us
    ppermute x1, waiting for transfers between devices, body(): far = lax.ppermute(late, 'stn', [(i, i ^ 2) for i in range(groups)])  23.2 us
    all_gather x1, blocking collectives, body(): gathered = lax.all_gather(packed, 'stn', axis=0, tiled=True)  19.8 us
    all_to_all x1, blocking collectives, body(): lax.all_to_all(visible.astype(jnp.bfloat16), 'stn', split_axis=2, concat_...  16.9 us
    pallas_call x1, Pallas kernels, scatter_kernel(): pl.pallas_call(_scatter_kernel, grid_spec=pltpu.PrefetchScalarGridSpec(nu...  12.3 us
    slice x2, local copies, waits for them, and re-layouts, to_dest(): piece = coords[..., q]  11.1 us
    all_to_all x1, starting transfers between devices, body(): lax.all_to_all(send, 'stn', split_axis=1, concat_axis=1, tiled=True)  7.39 us
  transfers between devices with their start and end apart: 5, of which 4 were waited for; matrix products, arithmetic and copies ran while one was open for 4% of the time, Pallas kernels for 10%

profile of v14, /device:TPU:0, one launch (start us, length us, event | category | flops | bytes accessed | tf_op | source)
XLA Modules:
  0.0 214.9 jit_solution(1761514329852365174)
XLA Ops:
  0.0 6.5 %reshape.253 = f32[2,4,4,256,4]{4,3,2,1,0:T(8,128)} reshape(f32[2,1,1,16,1024]{4,3,2,1,0:T(8,128)} %param.9) | data formatting | bytes 262144 | tf_op jit(solution)/shard_map/reshape | solution.py:257
  6.5 2.3 %ge.18 = pred[4,4,256,4]{3,2,1,0:T(8,128)(4,1)S(1)} reshape(pred[1,1,16,1024]{3,2,1,0:T(8,128)(4,1)S(1)} %broadcast_compare_fusion) | data formatting | bytes 32768 | tf_op jit(solution)/shard_map/ge | solution.py:258
  8.8 2.6 %broadcast_select_fusion = f32[2,4,4,256,4]{4,3,2,1,0:T(8,128)S(1)} fusion(f32[2,4,4,256,4]{4,3,2,1,0:T(8,128)} %reshape.253, pred[4,4,256,4]{3,2,1,0:T(8,128)(4,1)S(1)} %ge.18), kind=kLoop, calls=%fused_computation.11 | loop fusion | flops 32768 | bytes 278528 | tf_op jit(solution)/shard_map/jit(_where)/select_n | solution.py:259
  11.4 8.2 %slice_reduce_fusion.2 = (f32[2,4,4,256]{3,2,1,0:T(4,128)S(1)}, f32[2,4,4,256]{3,2,1,0:T(4,128)S(1)}, f32[2,4,4,256]{3,2,1,0:T(4,128)S(1)}, f32[2,4,4,256,1]{4,3,2,1,0:T(8,128)}) fusion(f32[2,4,4,256,4]{4,3,2,1,0:T(8,128)S(1)} %broadcast_select_fusion), kind=kLoop, calls=%fused_computation.2 | loop fusion | bytes 262144 | tf_op jit(solution)/shard_map/slice | solution.py:262
  19.9 2.9 %copy.67 = f32[2,4,4,256,1]{3,0,2,1,4:T(2,128)S(1)} copy(f32[2,4,4,256,1]{4,3,2,1,0:T(8,128)} %get-tuple-element.24) | data formatting | bytes 65536 | tf_op jit(solution)/shard_map/slice | solution.py:262
  22.8 0.1 pad_maximum_fusion
  22.9 0.7 copy.71
  23.5 7.4 %all-to-all-start = ((f32[2,16,4,256]{3,0,2,1:T(2,128)}), f32[2,16,4,256]{3,0,2,1:T(2,128)S(1)}, u32[]{:S(2)}, u32[]{:S(2)}) async-start(f32[2,16,4,256]{3,0,2,1:T(2,128)} %copy.71), calls=%async_computation | async-start | bytes 262144 | tf_op jit(solution)/shard_map/all_to_all | solution.py:266
  30.9 1.9 reshape.252.refs_0_
  32.9 0.5 collective-permute-start
  33.4 5.5 %all-to-all-done = f32[2,16,4,256]{3,0,2,1:T(2,128)S(1)} async-done(((f32[2,16,4,256]{3,0,2,1:T(2,128)}), f32[2,16,4,256]{3,0,2,1:T(2,128)S(1)}, u32[]{:S(2)}, u32[]{:S(2)}) %all-to-all-start) | async-done | bytes 131104 | tf_op jit(solution)/shard_map/all_to_all | solution.py:266
  38.9 0.1 copy.85
  39.1 0.1 copy.84
  39.1 0.1 collective-permute-start.1
  39.3 0.2 shift-left_or_fusion
  39.4 0.7 copy.83
  40.1 0.6 reshape.254.n_ref
  40.7 0.8 pad_maximum_fusion.1.c_ref
  41.5 21.4 %shard_map.82 = f32[8192,1]{1,0:T(8,128)} custom-call(s32[64]{0:T(128)} %reshape.254.n_ref, s32[16384]{0:T(1024)} %bitcast.37, f32[2,16384]{1,0:T(2,128)} %pad_maximum_fusion.1.c_ref, f32[1024,4,128]{2,1,0:T(4,128)} %copy-done, f32[1024,4,128]{2,1,0:T(4,128)} %collective-permute-done.refs_1_), custom_call_target="tpu_custom_call" | custom-call | tf_op jit(solution)/shard_map/pallas_call | solution.py:158
  63.0 23.2 %collective-permute-done.1.refs_0_ = f32[1024,4,128]{2,1,0:T(4,128)} collective-permute-done((f32[1024,4,128]{2,1,0:T(4,128)S(1)}, f32[1024,4,128]{2,1,0:T(4,128)}, u32[]{:S(2)}, u32[]{:S(2)}) %collective-permute-start.1) | collective-permute-done | bytes 2097184 | tf_op jit(solution)/shard_map/ppermute | solution.py:274
  86.1 0.1 fusion.14
  86.2 0.1 multiply_multiply_fusion
  86.3 2.8 %copy.75 = f32[8192,1]{0,1:T(1,128)S(1)} copy(f32[8192,1]{1,0:T(8,128)} %shard_map.82) | data formatting | bytes 65536 | tf_op jit(solution)/shard_map/pallas_call | solution.py:158
  89.2 1.3 collective-permute-done.2.refs_1_
  90.5 1.3 copy-done.1
  91.8 22.7 %shard_map.83 = f32[8192,1]{1,0:T(8,128)} custom-call(s32[64]{0:T(128)} %reshape.254.n_ref, s32[16384]{0:T(1024)} %bitcast.38, f32[2,16384]{1,0:T(2,128)} %pad_maximum_fusion.1.c_ref, f32[1024,4,128]{2,1,0:T(4,128)} %collective-permute-done.1.refs_0_, f32[1024,4,128]{2,1,0:T(4,128)} %copy-done.1), custom_call_target="tpu_custom_call" | custom-call | tf_op jit(solution)/shard_map/pallas_call | solution.py:158
  114.5 2.8 %copy.76 = f32[8192,1]{0,1:T(1,128)S(1)} copy(f32[8192,1]{1,0:T(8,128)} %shard_map.83) | data formatting | bytes 65536 | tf_op jit(solution)/shard_map/pallas_call | solution.py:158
  117.3 0.2 maximum_reduce_fusion
  117.6 0.7 copy.77
  118.2 23.4 %all-to-all-start.1 = ((f32[16,4,256]{2,1,0:T(4,128)}), f32[16,4,256]{2,1,0:T(4,128)S(1)}, u32[]{:S(2)}, u32[]{:S(2)}) async-start(f32[16,4,256]{2,1,0:T(4,128)} %copy.77), calls=%async_computation.1 | async-start | bytes 131072 | tf_op jit(solution)/shard_map/all_to_all | solution.py:281
  141.7 0.6 copy.82
  142.3 0.1 copy.78
  142.4 0.6 convert_reduce_fusion.1.n_ref
  143.0 5.5 %all-to-all-done.1 = f32[16,4,256]{2,1,0:T(4,128)S(1)} async-done(((f32[16,4,256]{2,1,0:T(4,128)}), f32[16,4,256]{2,1,0:T(4,128)S(1)}, u32[]{:S(2)}, u32[]{:S(2)}) %all-to-all-start.1) | async-done | bytes 65568 | tf_op jit(solution)/shard_map/all_to_all | solution.py:281
  148.6 0.7 copy.86
  149.2 12.3 %shard_map.84 = f32[4097]{0:T(1024)} custom-call(s32[16]{0:T(128)} %convert_reduce_fusion.1.n_ref, s32[16384]{0:T(1024)} %bitcast.42, f32[16384]{0:T(1024)} %bitcast.43), custom_call_target="tpu_custom_call" | custom-call | tf_op jit(solution)/shard_map/pallas_call | solution.py:196
  161.5 0.7 slice.134
  162.2 4.4 %all_gather.6 = f32[16,512]{1,0:T(8,128)S(1)} all-gather(f32[16,256]{1,0:T(8,128)S(1)} %reshape.257), channel_id=1, replica_groups=mesh['stn'=16,'chan'=2] {'chan'}, dimensions={1}, use_global_device_ids=true | all-gather | bytes 49152 | tf_op jit(solution)/shard_map/all_gather | solution.py:291
  166.6 19.8 %all_gather.7 = f32[256,515]{1,0:T(8,128)S(1)} all-gather(f32[16,515]{1,0:T(8,128)S(1)} %pad_maximum_fusion.2), channel_id=1, replica_groups=mesh['stn'=16,'chan'=2] {'stn'}, dimensions={0}, use_global_device_ids=true | all-gather | bytes 560320 | tf_op jit(solution)/shard_map/all_gather | solution.py:293
  186.4 0.3 slice_reduce_fusion.5
  186.7 0.2 multiply_add_fusion
  186.9 3.9 %multiply_convert_fusion = (bf16[256,2,512]{2,0,1:T(8,128)(2,1)S(1)}, bf16[256,2,512]{2,0,1:T(8,128)(2,1)S(1)}) fusion(f32[2,512]{1,0:T(2,128)S(1)} %multiply_multiply_fusion, f32[2]{0:T(128)S(1)} %get-tuple-element.23, f32[256,512]{1,0:T(8,128)S(1)} %slice.138, f32[256,512]{1,0:T(8,128)S(1)} %multiply_add_fusion, f32[2]{0:T(128)S(1)} %broadcast_multiply_fusion), kind=kLoop, calls=%fused_computation.19 | loop fusion | flops 1835008 | bytes 2101264 | tf_op jit(solution)/shard_map/convert_element_type | solution.py:231
  190.8 3.9 %fusion.13 = (bf16[256,2,512]{2,0,1:T(8,128)(2,1)S(1)}, bf16[256,2,512]{2,0,1:T(8,128)(2,1)S(1)}, bf16[256,2,512]{2,0,1:T(8,128)(2,1)S(1)}) fusion(f32[2,512]{1,0:T(2,128)S(1)} %multiply_multiply_fusion, f32[2]{0:T(128)S(1)} %get-tuple-element.23, f32[256,512]{1,0:T(8,128)S(1)} %slice.138, f32[256,512]{1,0:T(8,128)S(1)} %multiply_add_fusion, ...), kind=kLoop, calls=%fused_computation.47 | loop fusion | flops 2621440 | bytes 2625552 | tf_op jit(solution)/shard_map/neg | solution.py:233
  194.8 0.7 fusion
  195.5 0.9 fusion.11
  196.4 16.9 %all_to_all.19 = bf16[2,2,256,256]{3,1,0,2:T(2,128)(2,1)S(1)} all-to-all(bf16[2,2,256,256]{3,1,0,2:T(2,128)(2,1)S(1)} %fusion.11), channel_id=1, replica_groups=mesh['stn'=16,'chan'=2] {'stn'}, dimensions={2} | all-to-all | bytes 1048576 | tf_op jit(solution)/shard_map/all_to_all | solution.py:306
  213.3 0.4 convert_bitcast_fusion
  213.7 1.2 copy.80
  (37 shorter events, 0.6 us)
Async XLA Ops:
  0.0 6.5 %copy-start.2 = (s32[1,1,16,1024]{3,2,1,0:T(8,128)S(1)}, s32[1,1,16,1024]{3,2,1,0:T(8,128)}, u32[]{:S(2)}) copy-start(s32[1,1,16,1024]{3,2,1,0:T(8,128)} %param.10) | copy-start | bytes 196612
  23.5 15.3 %all-to-all-start = ((f32[2,16,4,256]{3,0,2,1:T(2,128)}), f32[2,16,4,256]{3,0,2,1:T(2,128)S(1)}, u32[]{:S(2)}, u32[]{:S(2)}) async-start(f32[2,16,4,256]{3,0,2,1:T(2,128)} %copy.71), calls=%async_computation | async-start | bytes 262144 | tf_op jit(solution)/shard_map/all_to_all | solution.py:266
  32.9 8.6 %copy-start = (f32[1024,4,128]{2,1,0:T(4,128)}, f32[1024,4,128]{2,1,0:T(4,128)S(1)}, u32[]{:S(2)}) copy-start(f32[1024,4,128]{2,1,0:T(4,128)S(1)} %reshape.252.refs_0_) | copy-start | bytes 6291460
  32.9 8.6 %collective-permute-start = (f32[1024,4,128]{2,1,0:T(4,128)S(1)}, f32[1024,4,128]{2,1,0:T(4,128)}, u32[]{:S(2)}, u32[]{:S(2)}) collective-permute-start(f32[1024,4,128]{2,1,0:T(4,128)S(1)} %reshape.252.refs_0_), channel_id=1, source_target_pairs={{0,2},{2,0},{4,6},{6,4},{8,10},{10,8},{12,14},{14,12},{16,18},{18,... | collective-permute-start | bytes 6291464 | tf_op jit(solution)/shard_map/ppermute | solution.py:270
  39.1 47.0 %collective-permute-start.1 = (f32[1024,4,128]{2,1,0:T(4,128)S(1)}, f32[1024,4,128]{2,1,0:T(4,128)}, u32[]{:S(2)}, u32[]{:S(2)}) collective-permute-start(f32[1024,4,128]{2,1,0:T(4,128)S(1)} %reshape.252.refs_0_), channel_id=1, source_target_pairs={{0,4},{2,6},{4,0},{6,2},{8,12},{10,14},{12,8},{14,10},{16,20},{18,... | collective-permute-start | bytes 6291464 | tf_op jit(solution)/shard_map/ppermute | solution.py:274
  41.5 44.6 %copy-start.7 = (f32[32]{0:T(128)S(1)}, f32[32]{0:T(128)}, u32[]{:S(2)}) copy-start(f32[32]{0:T(128)} %param.13) | copy-start | bytes 388
  41.5 44.7 %copy-start.4 = (f32[512]{0:T(512)S(1)}, f32[512]{0:T(512)}, u32[]{:S(2)}) copy-start(f32[512]{0:T(512)} %param.15) | copy-start | bytes 6148
  41.5 44.7 %copy-start.5 = (f32[512]{0:T(512)S(1)}, f32[512]{0:T(512)}, u32[]{:S(2)}) copy-start(f32[512]{0:T(512)} %param.14) | copy-start | bytes 6148
  41.5 44.8 %copy-start.3 = (f32[3,512]{1,0:T(4,128)S(1)}, f32[3,512]{1,0:T(4,128)}, u32[]{:S(2)}) copy-start(f32[3,512]{1,0:T(4,128)} %param.12) | copy-start | bytes 18436
  86.1 4.4 %collective-permute-start.2 = (f32[1024,4,128]{2,1,0:T(4,128)}, f32[1024,4,128]{2,1,0:T(4,128)S(1)}, u32[]{:S(2)}, u32[]{:S(2)}) collective-permute-start(f32[1024,4,128]{2,1,0:T(4,128)} %collective-permute-done.1.refs_0_), channel_id=1, source_target_pairs={{0,2},{2,0},{4,6},{6,4},{8,10},{10,8},{12,14},{14,12},{16,18},{18,... | collective-permute-start | bytes 6291464 | tf_op jit(solution)/shard_map/ppermute | solution.py:278
  90.5 1.3 copy-start.1
  114.5 27.8 %copy-start.6 = (f32[3,16]{1,0:T(4,128)S(1)}, f32[3,16]{1,0:T(4,128)}, u32[]{:S(2)}) copy-start(f32[3,16]{1,0:T(4,128)} %param.11) | copy-start | bytes 580
  118.2 30.3 %all-to-all-start.1 = ((f32[16,4,256]{2,1,0:T(4,128)}), f32[16,4,256]{2,1,0:T(4,128)S(1)}, u32[]{:S(2)}, u32[]{:S(2)}) async-start(f32[16,4,256]{2,1,0:T(4,128)} %copy.77), calls=%async_computation.1 | async-start | bytes 131072 | tf_op jit(solution)/shard_map/all_to_all | solution.py:281

commit v15 on v11

--- a/solution.py
+++ b/solution.py
@@ -25,7 +25,7 @@
     return (1.0 - frac_y) * lower_pair + frac_y * upper_pair
 
 
-UNROLL = 32
+UNROLL = 64
 KBITS = 12
 
 
@@ -156,7 +156,7 @@
     rows = n_ref.shape[0]
     width = d_ref.shape[0] // rows
     half = width // 2
-    step = 8 if width % 8 == 0 else 2
+    step = 16 if width % 16 == 0 else 2
     for row in range(rows):
         def body(i, carry, row=row):
             for u in range(step):

time: 185 us -> 172 us (0.930)
  starting transfers between devices: 57.3 us -> 42.3 us
    all_to_all x1, starting transfers between devices: 49.4 us -> 34.4 us  [body(): lax.all_to_all(sampled, 'stn', split_axis=0, concat_axis=0, tiled=True)]
    pallas_call x1, Pallas kernels: 34.1 us -> 36.2 us  [interpolate_balanced(): pl.pallas_call(_balanced_kernel, grid_spec=pltpu.PrefetchScalarGridSpec(n...]
  transfers between devices with their start and end apart: 3 -> 3, of which waited for: 2 -> 2; matrix products, arithmetic and copies ran while one was open for 3% -> 4% of each run, Pallas kernels for 0% -> 0%
where the time goes in v15:
time: 172 us
  Pallas kernels  47.6 us (28%)
  starting transfers between devices  42.3 us (25%)
  blocking collectives  41 us (24%)
  other arithmetic  17.4 us (10%)
  local copies, waits for them, and re-layouts  11.7 us (7%)
  waiting for transfers between devices  10.7 us (6%)
    pallas_call x1, Pallas kernels, interpolate_balanced(): pl.pallas_call(_balanced_kernel, grid_spec=pltpu.PrefetchScalarGridSpec(n...  36.2 us
    all_to_all x1, starting transfers between devices, body(): lax.all_to_all(sampled, 'stn', split_axis=0, concat_axis=0, tiled=True)  34.4 us
    all_gather x1, blocking collectives, body(): gathered = lax.all_gather(packed, 'stn', axis=0, tiled=True)  19.8 us
    all_to_all x1, blocking collectives, body(): lax.all_to_all(visible.astype(jnp.bfloat16), 'stn', split_axis=2, concat_...  16.9 us
    pallas_call x1, Pallas kernels, scatter_kernel(): pl.pallas_call(_scatter_kernel, grid_spec=pltpu.PrefetchScalarGridSpec(nu...  11.4 us
    all_to_all x1, starting transfers between devices, body(): lax.all_to_all(send, 'stn', split_axis=1, concat_axis=1, tiled=True)  7.39 us
    all_to_all x1, waiting for transfers between devices, body(): lax.all_to_all(sampled, 'stn', split_axis=0, concat_axis=0, tiled=True)  5.44 us
    all_to_all x1, waiting for transfers between devices, body(): lax.all_to_all(send, 'stn', split_axis=1, concat_axis=1, tiled=True)  5.22 us
  transfers between devices with their start and end apart: 3, of which 2 were waited for; matrix products, arithmetic and copies ran while one was open for 4% of the time, Pallas kernels for 0%

profile of v15, /device:TPU:0, one launch (start us, length us, event | category | flops | bytes accessed | tf_op | source)
XLA Modules:
  0.0 171.8 jit_solution(12275422427549407244)
XLA Ops:
  0.0 1.2 copy.71
  1.2 0.9 broadcast_compare_fusion
  2.1 0.3 copy.70
  2.4 0.2 ge.18
  2.6 0.7 broadcast_select_fusion
  3.3 0.8 fusion.15
  4.1 0.3 copy.72
  4.4 0.2 copy.73
  4.6 0.1 pad_maximum_fusion
  4.7 1.0 copy.74
  5.7 7.4 %all-to-all-start = ((f32[2,16,2,512]{3,2,0,1:T(2,128)}), f32[2,16,2,512]{3,2,0,1:T(2,128)S(1)}, u32[]{:S(2)}, u32[]{:S(2)}) async-start(f32[2,16,2,512]{3,2,0,1:T(2,128)} %copy.74), calls=%async_computation | async-start | bytes 262144 | tf_op jit(solution)/shard_map/all_to_all | solution.py:239
  13.1 0.0 copy-start.4
  13.1 0.0 copy-start.2
  13.1 1.9 %reshape.244.own_ref = f32[1024,4,128]{2,1,0:T(4,128)S(1)} reshape(f32[2,512,512]{2,1,0:T(8,128)} %param.8) | data formatting | bytes 4194304 | tf_op jit(solution)/shard_map/reshape | solution.py:242
  15.1 0.5 collective-permute-start
  15.5 0.1 fusion.14
  15.6 0.1 multiply_multiply_fusion
  15.7 5.2 %all-to-all-done = f32[2,16,2,512]{3,2,0,1:T(2,128)S(1)} async-done(((f32[2,16,2,512]{3,2,0,1:T(2,128)}), f32[2,16,2,512]{3,2,0,1:T(2,128)S(1)}, u32[]{:S(2)}, u32[]{:S(2)}) %all-to-all-start) | async-done | bytes 131104 | tf_op jit(solution)/shard_map/all_to_all | solution.py:239
  21.0 0.1 copy.85
  21.1 0.1 copy.86
  21.2 0.1 clamp_subtract_fusion
  21.3 0.1 shift-left_or_fusion
  21.5 0.6 copy.84
  22.1 0.6 reshape.243.n_ref
  22.7 0.8 pad_maximum_fusion.1.c_ref
  23.5 36.2 %shard_map.82 = f32[16384,1]{1,0:T(8,128)} custom-call(s32[32]{0:T(128)} %reshape.243.n_ref, s32[16384]{0:T(1024)} %bitcast.41, f32[2,16384]{1,0:T(2,128)} %pad_maximum_fusion.1.c_ref, f32[1024,4,128]{2,1,0:T(4,128)} %copy-done, f32[1024,4,128]{2,1,0:T(4,128)} %collective-permute-done.partner_ref), custom_call_target="tpu_custom_call" | custom-call | tf_op jit(solution)/shard_map/pallas_call | solution.py:142
  59.7 4.6 %reduce.2 = f32[16384]{0:T(1024)S(1)} reduce(f32[16384,1]{1,0:T(8,128)} %shard_map.82, f32[]{:T(128)} %constant.38), dimensions={1}, to_apply=%pallas_call.6.reduce_sub_computation | reduce | bytes 131076 | tf_op jit(solution)/shard_map/pallas_call | solution.py:142
  64.4 0.7 copy.78
  65.0 34.4 %all-to-all-start.1 = ((f32[16,2,512]{2,1,0:T(2,128)}), f32[16,2,512]{2,1,0:T(2,128)S(1)}, u32[]{:S(2)}, u32[]{:S(2)}) async-start(f32[16,2,512]{2,1,0:T(2,128)} %copy.78), calls=%async_computation.1 | async-start | bytes 131072 | tf_op jit(solution)/shard_map/all_to_all | solution.py:245
  99.5 0.6 copy.83
  100.2 0.1 copy.79
  100.3 0.7 convert_reduce_fusion.1.n_ref
  100.9 5.4 %all-to-all-done.1 = f32[16,2,512]{2,1,0:T(2,128)S(1)} async-done(((f32[16,2,512]{2,1,0:T(2,128)}), f32[16,2,512]{2,1,0:T(2,128)S(1)}, u32[]{:S(2)}, u32[]{:S(2)}) %all-to-all-start.1) | async-done | bytes 65568 | tf_op jit(solution)/shard_map/all_to_all | solution.py:245
  106.4 0.6 copy.87
  107.0 11.4 %shard_map.83 = f32[4097]{0:T(1024)} custom-call(s32[16]{0:T(128)} %convert_reduce_fusion.1.n_ref, s32[16384]{0:T(1024)} %bitcast.45, f32[16384]{0:T(1024)} %bitcast.46), custom_call_target="tpu_custom_call" | custom-call | tf_op jit(solution)/shard_map/pallas_call | solution.py:174
  118.5 0.7 slice.67
  119.2 4.4 %all_gather.6 = f32[16,512]{1,0:T(8,128)S(1)} all-gather(f32[16,256]{1,0:T(8,128)S(1)} %reshape.247), channel_id=1, replica_groups=mesh['stn'=16,'chan'=2] {'chan'}, dimensions={1}, use_global_device_ids=true | all-gather | bytes 49152 | tf_op jit(solution)/shard_map/all_gather | solution.py:254
  123.6 19.8 %all_gather.7 = f32[256,515]{1,0:T(8,128)S(1)} all-gather(f32[16,515]{1,0:T(8,128)S(1)} %pad_maximum_fusion.2), channel_id=1, replica_groups=mesh['stn'=16,'chan'=2] {'stn'}, dimensions={0}, use_global_device_ids=true | all-gather | bytes 560320 | tf_op jit(solution)/shard_map/all_gather | solution.py:256
  143.4 0.3 slice_reduce_fusion.2
  143.6 0.1 slice.71
  143.7 0.2 multiply_add_fusion
  143.9 3.9 %multiply_convert_fusion = (bf16[256,2,512]{2,0,1:T(8,128)(2,1)S(1)}, bf16[256,2,512]{2,0,1:T(8,128)(2,1)S(1)}) fusion(f32[2,512]{1,0:T(2,128)S(1)} %multiply_multiply_fusion, f32[2]{0:T(128)S(1)} %get-tuple-element.14, f32[256,512]{1,0:T(8,128)S(1)} %slice.71, f32[256,512]{1,0:T(8,128)S(1)} %multiply_add_fusion, f32[2]{0:T(128)S(1)} %broadcast_multiply_fusion), kind=kLoop, calls=%fused_computation.16 | loop fusion | flops 1835008 | bytes 2101264 | tf_op jit(solution)/shard_map/convert_element_type | solution.py:209
  147.8 3.9 %fusion.13 = (bf16[256,2,512]{2,0,1:T(8,128)(2,1)S(1)}, bf16[256,2,512]{2,0,1:T(8,128)(2,1)S(1)}, bf16[256,2,512]{2,0,1:T(8,128)(2,1)S(1)}) fusion(f32[2,512]{1,0:T(2,128)S(1)} %multiply_multiply_fusion, f32[2]{0:T(128)S(1)} %get-tuple-element.14, f32[256,512]{1,0:T(8,128)S(1)} %slice.71, f32[256,512]{1,0:T(8,128)S(1)} %multiply_add_fusion, ...), kind=kLoop, calls=%fused_computation.40 | loop fusion | flops 2621440 | bytes 2625552 | tf_op jit(solution)/shard_map/neg | solution.py:211
  151.7 0.7 fusion
  152.5 0.9 fusion.11
  153.4 16.9 %all_to_all.19 = bf16[2,2,256,256]{3,1,0,2:T(2,128)(2,1)S(1)} all-to-all(bf16[2,2,256,256]{3,1,0,2:T(2,128)(2,1)S(1)} %fusion.11), channel_id=1, replica_groups=mesh['stn'=16,'chan'=2] {'stn'}, dimensions={2} | all-to-all | bytes 1048576 | tf_op jit(solution)/shard_map/all_to_all | solution.py:269
  170.2 0.4 convert_bitcast_fusion
  170.7 1.2 copy.81
  (22 shorter events, 0.2 us)
Async XLA Ops:
  5.7 15.3 %all-to-all-start = ((f32[2,16,2,512]{3,2,0,1:T(2,128)}), f32[2,16,2,512]{3,2,0,1:T(2,128)S(1)}, u32[]{:S(2)}, u32[]{:S(2)}) async-start(f32[2,16,2,512]{3,2,0,1:T(2,128)} %copy.74), calls=%async_computation | async-start | bytes 262144 | tf_op jit(solution)/shard_map/all_to_all | solution.py:239
  13.1 2.5 %copy-start.6 = (f32[32]{0:T(128)S(1)}, f32[32]{0:T(128)}, u32[]{:S(2)}) copy-start(f32[32]{0:T(128)} %param.13) | copy-start | bytes 388
  13.1 2.6 %copy-start.3 = (f32[512]{0:T(512)S(1)}, f32[512]{0:T(512)}, u32[]{:S(2)}) copy-start(f32[512]{0:T(512)} %param.15) | copy-start | bytes 6148
  13.1 2.5 %copy-start.4 = (f32[512]{0:T(512)S(1)}, f32[512]{0:T(512)}, u32[]{:S(2)}) copy-start(f32[512]{0:T(512)} %param.14) | copy-start | bytes 6148
  13.1 2.6 %copy-start.2 = (f32[3,512]{1,0:T(4,128)S(1)}, f32[3,512]{1,0:T(4,128)}, u32[]{:S(2)}) copy-start(f32[3,512]{1,0:T(4,128)} %param.12) | copy-start | bytes 18436
  15.1 8.4 %copy-start = (f32[1024,4,128]{2,1,0:T(4,128)}, f32[1024,4,128]{2,1,0:T(4,128)S(1)}, u32[]{:S(2)}) copy-start(f32[1024,4,128]{2,1,0:T(4,128)S(1)} %reshape.244.own_ref) | copy-start | bytes 6291460
  15.1 8.4 %collective-permute-start = (f32[1024,4,128]{2,1,0:T(4,128)S(1)}, f32[1024,4,128]{2,1,0:T(4,128)}, u32[]{:S(2)}, u32[]{:S(2)}) collective-permute-start(f32[1024,4,128]{2,1,0:T(4,128)S(1)} %reshape.244.own_ref), channel_id=1, source_target_pairs={{0,2},{2,0},{4,6},{6,4},{8,10},{10,8},{12,14},{14,12},{16,18},{18,... | collective-permute-start | bytes 6291464 | tf_op jit(solution)/shard_map/ppermute | solution.py:243
  59.7 39.8 %copy-start.1 = (s32[1,1,16,1024]{3,2,1,0:T(8,128)S(1)}, s32[1,1,16,1024]{3,2,1,0:T(8,128)}, u32[]{:S(2)}) copy-start(s32[1,1,16,1024]{3,2,1,0:T(8,128)} %param.10) | copy-start | bytes 196612
  59.7 40.5 %copy-start.5 = (f32[3,16]{1,0:T(4,128)S(1)}, f32[3,16]{1,0:T(4,128)}, u32[]{:S(2)}) copy-start(f32[3,16]{1,0:T(4,128)} %param.11) | copy-start | bytes 580
  65.0 41.3 %all-to-all-start.1 = ((f32[16,2,512]{2,1,0:T(2,128)}), f32[16,2,512]{2,1,0:T(2,128)S(1)}, u32[]{:S(2)}, u32[]{:S(2)}) async-start(f32[16,2,512]{2,1,0:T(2,128)} %copy.78), calls=%async_computation.1 | async-start | bytes 131072 | tf_op jit(solution)/shard_map/all_to_all | solution.py:245

commit v16 on v15

--- a/solution.py
+++ b/solution.py
@@ -25,7 +25,7 @@
     return (1.0 - frac_y) * lower_pair + frac_y * upper_pair
 
 
-UNROLL = 64
+UNROLL = 128
 KBITS = 12
 
 

time: 172 us -> 171 us (level)
  starting transfers between devices: 42.3 us -> 11.3 us
  Pallas kernels: 47.6 us -> 78.5 us
    all_to_all x1, starting transfers between devices: 34.4 us -> 3.49 us  [body(): lax.all_to_all(sampled, 'stn', split_axis=0, concat_axis=0, tiled=True)]
    pallas_call x1, Pallas kernels: 36.2 us -> 67 us  [interpolate_balanced(): pl.pallas_call(_balanced_kernel, grid_spec=pltpu.PrefetchScalarGridSpec(n...]
where the time goes in v16:
time: 171 us; the launch traced here: 172 us
  Pallas kernels  78.5 us (46%)
  blocking collectives  40.9 us (24%)
  other arithmetic  17.4 us (10%)
  local copies, waits for them, and re-layouts  11.7 us (7%)
  starting transfers between devices  11.3 us (7%)
  waiting for transfers between devices  10.6 us (6%)
    pallas_call x1, Pallas kernels, interpolate_balanced(): pl.pallas_call(_balanced_kernel, grid_spec=pltpu.PrefetchScalarGridSpec(n...  67 us
    all_gather x1, blocking collectives, body(): gathered = lax.all_gather(packed, 'stn', axis=0, tiled=True)  19.6 us
    all_to_all x1, blocking collectives, body(): lax.all_to_all(visible.astype(jnp.bfloat16), 'stn', split_axis=2, concat_...  16.9 us
    pallas_call x1, Pallas kernels, scatter_kernel(): pl.pallas_call(_scatter_kernel, grid_spec=pltpu.PrefetchScalarGridSpec(nu...  11.5 us
    all_to_all x1, starting transfers between devices, body(): lax.all_to_all(send, 'stn', split_axis=1, concat_axis=1, tiled=True)  7.39 us
    all_to_all x1, waiting for transfers between devices, body(): lax.all_to_all(sampled, 'stn', split_axis=0, concat_axis=0, tiled=True)  5.4 us
    all_to_all x1, waiting for transfers between devices, body(): lax.all_to_all(send, 'stn', split_axis=1, concat_axis=1, tiled=True)  5.22 us
    pallas_call x1, other arithmetic, interpolate_balanced(): pl.pallas_call(_balanced_kernel, grid_spec=pltpu.PrefetchScalarGridSpec(n...  4.65 us
  transfers between devices with their start and end apart: 3, of which 2 were waited for; matrix products, arithmetic and copies ran while one was open for 4% of the time, Pallas kernels for 0%

profile of v16, /device:TPU:0, one launch (start us, length us, event | category | flops | bytes accessed | tf_op | source)
XLA Modules:
  0.0 171.6 jit_solution(4630369764184786945)
XLA Ops:
  0.0 1.2 copy.71
  1.2 0.9 broadcast_compare_fusion
  2.1 0.3 copy.70
  2.4 0.2 ge.18
  2.6 0.7 broadcast_select_fusion
  3.3 0.8 fusion.15
  4.1 0.3 copy.72
  4.4 0.2 copy.73
  4.6 0.1 pad_maximum_fusion
  4.7 1.0 copy.74
  5.7 7.4 %all-to-all-start = ((f32[2,16,2,512]{3,2,0,1:T(2,128)}), f32[2,16,2,512]{3,2,0,1:T(2,128)S(1)}, u32[]{:S(2)}, u32[]{:S(2)}) async-start(f32[2,16,2,512]{3,2,0,1:T(2,128)} %copy.74), calls=%async_computation | async-start | bytes 262144 | tf_op jit(solution)/shard_map/all_to_all | solution.py:239
  13.1 0.0 copy-start.4
  13.1 0.0 copy-start.2
  13.1 1.9 %reshape.244.own_ref = f32[1024,4,128]{2,1,0:T(4,128)S(1)} reshape(f32[2,512,512]{2,1,0:T(8,128)} %param.8) | data formatting | bytes 4194304 | tf_op jit(solution)/shard_map/reshape | solution.py:242
  15.1 0.5 collective-permute-start
  15.5 0.1 fusion.14
  15.6 0.1 multiply_multiply_fusion
  15.7 5.2 %all-to-all-done = f32[2,16,2,512]{3,2,0,1:T(2,128)S(1)} async-done(((f32[2,16,2,512]{3,2,0,1:T(2,128)}), f32[2,16,2,512]{3,2,0,1:T(2,128)S(1)}, u32[]{:S(2)}, u32[]{:S(2)}) %all-to-all-start) | async-done | bytes 131104 | tf_op jit(solution)/shard_map/all_to_all | solution.py:239
  21.0 0.1 copy.85
  21.1 0.1 copy.86
  21.2 0.1 clamp_subtract_fusion
  21.3 0.1 shift-left_or_fusion
  21.5 0.6 copy.84
  22.1 0.6 reshape.243.n_ref
  22.7 0.8 pad_maximum_fusion.1.c_ref
  23.5 67.0 %shard_map.82 = f32[16384,1]{1,0:T(8,128)} custom-call(s32[32]{0:T(128)} %reshape.243.n_ref, s32[16384]{0:T(1024)} %bitcast.41, f32[2,16384]{1,0:T(2,128)} %pad_maximum_fusion.1.c_ref, f32[1024,4,128]{2,1,0:T(4,128)} %copy-done, f32[1024,4,128]{2,1,0:T(4,128)} %collective-permute-done.partner_ref), custom_call_target="tpu_custom_call" | custom-call | tf_op jit(solution)/shard_map/pallas_call | solution.py:142
  90.5 4.6 %reduce.2 = f32[16384]{0:T(1024)S(1)} reduce(f32[16384,1]{1,0:T(8,128)} %shard_map.82, f32[]{:T(128)} %constant.38), dimensions={1}, to_apply=%pallas_call.6.reduce_sub_computation | reduce | bytes 131076 | tf_op jit(solution)/shard_map/pallas_call | solution.py:142
  95.2 0.7 copy.78
  95.8 3.5 %all-to-all-start.1 = ((f32[16,2,512]{2,1,0:T(2,128)}), f32[16,2,512]{2,1,0:T(2,128)S(1)}, u32[]{:S(2)}, u32[]{:S(2)}) async-start(f32[16,2,512]{2,1,0:T(2,128)} %copy.78), calls=%async_computation.1 | async-start | bytes 131072 | tf_op jit(solution)/shard_map/all_to_all | solution.py:245
  99.4 0.6 copy.83
  100.0 0.1 copy.79
  100.1 0.7 convert_reduce_fusion.1.n_ref
  100.8 5.4 %all-to-all-done.1 = f32[16,2,512]{2,1,0:T(2,128)S(1)} async-done(((f32[16,2,512]{2,1,0:T(2,128)}), f32[16,2,512]{2,1,0:T(2,128)S(1)}, u32[]{:S(2)}, u32[]{:S(2)}) %all-to-all-start.1) | async-done | bytes 65568 | tf_op jit(solution)/shard_map/all_to_all | solution.py:245
  106.2 0.6 copy.87
  106.8 11.5 %shard_map.83 = f32[4097]{0:T(1024)} custom-call(s32[16]{0:T(128)} %convert_reduce_fusion.1.n_ref, s32[16384]{0:T(1024)} %bitcast.45, f32[16384]{0:T(1024)} %bitcast.46), custom_call_target="tpu_custom_call" | custom-call | tf_op jit(solution)/shard_map/pallas_call | solution.py:174
  118.4 0.7 slice.67
  119.1 4.4 %all_gather.6 = f32[16,512]{1,0:T(8,128)S(1)} all-gather(f32[16,256]{1,0:T(8,128)S(1)} %reshape.247), channel_id=1, replica_groups=mesh['stn'=16,'chan'=2] {'chan'}, dimensions={1}, use_global_device_ids=true | all-gather | bytes 49152 | tf_op jit(solution)/shard_map/all_gather | solution.py:254
  123.5 19.6 %all_gather.7 = f32[256,515]{1,0:T(8,128)S(1)} all-gather(f32[16,515]{1,0:T(8,128)S(1)} %pad_maximum_fusion.2), channel_id=1, replica_groups=mesh['stn'=16,'chan'=2] {'stn'}, dimensions={0}, use_global_device_ids=true | all-gather | bytes 560320 | tf_op jit(solution)/shard_map/all_gather | solution.py:256
  143.1 0.3 slice_reduce_fusion.2
  143.4 0.1 slice.71
  143.5 0.2 multiply_add_fusion
  143.6 3.9 %multiply_convert_fusion = (bf16[256,2,512]{2,0,1:T(8,128)(2,1)S(1)}, bf16[256,2,512]{2,0,1:T(8,128)(2,1)S(1)}) fusion(f32[2,512]{1,0:T(2,128)S(1)} %multiply_multiply_fusion, f32[2]{0:T(128)S(1)} %get-tuple-element.14, f32[256,512]{1,0:T(8,128)S(1)} %slice.71, f32[256,512]{1,0:T(8,128)S(1)} %multiply_add_fusion, f32[2]{0:T(128)S(1)} %broadcast_multiply_fusion), kind=kLoop, calls=%fused_computation.16 | loop fusion | flops 1835008 | bytes 2101264 | tf_op jit(solution)/shard_map/convert_element_type | solution.py:209
  147.6 3.9 %fusion.13 = (bf16[256,2,512]{2,0,1:T(8,128)(2,1)S(1)}, bf16[256,2,512]{2,0,1:T(8,128)(2,1)S(1)}, bf16[256,2,512]{2,0,1:T(8,128)(2,1)S(1)}) fusion(f32[2,512]{1,0:T(2,128)S(1)} %multiply_multiply_fusion, f32[2]{0:T(128)S(1)} %get-tuple-element.14, f32[256,512]{1,0:T(8,128)S(1)} %slice.71, f32[256,512]{1,0:T(8,128)S(1)} %multiply_add_fusion, ...), kind=kLoop, calls=%fused_computation.40 | loop fusion | flops 2621440 | bytes 2625552 | tf_op jit(solution)/shard_map/neg | solution.py:211
  151.5 0.7 fusion
  152.3 0.9 fusion.11
  153.1 16.9 %all_to_all.19 = bf16[2,2,256,256]{3,1,0,2:T(2,128)(2,1)S(1)} all-to-all(bf16[2,2,256,256]{3,1,0,2:T(2,128)(2,1)S(1)} %fusion.11), channel_id=1, replica_groups=mesh['stn'=16,'chan'=2] {'stn'}, dimensions={2} | all-to-all | bytes 1048576 | tf_op jit(solution)/shard_map/all_to_all | solution.py:269
  170.0 0.4 convert_bitcast_fusion
  170.5 1.2 copy.81
  (22 shorter events, 0.2 us)
Async XLA Ops:
  5.7 15.3 %all-to-all-start = ((f32[2,16,2,512]{3,2,0,1:T(2,128)}), f32[2,16,2,512]{3,2,0,1:T(2,128)S(1)}, u32[]{:S(2)}, u32[]{:S(2)}) async-start(f32[2,16,2,512]{3,2,0,1:T(2,128)} %copy.74), calls=%async_computation | async-start | bytes 262144 | tf_op jit(solution)/shard_map/all_to_all | solution.py:239
  13.1 2.5 %copy-start.6 = (f32[32]{0:T(128)S(1)}, f32[32]{0:T(128)}, u32[]{:S(2)}) copy-start(f32[32]{0:T(128)} %param.13) | copy-start | bytes 388
  13.1 2.6 %copy-start.3 = (f32[512]{0:T(512)S(1)}, f32[512]{0:T(512)}, u32[]{:S(2)}) copy-start(f32[512]{0:T(512)} %param.15) | copy-start | bytes 6148
  13.1 2.5 %copy-start.4 = (f32[512]{0:T(512)S(1)}, f32[512]{0:T(512)}, u32[]{:S(2)}) copy-start(f32[512]{0:T(512)} %param.14) | copy-start | bytes 6148
  13.1 2.6 %copy-start.2 = (f32[3,512]{1,0:T(4,128)S(1)}, f32[3,512]{1,0:T(4,128)}, u32[]{:S(2)}) copy-start(f32[3,512]{1,0:T(4,128)} %param.12) | copy-start | bytes 18436
  15.1 8.4 %copy-start = (f32[1024,4,128]{2,1,0:T(4,128)}, f32[1024,4,128]{2,1,0:T(4,128)S(1)}, u32[]{:S(2)}) copy-start(f32[1024,4,128]{2,1,0:T(4,128)S(1)} %reshape.244.own_ref) | copy-start | bytes 6291460
  15.1 8.4 %collective-permute-start = (f32[1024,4,128]{2,1,0:T(4,128)S(1)}, f32[1024,4,128]{2,1,0:T(4,128)}, u32[]{:S(2)}, u32[]{:S(2)}) collective-permute-start(f32[1024,4,128]{2,1,0:T(4,128)S(1)} %reshape.244.own_ref), channel_id=1, source_target_pairs={{0,2},{2,0},{4,6},{6,4},{8,10},{10,8},{12,14},{14,12},{16,18},{18,... | collective-permute-start | bytes 6291464 | tf_op jit(solution)/shard_map/ppermute | solution.py:243
  90.5 8.9 %copy-start.1 = (s32[1,1,16,1024]{3,2,1,0:T(8,128)S(1)}, s32[1,1,16,1024]{3,2,1,0:T(8,128)}, u32[]{:S(2)}) copy-start(s32[1,1,16,1024]{3,2,1,0:T(8,128)} %param.10) | copy-start | bytes 196612
  90.5 9.5 %copy-start.5 = (f32[3,16]{1,0:T(4,128)S(1)}, f32[3,16]{1,0:T(4,128)}, u32[]{:S(2)}) copy-start(f32[3,16]{1,0:T(4,128)} %param.11) | copy-start | bytes 580
  95.8 10.4 %all-to-all-start.1 = ((f32[16,2,512]{2,1,0:T(2,128)}), f32[16,2,512]{2,1,0:T(2,128)S(1)}, u32[]{:S(2)}, u32[]{:S(2)}) async-start(f32[16,2,512]{2,1,0:T(2,128)} %copy.78), calls=%async_computation.1 | async-start | bytes 131072 | tf_op jit(solution)/shard_map/all_to_all | solution.py:245

commit v17 on v16

--- a/solution.py
+++ b/solution.py
@@ -25,7 +25,7 @@
     return (1.0 - frac_y) * lower_pair + frac_y * upper_pair
 
 
-UNROLL = 128
+UNROLL = 256
 KBITS = 12
 
 

time: 171 us -> 172 us (level)
  Pallas kernels: 78.5 us -> 60.4 us
  starting transfers between devices: 11.3 us -> 28.6 us
    pallas_call x1, Pallas kernels: 67 us -> 48.9 us  [interpolate_balanced(): pl.pallas_call(_balanced_kernel, grid_spec=pltpu.PrefetchScalarGridSpec(n...]
    all_to_all x1, starting transfers between devices: 3.49 us -> 20.8 us  [body(): lax.all_to_all(sampled, 'stn', split_axis=0, concat_axis=0, tiled=True)]
where the time goes in v17:
time: 172 us; the launch traced here: 171 us
  Pallas kernels  60.4 us (35%)
  blocking collectives  41 us (24%)
  starting transfers between devices  28.6 us (17%)
  other arithmetic  17.4 us (10%)
  local copies, waits for them, and re-layouts  11.7 us (7%)
  waiting for transfers between devices  10.7 us (6%)
    pallas_call x1, Pallas kernels, interpolate_balanced(): pl.pallas_call(_balanced_kernel, grid_spec=pltpu.PrefetchScalarGridSpec(n...  48.9 us
    all_to_all x1, starting transfers between devices, body(): lax.all_to_all(sampled, 'stn', split_axis=0, concat_axis=0, tiled=True)  20.8 us
    all_gather x1, blocking collectives, body(): gathered = lax.all_gather(packed, 'stn', axis=0, tiled=True)  19.7 us
    all_to_all x1, blocking collectives, body(): lax.all_to_all(visible.astype(jnp.bfloat16), 'stn', split_axis=2, concat_...  16.9 us
    pallas_call x1, Pallas kernels, scatter_kernel(): pl.pallas_call(_scatter_kernel, grid_spec=pltpu.PrefetchScalarGridSpec(nu...  11.6 us
    all_to_all x1, starting transfers between devices, body(): lax.all_to_all(send, 'stn', split_axis=1, concat_axis=1, tiled=True)  7.39 us
    all_to_all x1, waiting for transfers between devices, body(): lax.all_to_all(sampled, 'stn', split_axis=0, concat_axis=0, tiled=True)  5.44 us
    all_to_all x1, waiting for transfers between devices, body(): lax.all_to_all(send, 'stn', split_axis=1, concat_axis=1, tiled=True)  5.22 us
  transfers between devices with their start and end apart: 3, of which 2 were waited for; matrix products, arithmetic and copies ran while one was open for 4% of the time, Pallas kernels for 0%

profile of v17, /device:TPU:0, one launch (start us, length us, event | category | flops | bytes accessed | tf_op | source)
XLA Modules:
  0.0 170.9 jit_solution(16842417377274864644)
XLA Ops:
  0.0 1.2 copy.71
  1.2 0.9 broadcast_compare_fusion
  2.1 0.3 copy.70
  2.4 0.2 ge.18
  2.6 0.7 broadcast_select_fusion
  3.3 0.8 fusion.15
  4.1 0.3 copy.72
  4.4 0.2 copy.73
  4.6 0.1 pad_maximum_fusion
  4.7 1.0 copy.74
  5.7 7.4 %all-to-all-start = ((f32[2,16,2,512]{3,2,0,1:T(2,128)}), f32[2,16,2,512]{3,2,0,1:T(2,128)S(1)}, u32[]{:S(2)}, u32[]{:S(2)}) async-start(f32[2,16,2,512]{3,2,0,1:T(2,128)} %copy.74), calls=%async_computation | async-start | bytes 262144 | tf_op jit(solution)/shard_map/all_to_all | solution.py:239
  13.1 0.0 copy-start.3
  13.1 0.0 copy-start.4
  13.1 1.9 %reshape.244.own_ref = f32[1024,4,128]{2,1,0:T(4,128)S(1)} reshape(f32[2,512,512]{2,1,0:T(8,128)} %param.8) | data formatting | bytes 4194304 | tf_op jit(solution)/shard_map/reshape | solution.py:242
  15.1 0.5 collective-permute-start
  15.5 0.1 fusion.14
  15.6 0.1 multiply_multiply_fusion
  15.7 5.2 %all-to-all-done = f32[2,16,2,512]{3,2,0,1:T(2,128)S(1)} async-done(((f32[2,16,2,512]{3,2,0,1:T(2,128)}), f32[2,16,2,512]{3,2,0,1:T(2,128)S(1)}, u32[]{:S(2)}, u32[]{:S(2)}) %all-to-all-start) | async-done | bytes 131104 | tf_op jit(solution)/shard_map/all_to_all | solution.py:239
  21.0 0.1 copy.85
  21.1 0.1 copy.86
  21.2 0.1 clamp_subtract_fusion
  21.3 0.1 shift-left_or_fusion
  21.5 0.6 copy.84
  22.1 0.6 reshape.243.n_ref
  22.7 0.8 pad_maximum_fusion.1.c_ref
  23.5 48.9 %shard_map.82 = f32[16384,1]{1,0:T(8,128)} custom-call(s32[32]{0:T(128)} %reshape.243.n_ref, s32[16384]{0:T(1024)} %bitcast.41, f32[2,16384]{1,0:T(2,128)} %pad_maximum_fusion.1.c_ref, f32[1024,4,128]{2,1,0:T(4,128)} %copy-done, f32[1024,4,128]{2,1,0:T(4,128)} %collective-permute-done.partner_ref), custom_call_target="tpu_custom_call" | custom-call | tf_op jit(solution)/shard_map/pallas_call | solution.py:142
  72.4 4.6 %reduce.2 = f32[16384]{0:T(1024)S(1)} reduce(f32[16384,1]{1,0:T(8,128)} %shard_map.82, f32[]{:T(128)} %constant.38), dimensions={1}, to_apply=%pallas_call.6.reduce_sub_computation | reduce | bytes 131076 | tf_op jit(solution)/shard_map/pallas_call | solution.py:142
  77.0 0.7 copy.78
  77.7 20.8 %all-to-all-start.1 = ((f32[16,2,512]{2,1,0:T(2,128)}), f32[16,2,512]{2,1,0:T(2,128)S(1)}, u32[]{:S(2)}, u32[]{:S(2)}) async-start(f32[16,2,512]{2,1,0:T(2,128)} %copy.78), calls=%async_computation.1 | async-start | bytes 131072 | tf_op jit(solution)/shard_map/all_to_all | solution.py:245
  98.6 0.6 copy.83
  99.2 0.1 copy.79
  99.3 0.7 convert_reduce_fusion.1.n_ref
  100.0 5.4 %all-to-all-done.1 = f32[16,2,512]{2,1,0:T(2,128)S(1)} async-done(((f32[16,2,512]{2,1,0:T(2,128)}), f32[16,2,512]{2,1,0:T(2,128)S(1)}, u32[]{:S(2)}, u32[]{:S(2)}) %all-to-all-start.1) | async-done | bytes 65568 | tf_op jit(solution)/shard_map/all_to_all | solution.py:245
  105.4 0.6 copy.87
  106.0 11.6 %shard_map.83 = f32[4097]{0:T(1024)} custom-call(s32[16]{0:T(128)} %convert_reduce_fusion.1.n_ref, s32[16384]{0:T(1024)} %bitcast.45, f32[16384]{0:T(1024)} %bitcast.46), custom_call_target="tpu_custom_call" | custom-call | tf_op jit(solution)/shard_map/pallas_call | solution.py:174
  117.6 0.7 slice.67
  118.3 4.4 %all_gather.6 = f32[16,512]{1,0:T(8,128)S(1)} all-gather(f32[16,256]{1,0:T(8,128)S(1)} %reshape.247), channel_id=1, replica_groups=mesh['stn'=16,'chan'=2] {'chan'}, dimensions={1}, use_global_device_ids=true | all-gather | bytes 49152 | tf_op jit(solution)/shard_map/all_gather | solution.py:254
  122.7 19.7 %all_gather.7 = f32[256,515]{1,0:T(8,128)S(1)} all-gather(f32[16,515]{1,0:T(8,128)S(1)} %pad_maximum_fusion.2), channel_id=1, replica_groups=mesh['stn'=16,'chan'=2] {'stn'}, dimensions={0}, use_global_device_ids=true | all-gather | bytes 560320 | tf_op jit(solution)/shard_map/all_gather | solution.py:256
  142.4 0.3 slice_reduce_fusion.2
  142.7 0.1 slice.71
  142.8 0.2 multiply_add_fusion
  142.9 3.9 %multiply_convert_fusion = (bf16[256,2,512]{2,0,1:T(8,128)(2,1)S(1)}, bf16[256,2,512]{2,0,1:T(8,128)(2,1)S(1)}) fusion(f32[2,512]{1,0:T(2,128)S(1)} %multiply_multiply_fusion, f32[2]{0:T(128)S(1)} %get-tuple-element.14, f32[256,512]{1,0:T(8,128)S(1)} %slice.71, f32[256,512]{1,0:T(8,128)S(1)} %multiply_add_fusion, f32[2]{0:T(128)S(1)} %broadcast_multiply_fusion), kind=kLoop, calls=%fused_computation.16 | loop fusion | flops 1835008 | bytes 2101264 | tf_op jit(solution)/shard_map/convert_element_type | solution.py:209
  146.9 3.9 %fusion.13 = (bf16[256,2,512]{2,0,1:T(8,128)(2,1)S(1)}, bf16[256,2,512]{2,0,1:T(8,128)(2,1)S(1)}, bf16[256,2,512]{2,0,1:T(8,128)(2,1)S(1)}) fusion(f32[2,512]{1,0:T(2,128)S(1)} %multiply_multiply_fusion, f32[2]{0:T(128)S(1)} %get-tuple-element.14, f32[256,512]{1,0:T(8,128)S(1)} %slice.71, f32[256,512]{1,0:T(8,128)S(1)} %multiply_add_fusion, ...), kind=kLoop, calls=%fused_computation.40 | loop fusion | flops 2621440 | bytes 2625552 | tf_op jit(solution)/shard_map/neg | solution.py:211
  150.8 0.7 fusion
  151.6 0.9 fusion.11
  152.4 16.9 %all_to_all.19 = bf16[2,2,256,256]{3,1,0,2:T(2,128)(2,1)S(1)} all-to-all(bf16[2,2,256,256]{3,1,0,2:T(2,128)(2,1)S(1)} %fusion.11), channel_id=1, replica_groups=mesh['stn'=16,'chan'=2] {'stn'}, dimensions={2} | all-to-all | bytes 1048576 | tf_op jit(solution)/shard_map/all_to_all | solution.py:269
  169.3 0.4 convert_bitcast_fusion
  169.8 1.2 copy.81
  (22 shorter events, 0.2 us)
Async XLA Ops:
  5.7 15.3 %all-to-all-start = ((f32[2,16,2,512]{3,2,0,1:T(2,128)}), f32[2,16,2,512]{3,2,0,1:T(2,128)S(1)}, u32[]{:S(2)}, u32[]{:S(2)}) async-start(f32[2,16,2,512]{3,2,0,1:T(2,128)} %copy.74), calls=%async_computation | async-start | bytes 262144 | tf_op jit(solution)/shard_map/all_to_all | solution.py:239
  13.1 2.5 %copy-start.6 = (f32[32]{0:T(128)S(1)}, f32[32]{0:T(128)}, u32[]{:S(2)}) copy-start(f32[32]{0:T(128)} %param.13) | copy-start | bytes 388
  13.1 2.6 %copy-start.3 = (f32[512]{0:T(512)S(1)}, f32[512]{0:T(512)}, u32[]{:S(2)}) copy-start(f32[512]{0:T(512)} %param.15) | copy-start | bytes 6148
  13.1 2.5 %copy-start.4 = (f32[512]{0:T(512)S(1)}, f32[512]{0:T(512)}, u32[]{:S(2)}) copy-start(f32[512]{0:T(512)} %param.14) | copy-start | bytes 6148
  13.1 2.6 %copy-start.2 = (f32[3,512]{1,0:T(4,128)S(1)}, f32[3,512]{1,0:T(4,128)}, u32[]{:S(2)}) copy-start(f32[3,512]{1,0:T(4,128)} %param.12) | copy-start | bytes 18436
  15.1 8.4 %copy-start = (f32[1024,4,128]{2,1,0:T(4,128)}, f32[1024,4,128]{2,1,0:T(4,128)S(1)}, u32[]{:S(2)}) copy-start(f32[1024,4,128]{2,1,0:T(4,128)S(1)} %reshape.244.own_ref) | copy-start | bytes 6291460
  15.1 8.4 %collective-permute-start = (f32[1024,4,128]{2,1,0:T(4,128)S(1)}, f32[1024,4,128]{2,1,0:T(4,128)}, u32[]{:S(2)}, u32[]{:S(2)}) collective-permute-start(f32[1024,4,128]{2,1,0:T(4,128)S(1)} %reshape.244.own_ref), channel_id=1, source_target_pairs={{0,2},{2,0},{4,6},{6,4},{8,10},{10,8},{12,14},{14,12},{16,18},{18,... | collective-permute-start | bytes 6291464 | tf_op jit(solution)/shard_map/ppermute | solution.py:243
  72.4 26.2 %copy-start.1 = (s32[1,1,16,1024]{3,2,1,0:T(8,128)S(1)}, s32[1,1,16,1024]{3,2,1,0:T(8,128)}, u32[]{:S(2)}) copy-start(s32[1,1,16,1024]{3,2,1,0:T(8,128)} %param.10) | copy-start | bytes 196612
  72.4 26.8 %copy-start.5 = (f32[3,16]{1,0:T(4,128)S(1)}, f32[3,16]{1,0:T(4,128)}, u32[]{:S(2)}) copy-start(f32[3,16]{1,0:T(4,128)} %param.11) | copy-start | bytes 580
  77.7 27.7 %all-to-all-start.1 = ((f32[16,2,512]{2,1,0:T(2,128)}), f32[16,2,512]{2,1,0:T(2,128)S(1)}, u32[]{:S(2)}, u32[]{:S(2)}) async-start(f32[16,2,512]{2,1,0:T(2,128)} %copy.78), calls=%async_computation.1 | async-start | bytes 131072 | tf_op jit(solution)/shard_map/all_to_all | solution.py:245

commit v18 on v16

--- a/solution.py
+++ b/solution.py
@@ -156,7 +156,7 @@
     rows = n_ref.shape[0]
     width = d_ref.shape[0] // rows
     half = width // 2
-    step = 16 if width % 16 == 0 else 2
+    step = 32 if width % 32 == 0 else 2
     for row in range(rows):
         def body(i, carry, row=row):
             for u in range(step):

time: 171 us -> 168 us (0.982)
  Pallas kernels: 78.5 us -> 75.5 us
    pallas_call x1, Pallas kernels: 67 us -> 64.4 us  [interpolate_balanced(): pl.pallas_call(_balanced_kernel, grid_spec=pltpu.PrefetchScalarGridSpec(n...]
where the time goes in v18:
time: 168 us; the launch traced here: 170 us
  Pallas kernels  75.5 us (45%)
  blocking collectives  41.9 us (25%)
  other arithmetic  17.4 us (10%)
  local copies, waits for them, and re-layouts  11.7 us (7%)
  starting transfers between devices  11.3 us (7%)
  waiting for transfers between devices  10.6 us (6%)
    pallas_call x1, Pallas kernels, interpolate_balanced(): pl.pallas_call(_balanced_kernel, grid_spec=pltpu.PrefetchScalarGridSpec(n...  64.4 us
    all_gather x1, blocking collectives, body(): gathered = lax.all_gather(packed, 'stn', axis=0, tiled=True)  19.8 us
    all_to_all x1, blocking collectives, body(): lax.all_to_all(visible.astype(jnp.bfloat16), 'stn', split_axis=2, concat_...  16.9 us
    pallas_call x1, Pallas kernels, scatter_kernel(): pl.pallas_call(_scatter_kernel, grid_spec=pltpu.PrefetchScalarGridSpec(nu...  11.1 us
    all_to_all x1, starting transfers between devices, body(): lax.all_to_all(send, 'stn', split_axis=1, concat_axis=1, tiled=True)  7.39 us
    all_to_all x1, waiting for transfers between devices, body(): lax.all_to_all(sampled, 'stn', split_axis=0, concat_axis=0, tiled=True)  5.4 us
    all_to_all x1, waiting for transfers between devices, body(): lax.all_to_all(send, 'stn', split_axis=1, concat_axis=1, tiled=True)  5.22 us
    all_gather x1, blocking collectives, body(): iono_phase = lax.all_gather(own_iono, 'chan', axis=1, tiled=True)  5.19 us
  transfers between devices with their start and end apart: 3, of which 2 were waited for; matrix products, arithmetic and copies ran while one was open for 4% of the time, Pallas kernels for 0%

profile of v18, /device:TPU:0, one launch (start us, length us, event | category | flops | bytes accessed | tf_op | source)
XLA Modules:
  0.0 169.5 jit_solution(18158787886100065538)
XLA Ops:
  0.0 1.2 copy.71
  1.2 0.9 broadcast_compare_fusion
  2.1 0.3 copy.70
  2.4 0.2 ge.18
  2.6 0.7 broadcast_select_fusion
  3.3 0.8 fusion.15
  4.1 0.3 copy.72
  4.4 0.2 copy.73
  4.6 0.1 pad_maximum_fusion
  4.7 1.0 copy.74
  5.7 7.4 %all-to-all-start = ((f32[2,16,2,512]{3,2,0,1:T(2,128)}), f32[2,16,2,512]{3,2,0,1:T(2,128)S(1)}, u32[]{:S(2)}, u32[]{:S(2)}) async-start(f32[2,16,2,512]{3,2,0,1:T(2,128)} %copy.74), calls=%async_computation | async-start | bytes 262144 | tf_op jit(solution)/shard_map/all_to_all | solution.py:239
  13.1 0.0 copy-start.6
  13.1 0.0 copy-start.2
  13.1 1.9 %reshape.244.own_ref = f32[1024,4,128]{2,1,0:T(4,128)S(1)} reshape(f32[2,512,512]{2,1,0:T(8,128)} %param.8) | data formatting | bytes 4194304 | tf_op jit(solution)/shard_map/reshape | solution.py:242
  15.1 0.5 collective-permute-start
  15.5 0.1 fusion.14
  15.6 0.1 multiply_multiply_fusion
  15.7 5.2 %all-to-all-done = f32[2,16,2,512]{3,2,0,1:T(2,128)S(1)} async-done(((f32[2,16,2,512]{3,2,0,1:T(2,128)}), f32[2,16,2,512]{3,2,0,1:T(2,128)S(1)}, u32[]{:S(2)}, u32[]{:S(2)}) %all-to-all-start) | async-done | bytes 131104 | tf_op jit(solution)/shard_map/all_to_all | solution.py:239
  21.0 0.1 copy.85
  21.1 0.1 copy.86
  21.2 0.1 clamp_subtract_fusion
  21.3 0.1 shift-left_or_fusion
  21.5 0.6 copy.84
  22.1 0.6 reshape.243.n_ref
  22.7 0.8 pad_maximum_fusion.1.c_ref
  23.5 64.4 %shard_map.82 = f32[16384,1]{1,0:T(8,128)} custom-call(s32[32]{0:T(128)} %reshape.243.n_ref, s32[16384]{0:T(1024)} %bitcast.41, f32[2,16384]{1,0:T(2,128)} %pad_maximum_fusion.1.c_ref, f32[1024,4,128]{2,1,0:T(4,128)} %copy-done, f32[1024,4,128]{2,1,0:T(4,128)} %collective-permute-done.partner_ref), custom_call_target="tpu_custom_call" | custom-call | tf_op jit(solution)/shard_map/pallas_call | solution.py:142
  87.9 4.6 %reduce.2 = f32[16384]{0:T(1024)S(1)} reduce(f32[16384,1]{1,0:T(8,128)} %shard_map.82, f32[]{:T(128)} %constant.38), dimensions={1}, to_apply=%pallas_call.6.reduce_sub_computation | reduce | bytes 131076 | tf_op jit(solution)/shard_map/pallas_call | solution.py:142
  92.5 0.7 copy.78
  93.2 3.5 %all-to-all-start.1 = ((f32[16,2,512]{2,1,0:T(2,128)}), f32[16,2,512]{2,1,0:T(2,128)S(1)}, u32[]{:S(2)}, u32[]{:S(2)}) async-start(f32[16,2,512]{2,1,0:T(2,128)} %copy.78), calls=%async_computation.1 | async-start | bytes 131072 | tf_op jit(solution)/shard_map/all_to_all | solution.py:245
  96.8 0.6 copy.83
  97.4 0.1 copy.79
  97.5 0.7 convert_reduce_fusion.1.n_ref
  98.2 5.4 %all-to-all-done.1 = f32[16,2,512]{2,1,0:T(2,128)S(1)} async-done(((f32[16,2,512]{2,1,0:T(2,128)}), f32[16,2,512]{2,1,0:T(2,128)S(1)}, u32[]{:S(2)}, u32[]{:S(2)}) %all-to-all-start.1) | async-done | bytes 65568 | tf_op jit(solution)/shard_map/all_to_all | solution.py:245
  103.6 0.6 copy.87
  104.2 11.1 %shard_map.83 = f32[4097]{0:T(1024)} custom-call(s32[16]{0:T(128)} %convert_reduce_fusion.1.n_ref, s32[16384]{0:T(1024)} %bitcast.45, f32[16384]{0:T(1024)} %bitcast.46), custom_call_target="tpu_custom_call" | custom-call | tf_op jit(solution)/shard_map/pallas_call | solution.py:174
  115.3 0.7 slice.67
  116.0 5.2 %all_gather.6 = f32[16,512]{1,0:T(8,128)S(1)} all-gather(f32[16,256]{1,0:T(8,128)S(1)} %reshape.247), channel_id=1, replica_groups=mesh['stn'=16,'chan'=2] {'chan'}, dimensions={1}, use_global_device_ids=true | all-gather | bytes 49152 | tf_op jit(solution)/shard_map/all_gather | solution.py:254
  121.2 19.8 %all_gather.7 = f32[256,515]{1,0:T(8,128)S(1)} all-gather(f32[16,515]{1,0:T(8,128)S(1)} %pad_maximum_fusion.2), channel_id=1, replica_groups=mesh['stn'=16,'chan'=2] {'stn'}, dimensions={0}, use_global_device_ids=true | all-gather | bytes 560320 | tf_op jit(solution)/shard_map/all_gather | solution.py:256
  141.0 0.3 slice_reduce_fusion.2
  141.3 0.1 slice.71
  141.4 0.2 multiply_add_fusion
  141.5 3.9 %multiply_convert_fusion = (bf16[256,2,512]{2,0,1:T(8,128)(2,1)S(1)}, bf16[256,2,512]{2,0,1:T(8,128)(2,1)S(1)}) fusion(f32[2,512]{1,0:T(2,128)S(1)} %multiply_multiply_fusion, f32[2]{0:T(128)S(1)} %get-tuple-element.14, f32[256,512]{1,0:T(8,128)S(1)} %slice.71, f32[256,512]{1,0:T(8,128)S(1)} %multiply_add_fusion, f32[2]{0:T(128)S(1)} %broadcast_multiply_fusion), kind=kLoop, calls=%fused_computation.16 | loop fusion | flops 1835008 | bytes 2101264 | tf_op jit(solution)/shard_map/convert_element_type | solution.py:209
  145.5 3.9 %fusion.13 = (bf16[256,2,512]{2,0,1:T(8,128)(2,1)S(1)}, bf16[256,2,512]{2,0,1:T(8,128)(2,1)S(1)}, bf16[256,2,512]{2,0,1:T(8,128)(2,1)S(1)}) fusion(f32[2,512]{1,0:T(2,128)S(1)} %multiply_multiply_fusion, f32[2]{0:T(128)S(1)} %get-tuple-element.14, f32[256,512]{1,0:T(8,128)S(1)} %slice.71, f32[256,512]{1,0:T(8,128)S(1)} %multiply_add_fusion, ...), kind=kLoop, calls=%fused_computation.40 | loop fusion | flops 2621440 | bytes 2625552 | tf_op jit(solution)/shard_map/neg | solution.py:211
  149.4 0.7 fusion
  150.2 0.9 fusion.11
  151.0 16.9 %all_to_all.19 = bf16[2,2,256,256]{3,1,0,2:T(2,128)(2,1)S(1)} all-to-all(bf16[2,2,256,256]{3,1,0,2:T(2,128)(2,1)S(1)} %fusion.11), channel_id=1, replica_groups=mesh['stn'=16,'chan'=2] {'stn'}, dimensions={2} | all-to-all | bytes 1048576 | tf_op jit(solution)/shard_map/all_to_all | solution.py:269
  167.9 0.4 convert_bitcast_fusion
  168.4 1.2 copy.81
  (22 shorter events, 0.2 us)
Async XLA Ops:
  5.7 15.3 %all-to-all-start = ((f32[2,16,2,512]{3,2,0,1:T(2,128)}), f32[2,16,2,512]{3,2,0,1:T(2,128)S(1)}, u32[]{:S(2)}, u32[]{:S(2)}) async-start(f32[2,16,2,512]{3,2,0,1:T(2,128)} %copy.74), calls=%async_computation | async-start | bytes 262144 | tf_op jit(solution)/shard_map/all_to_all | solution.py:239
  13.1 2.5 %copy-start.6 = (f32[32]{0:T(128)S(1)}, f32[32]{0:T(128)}, u32[]{:S(2)}) copy-start(f32[32]{0:T(128)} %param.13) | copy-start | bytes 388
  13.1 2.6 %copy-start.3 = (f32[512]{0:T(512)S(1)}, f32[512]{0:T(512)}, u32[]{:S(2)}) copy-start(f32[512]{0:T(512)} %param.15) | copy-start | bytes 6148
  13.1 2.5 %copy-start.4 = (f32[512]{0:T(512)S(1)}, f32[512]{0:T(512)}, u32[]{:S(2)}) copy-start(f32[512]{0:T(512)} %param.14) | copy-start | bytes 6148
  13.1 2.6 %copy-start.2 = (f32[3,512]{1,0:T(4,128)S(1)}, f32[3,512]{1,0:T(4,128)}, u32[]{:S(2)}) copy-start(f32[3,512]{1,0:T(4,128)} %param.12) | copy-start | bytes 18436
  15.1 8.4 %copy-start = (f32[1024,4,128]{2,1,0:T(4,128)}, f32[1024,4,128]{2,1,0:T(4,128)S(1)}, u32[]{:S(2)}) copy-start(f32[1024,4,128]{2,1,0:T(4,128)S(1)} %reshape.244.own_ref) | copy-start | bytes 6291460
  15.1 8.4 %collective-permute-start = (f32[1024,4,128]{2,1,0:T(4,128)S(1)}, f32[1024,4,128]{2,1,0:T(4,128)}, u32[]{:S(2)}, u32[]{:S(2)}) collective-permute-start(f32[1024,4,128]{2,1,0:T(4,128)S(1)} %reshape.244.own_ref), channel_id=1, source_target_pairs={{0,2},{2,0},{4,6},{6,4},{8,10},{10,8},{12,14},{14,12},{16,18},{18,... | collective-permute-start | bytes 6291464 | tf_op jit(solution)/shard_map/ppermute | solution.py:243
  87.9 8.9 %copy-start.1 = (s32[1,1,16,1024]{3,2,1,0:T(8,128)S(1)}, s32[1,1,16,1024]{3,2,1,0:T(8,128)}, u32[]{:S(2)}) copy-start(s32[1,1,16,1024]{3,2,1,0:T(8,128)} %param.10) | copy-start | bytes 196612
  87.9 9.5 %copy-start.5 = (f32[3,16]{1,0:T(4,128)S(1)}, f32[3,16]{1,0:T(4,128)}, u32[]{:S(2)}) copy-start(f32[3,16]{1,0:T(4,128)} %param.11) | copy-start | bytes 580
  93.2 10.4 %all-to-all-start.1 = ((f32[16,2,512]{2,1,0:T(2,128)}), f32[16,2,512]{2,1,0:T(2,128)S(1)}, u32[]{:S(2)}, u32[]{:S(2)}) async-start(f32[16,2,512]{2,1,0:T(2,128)} %copy.78), calls=%async_computation.1 | async-start | bytes 131072 | tf_op jit(solution)/shard_map/all_to_all | solution.py:245
